TPU v7x, 768 devices: a whole 4x8x12 slice. The times are simulated.
768 devices in a mesh: sec: 48 (over z_hi, y, core), tile: 16 (over z_lo, x).
Axes of the slice: x: 4, y: 8, z: 12 (z_hi: 3, z_lo: 4; z = z_hi * 4 + z_lo), core: 2. Of those that a mesh axis runs over, the one named last changes fastest.
Arguments:
- sections: bfloat16 [96, 2048, 128], P('sec', 'tile'), may hold values from -6 to 6
- offsets: int32 [96], P('sec'), may hold values from 1 to 2
- valid_mask: int32 [96, 16], P('sec', 'tile'), may hold values 0 or 1
- conv1_w: bfloat16 [9, 16], replicated, may hold values from -2 to 2
- conv1_b: float32 [16], replicated, may hold values from -3 to 3
- conv2_w: bfloat16 [9, 16, 16], replicated, may hold values from -0.5 to 0.5
Outputs:
- residual: float32 [2, 96, 16], P(None, 'sec', 'tile')
- affine: float32 [96, 4], P('sec')
All inputs are finite; a program needn't handle non-finite values. No bound on the sum of `valid_mask` on one device may be relied on, other than what follows from the above.
Results may differ from a plain program's by a relative error of at most 0.0085.
The roundings to bfloat16 on the way count: a program that leaves them out, or rounds other values in their place, can miss the bound.
Values may be sent and summed in bfloat16 or wider, within the bound.
No kernel may reach another device: no remote copies, remote signals or barrier semaphores. Data moves between devices by JAX's collectives and lax.ppermute only.
A program may use at most 32 MiB of HBM per device.

v0:
```python
import math

import jax
import jax.numpy as jnp
from jax import lax
from jax.sharding import PartitionSpec as P

RIDGE_TERM = 1.0
CORR_GAIN = 2.5
FLOW_UNIT = 8.0


def with_halo(x, sides, width):
    for axis, dim in sides:
        peers, length = (lax.axis_size(axis), x.shape[dim])
        up = [(i, (i + 1) % peers) for i in range(peers - 1)]
        down = [(j, i) for i, j in up]
        last = lax.slice_in_dim(x, length - width, length, axis=dim)
        initial = lax.slice_in_dim(x, 0, width, axis=dim)
        before = lax.ppermute(last, axis, up)
        after = lax.ppermute(initial, axis, down)
        x = jnp.concatenate([before, x, after], axis=dim)
    return x


def from_behind(block, axis, distance):
    devices = range(lax.axis_size(axis))
    route = [(i - distance, i) for i in devices if i - distance in devices]
    return lax.ppermute(block, axis, route)


def dft_tables(patch_len):
    index_row = jnp.arange(patch_len, dtype=jnp.int32)
    product = index_row[:, None] * index_row[None, :] % patch_len
    phase_angle = product.astype(jnp.float32) * (2.0 * math.pi / patch_len)
    return (jnp.cos(phase_angle).astype(jnp.bfloat16), jnp.sin(phase_angle).astype(jnp.bfloat16))


def conv_layers(rows_in, inside, conv1_w, conv1_b, conv2_w):
    sec_count = rows_in.shape[0]
    wide_rows = rows_in.shape[1] - 2
    strip_rows = wide_rows - 2
    patch_len = rows_in.shape[2]
    channels = conv1_w.shape[1]
    padded = jnp.pad(rows_in, ((0, 0), (0, 0), (1, 1)))
    layer_one = (
        jnp.zeros((sec_count, channels, wide_rows, patch_len), jnp.float32)
        + conv1_b[None, :, None, None]
    )
    for tap_row in range(3):
        for tap_col in range(3):
            weight_tap = conv1_w[3 * tap_row + tap_col].astype(jnp.float32)
            window = padded[:, tap_row : tap_row + wide_rows, tap_col : tap_col + patch_len].astype(
                jnp.float32
            )
            layer_one = layer_one + weight_tap[None, :, None, None] * window[:, None]
    hidden = jnp.where(inside[None, None, :, None], jax.nn.relu(layer_one), 0.0).astype(
        jnp.bfloat16
    )
    hidden_pad = jnp.pad(hidden, ((0, 0), (0, 0), (0, 0), (1, 1)))
    layer_two = jnp.zeros((sec_count, channels, strip_rows, patch_len), jnp.float32)
    for tap_row in range(3):
        for tap_col in range(3):
            window = hidden_pad[:, :, tap_row : tap_row + strip_rows, tap_col : tap_col + patch_len]
            layer_two = layer_two + jnp.einsum(
                "schw,co->sohw",
                window,
                conv2_w[3 * tap_row + tap_col],
                preferred_element_type=jnp.float32,
            )
    return layer_two.astype(jnp.bfloat16)


def patch_spectra(features, cosine, sin_table, rows_per):
    sec_count, channels, strip_rows, patch_len = features.shape
    patches = features.reshape(sec_count, channels, rows_per, patch_len, patch_len)
    patches = patches.transpose(0, 2, 1, 3, 4).reshape(-1, patch_len, patch_len)
    flat_rows = patches.reshape(-1, patch_len)
    half_cos = (
        jnp.dot(flat_rows, cosine, preferred_element_type=jnp.float32)
        .astype(jnp.bfloat16)
        .reshape(patches.shape)
    )
    half_sin = (
        jnp.dot(flat_rows, sin_table, preferred_element_type=jnp.float32)
        .astype(jnp.bfloat16)
        .reshape(patches.shape)
    )
    spec_real = jnp.einsum(
        "uy,byk->buk", cosine, half_cos, preferred_element_type=jnp.float32
    ) - jnp.einsum("uy,byk->buk", sin_table, half_sin, preferred_element_type=jnp.float32)
    spec_imag = -(
        jnp.einsum("uy,byk->buk", sin_table, half_cos, preferred_element_type=jnp.float32)
        + jnp.einsum("uy,byk->buk", cosine, half_sin, preferred_element_type=jnp.float32)
    )
    out_shape = (sec_count, rows_per, channels, patch_len, patch_len)
    return (
        spec_real.astype(jnp.bfloat16).reshape(out_shape),
        spec_imag.astype(jnp.bfloat16).reshape(out_shape),
    )


def correlate(own_real, own_imag, part_real, part_imag, cosine, sin_table):
    patch_len = own_real.shape[-1]
    channels = own_real.shape[2]
    own_re32 = own_real.astype(jnp.float32)
    own_im32 = own_imag.astype(jnp.float32)
    part_re32 = part_real.astype(jnp.float32)
    part_im32 = part_imag.astype(jnp.float32)
    freq_index = jnp.arange(patch_len, dtype=jnp.int32)
    zero_freq = (freq_index[:, None] == 0) & (freq_index[None, :] == 0)
    cross_real = jnp.sum(own_re32 * part_re32 + own_im32 * part_im32, axis=2).astype(jnp.bfloat16)
    cross_imag = jnp.sum(own_re32 * part_im32 - own_im32 * part_re32, axis=2).astype(jnp.bfloat16)
    cross_real = jnp.where(zero_freq[None, None], jnp.zeros_like(cross_real), cross_real)
    cross_imag = jnp.where(zero_freq[None, None], jnp.zeros_like(cross_imag), cross_imag)
    flat_real = cross_real.reshape(-1, patch_len)
    flat_imag = cross_imag.reshape(-1, patch_len)
    back_real = (
        jnp.dot(flat_real, cosine, preferred_element_type=jnp.float32)
        - jnp.dot(flat_imag, sin_table, preferred_element_type=jnp.float32)
    ).astype(jnp.bfloat16)
    back_imag = (
        jnp.dot(flat_real, sin_table, preferred_element_type=jnp.float32)
        + jnp.dot(flat_imag, cosine, preferred_element_type=jnp.float32)
    ).astype(jnp.bfloat16)
    back_real = back_real.reshape(-1, patch_len, patch_len)
    back_imag = back_imag.reshape(-1, patch_len, patch_len)
    raw_corr = jnp.einsum(
        "ju,buk->bjk", cosine, back_real, preferred_element_type=jnp.float32
    ) - jnp.einsum("ju,buk->bjk", sin_table, back_imag, preferred_element_type=jnp.float32)
    scores = raw_corr * (CORR_GAIN / (patch_len * patch_len * patch_len * math.sqrt(channels)))
    flat_scores = scores.reshape(-1, patch_len * patch_len)
    row_max = jnp.max(flat_scores, axis=1, keepdims=True)
    expos = jnp.exp(flat_scores - row_max)
    probability = expos / jnp.sum(expos, axis=1, keepdims=True)
    lag_index = jnp.arange(patch_len, dtype=jnp.int32)
    signed_lag = jnp.where(lag_index >= patch_len // 2, lag_index - patch_len, lag_index).astype(
        jnp.float32
    )
    lag_rows = jnp.broadcast_to(signed_lag[:, None], (patch_len, patch_len)).reshape(-1)
    lag_cols = jnp.broadcast_to(signed_lag[None, :], (patch_len, patch_len)).reshape(-1)
    flow_rows = jnp.sum(probability * lag_rows[None], axis=1) / FLOW_UNIT
    flow_cols = jnp.sum(probability * lag_cols[None], axis=1) / FLOW_UNIT
    return jnp.stack([flow_rows, flow_cols], axis=0)


def local(sections, offsets, valid_mask, conv1_w, conv1_b, conv2_w):
    sec_here = sections.shape[0]
    strip_rows = sections.shape[1]
    patch_len = sections.shape[2]
    rows_per = strip_rows // patch_len
    tile_count = lax.axis_size("tile")
    tile_pos = lax.axis_index("tile")
    cosine, sin_table = dft_tables(patch_len)
    padded_rows = with_halo(sections, (("tile", 1),), 2)
    row_global = tile_pos * strip_rows - 1 + jnp.arange(strip_rows + 2, dtype=jnp.int32)
    inside = (row_global >= 0) & (row_global < strip_rows * tile_count)
    own_feats = conv_layers(padded_rows, inside, conv1_w, conv1_b, conv2_w)
    own_real, own_imag = patch_spectra(own_feats, cosine, sin_table, rows_per)
    next_feats = from_behind(own_feats, "sec", -1)
    next_real, next_imag = patch_spectra(next_feats, cosine, sin_table, rows_per)
    combined_real = jnp.concatenate([own_real, next_real], axis=0)
    combined_imag = jnp.concatenate([own_imag, next_imag], axis=0)
    use_first = (offsets == 1)[:, None, None, None, None]
    part_real = jnp.where(
        use_first, combined_real[1 : sec_here + 1], combined_real[2 : sec_here + 2]
    )
    part_imag = jnp.where(
        use_first, combined_imag[1 : sec_here + 1], combined_imag[2 : sec_here + 2]
    )
    flow_est = correlate(own_real, own_imag, part_real, part_imag, cosine, sin_table).reshape(
        2, sec_here, rows_per
    )
    section_ids = lax.axis_index("sec") * sec_here + jnp.arange(sec_here, dtype=jnp.int32)
    total_sections = sec_here * lax.axis_size("sec")
    pair_ok = jnp.where(section_ids + offsets < total_sections, 1.0, 0.0).astype(jnp.float32)
    weights = valid_mask.astype(jnp.float32) * pair_ok[:, None]
    rows_all = rows_per * tile_count
    grid_y = (
        (tile_pos * rows_per + jnp.arange(rows_per, dtype=jnp.int32)).astype(jnp.float32) + 0.5
    ) / rows_all * 2.0 - 1.0
    flow_full, weight_full = (
        lax.all_gather(flow_est, "tile", axis=2, tiled=True),
        lax.all_gather(weights, "tile", axis=1, tiled=True),
    )
    grid_full = (
        jnp.arange(rows_all, dtype=jnp.int32).astype(jnp.float32) + 0.5
    ) / rows_all * 2.0 - 1.0
    weight_sum = jnp.sum(weight_full, axis=1)
    weighted_y = jnp.sum(weight_full * grid_full[None], axis=1)
    weighted_yy = jnp.sum(weight_full * grid_full[None] * grid_full[None], axis=1)
    flow_sum = jnp.sum(flow_full * weight_full[None], axis=2)
    flow_y_sum = jnp.sum(flow_full * (weight_full * grid_full[None])[None], axis=2)
    m_zero = weight_sum + RIDGE_TERM
    m_two = weighted_yy + RIDGE_TERM
    determinant = m_zero * m_two - weighted_y * weighted_y
    offset_coef = (m_two[None] * flow_sum - weighted_y[None] * flow_y_sum) / determinant[None]
    slope_coef = (m_zero[None] * flow_y_sum - weighted_y[None] * flow_sum) / determinant[None]
    affine = jnp.stack([offset_coef[0], slope_coef[0], offset_coef[1], slope_coef[1]], axis=1)
    fitted = offset_coef[:, :, None] + slope_coef[:, :, None] * grid_y[None, None, :]
    residual = (flow_est - fitted) * weights[None]
    return (residual, affine)


def solution(mesh):
    placed = (P("sec", "tile", None), P("sec"), P("sec", "tile"), P(), P(), P())
    return jax.shard_map(
        local,
        mesh=mesh,
        in_specs=placed,
        out_specs=(P(None, "sec", "tile"), P("sec", None)),
        check_vma=False,
    )
```

profile of v0, /device:TPU:57, one launch (start us, length us, event | category | flops | bytes accessed | tf_op | source)
XLA Modules:
  0.0 153.9 jit_solution(4720338391976275902)
XLA Ops:
  0.6 0.0 copy-start
  0.6 0.7 fusion.156
  1.4 3.1 %collective-permute-start = (bf16[2,2,128]{2,1,0:T(2,128)(2,1)S(1)}, bf16[2,2,128]{2,1,0:T(2,128)(2,1)S(1)}, u32[]{:S(2)}, u32[]{:S(2)}) collective-permute-start(bf16[2,2,128]{2,1,0:T(2,128)(2,1)S(1)} %get-tuple-element.30), channel_id=1, source_target_pairs={{0,1},{1,2},{2,3},{3,4},{4,5},{5,6},{6,7},{7,8},{8,9},{9,10},{10,1... | collective-permute-start | bytes 3080 | tf_op jit(solution)/shard_map/ppermute | solution.py:20
  4.5 1.3 collective-permute-start.1
  5.8 0.7 broadcast_compare_fusion
  6.5 0.7 fusion.177
  7.1 0.7 fusion.176
  7.8 1.0 bitcast_convert_fusion.8
  8.8 0.1 broadcast_and_fusion
  8.9 38.5 %all-gather = f32[16,1,2]{2,1,0:T(1,128)S(1)} all-gather(f32[1,1,2]{2,1,0:T(1,128)S(1)} %fusion.177), channel_id=1, replica_groups=mesh['sec'=48,'tile'=16] {'tile'}, dimensions={0}, use_global_device_ids=true | all-gather | bytes 136 | tf_op jit(solution)/shard_map/all_gather | solution.py:184
  47.4 0.1 copy.149
  47.6 0.1 multiply_reduce_fusion.4
  47.7 0.1 copy.151
  47.8 0.1 copy.150
  47.9 0.0 collective-permute-done
  47.9 0.0 collective-permute-done.1
  47.9 0.9 pad_maximum_fusion.2
  48.8 1.1 fusion.23
  49.9 4.4 %select_convert_fusion = bf16[2,16,130,128]{3,1,2,0:T(8,128)(2,1)S(1)} fusion(f32[2,130,128]{2,1,0:T(8,128)S(1)} %get-tuple-element.26, f32[16]{0:T(128)S(1)} %get-tuple-element.41, f32[2,130,128]{2,1,0:T(8,128)S(1)} %get-tuple-element.58, f32[16]{0:T(128)S(1)} %get-tuple-element.42, f32[2,130,128]{2,1,0:T(8,128)S(1)} %get-tuple-element.25, ...), kind=kLoop, calls=%fused_computation.14 | loop fusion | flops 11182080 | bytes 2263810 | tf_op jit(solution)/shard_map/convert_element_type | solution.py:57
  54.3 0.0 copy-done
  54.3 0.5 fusion.10
  54.8 0.5 fusion.11
  55.3 0.5 fusion.12
  55.8 0.5 fusion.15
  56.3 0.4 fusion.17
  56.7 0.5 fusion.19
  57.2 0.5 fusion.8
  57.7 0.5 fusion.9
  58.1 1.1 fusion.4
  59.2 10.6 %collective-permute-start.2 = (bf16[2,16,128,128]{3,1,2,0:T(8,128)(2,1)S(1)}, bf16[2,16,128,128]{3,1,2,0:T(8,128)(2,1)S(1)}, u32[]{:S(2)}, u32[]{:S(2)}) collective-permute-start(bf16[2,16,128,128]{3,1,2,0:T(8,128)(2,1)S(1)} %fusion.4), channel_id=1, source_target_pairs={{16,0},{32,16},{48,32},{64,48},{80,64},{96,80},{112,96},{128,112},... | collective-permute-start | bytes 3145736 | tf_op jit(solution)/shard_map/ppermute | solution.py:29
  69.8 0.3 copy.133
  70.1 0.7 convolution_convert_fusion.3
  70.7 0.7 fusion.48
  71.4 0.7 convolution_convert_fusion.2
  72.1 0.7 fusion.38
  72.8 0.7 subtract_convert_fusion.1
  73.5 0.7 negate_convert_fusion.1
  74.2 39.9 %collective-permute-done.2 = bf16[2,16,128,128]{3,1,2,0:T(8,128)(2,1)S(1)} collective-permute-done((bf16[2,16,128,128]{3,1,2,0:T(8,128)(2,1)S(1)}, bf16[2,16,128,128]{3,1,2,0:T(8,128)(2,1)S(1)}, u32[]{:S(2)}, u32[]{:S(2)}) %collective-permute-start.2) | collective-permute-done | bytes 1048608 | tf_op jit(solution)/shard_map/ppermute | solution.py:29
  114.1 0.3 copy.136
  114.4 0.7 convolution_convert_fusion.1
  115.0 0.7 convolution_convert_fusion
  115.7 0.7 fusion.46
  116.4 0.7 fusion.36
  117.1 0.7 subtract_convert_fusion
  117.8 0.7 negate_convert_fusion
  118.5 1.1 fusion.3
  119.5 0.1 copy.143
  119.7 0.1 copy.144
  119.8 0.4 fusion.51
  120.2 0.4 fusion.50
  120.6 0.4 fusion.7
  121.0 0.4 fusion.6
  121.4 0.4 fusion.42
  121.8 0.5 fusion.157
  122.3 0.2 fusion.21
  122.5 0.2 multiply_reduce_fusion.1
  122.8 29.8 %all_gather.7 = f32[2,2,16]{1,0,2:T(2,128)S(1)} all-gather(f32[2,2,1]{1,0,2:T(2,128)S(1)} %maximum_bitcast_fusion), channel_id=1, replica_groups=mesh['sec'=48,'tile'=16] {'tile'}, dimensions={2}, use_global_device_ids=true | all-gather | bytes 272 | tf_op jit(solution)/shard_map/all_gather | solution.py:183
  152.7 0.6 copy.153
  153.3 0.6 fusion.74
  (15 shorter events, 0.2 us)
Async XLA Ops:
  0.6 53.7 %copy-start = (bf16[9,16,16]{2,1,0:T(8,128)(2,1)S(1)}, bf16[9,16,16]{2,1,0:T(8,128)(2,1)}, u32[]{:S(2)}) copy-start(bf16[9,16,16]{2,1,0:T(8,128)(2,1)} %param.11) | copy-start | bytes 13828
  1.4 46.5 %collective-permute-start = (bf16[2,2,128]{2,1,0:T(2,128)(2,1)S(1)}, bf16[2,2,128]{2,1,0:T(2,128)(2,1)S(1)}, u32[]{:S(2)}, u32[]{:S(2)}) collective-permute-start(bf16[2,2,128]{2,1,0:T(2,128)(2,1)S(1)} %get-tuple-element.30), channel_id=1, source_target_pairs={{0,1},{1,2},{2,3},{3,4},{4,5},{5,6},{6,7},{7,8},{8,9},{9,10},{10,1... | collective-permute-start | bytes 3080 | tf_op jit(solution)/shard_map/ppermute | solution.py:20
  4.5 43.4 %collective-permute-start.1 = (bf16[2,2,128]{2,1,0:T(2,128)(2,1)S(1)}, bf16[2,2,128]{2,1,0:T(2,128)(2,1)S(1)}, u32[]{:S(2)}, u32[]{:S(2)}) collective-permute-start(bf16[2,2,128]{2,1,0:T(2,128)(2,1)S(1)} %get-tuple-element.31), channel_id=1, source_target_pairs={{1,0},{2,1},{3,2},{4,3},{5,4},{6,5},{7,6},{8,7},{9,8},{10,9},{11,1... | collective-permute-start | bytes 3080 | tf_op jit(solution)/shard_map/ppermute | solution.py:21
  59.2 54.9 %collective-permute-start.2 = (bf16[2,16,128,128]{3,1,2,0:T(8,128)(2,1)S(1)}, bf16[2,16,128,128]{3,1,2,0:T(8,128)(2,1)S(1)}, u32[]{:S(2)}, u32[]{:S(2)}) collective-permute-start(bf16[2,16,128,128]{3,1,2,0:T(8,128)(2,1)S(1)} %fusion.4), channel_id=1, source_target_pairs={{16,0},{32,16},{48,32},{64,48},{80,64},{96,80},{112,96},{128,112},... | collective-permute-start | bytes 3145736 | tf_op jit(solution)/shard_map/ppermute | solution.py:29
where the time goes:
time: 155 us; the launch traced here: 154 us
  blocking collectives  68.4 us (44%)
  waiting for transfers between devices  40 us (26%)
  matrix products  15.5 us (10%)
  starting transfers between devices  14.9 us (10%)
  other arithmetic  11.8 us (8%)
  local copies, waits for them, and re-layouts  2.41 us (2%)
    ppermute x1, waiting for transfers between devices, from_behind(): return lax.ppermute(block, axis, route)  39.9 us
    all_gather x1, blocking collectives, local(): lax.all_gather(weights, 'tile', axis=1, tiled=True)  38.5 us
    all_gather x1, blocking collectives, local(): lax.all_gather(flow_est, 'tile', axis=2, tiled=True)  29.8 us
    ppermute x1, starting transfers between devices, from_behind(): return lax.ppermute(block, axis, route)  10.6 us
    dot_general x9, matrix products, conv_layers(): jnp.einsum('schw,co->sohw', window, conv2_w[3 * tap_row + tap_col], prefe...  4.87 us
    convert_element_type x1, other arithmetic, conv_layers(): jnp.where(inside[None, None, :, None], jax.nn.relu(layer_one), 0.0)  4.42 us
    ppermute x1, starting transfers between devices, with_halo(): before = lax.ppermute(last, axis, up)  3.1 us
  transfers between devices with their start and end apart: 3, of which 1 were waited for; matrix products, arithmetic and copies ran while one was open for 5% of the time, Pallas kernels for 0%

commit v1 on v0

--- a/solution.py
+++ b/solution.py
@@ -27,6 +27,17 @@
     devices = range(lax.axis_size(axis))
     route = [(i - distance, i) for i in devices if i - distance in devices]
     return lax.ppermute(block, axis, route)
+
+
+def tile_sum(v, axis):
+    peers = lax.axis_size(axis)
+    if peers & (peers - 1):
+        return lax.psum(v, axis)
+    step = 1
+    while step < peers:
+        v = v + lax.ppermute(v, axis, [(i, i ^ step) for i in range(peers)])
+        step *= 2
+    return v
 
 
 def dft_tables(patch_len):
@@ -179,18 +190,21 @@
     grid_y = (
         (tile_pos * rows_per + jnp.arange(rows_per, dtype=jnp.int32)).astype(jnp.float32) + 0.5
     ) / rows_all * 2.0 - 1.0
-    flow_full, weight_full = (
-        lax.all_gather(flow_est, "tile", axis=2, tiled=True),
-        lax.all_gather(weights, "tile", axis=1, tiled=True),
-    )
-    grid_full = (
-        jnp.arange(rows_all, dtype=jnp.int32).astype(jnp.float32) + 0.5
-    ) / rows_all * 2.0 - 1.0
-    weight_sum = jnp.sum(weight_full, axis=1)
-    weighted_y = jnp.sum(weight_full * grid_full[None], axis=1)
-    weighted_yy = jnp.sum(weight_full * grid_full[None] * grid_full[None], axis=1)
-    flow_sum = jnp.sum(flow_full * weight_full[None], axis=2)
-    flow_y_sum = jnp.sum(flow_full * (weight_full * grid_full[None])[None], axis=2)
+    weight_y = weights * grid_y[None]
+    partial = jnp.concatenate(
+        [
+            jnp.sum(weights, axis=1)[:, None],
+            jnp.sum(weight_y, axis=1)[:, None],
+            jnp.sum(weight_y * grid_y[None], axis=1)[:, None],
+            jnp.sum(flow_est * weights[None], axis=2).T,
+            jnp.sum(flow_est * weight_y[None], axis=2).T,
+        ],
+        axis=1,
+    )
+    totals = tile_sum(partial, "tile")
+    weight_sum, weighted_y, weighted_yy = totals[:, 0], totals[:, 1], totals[:, 2]
+    flow_sum = totals[:, 3:5].T
+    flow_y_sum = totals[:, 5:7].T
     m_zero = weight_sum + RIDGE_TERM
     m_two = weighted_yy + RIDGE_TERM
     determinant = m_zero * m_two - weighted_y * weighted_y

time: 155 us -> 111 us (0.72)
  blocking collectives: 68.4 us -> 0 us
  waiting for transfers between devices: 40 us -> 58 us
  starting transfers between devices: 14.9 us -> 22.6 us
    all_gather x2 -> x0, blocking collectives: 68.4 us -> none  [the longest x1 38.5 us: local(): lax.all_gather(weights, 'tile', axis=1, tiled=True)]
    ppermute x0 -> x4, starting transfers between devices: none -> 14 us  [tile_sum(): v = v + lax.ppermute(v, axis, [(i, i ^ step) for i in range(peers)])]
    ppermute x1, waiting for transfers between devices: 39.9 us -> 49.6 us  [from_behind(): return lax.ppermute(block, axis, route)]
    ppermute x0 -> x4, waiting for transfers between devices: none -> 7.91 us  [tile_sum(): v = v + lax.ppermute(v, axis, [(i, i ^ step) for i in range(peers)])]
    ppermute x1, starting transfers between devices: 10.6 us -> 4.19 us  [from_behind(): return lax.ppermute(block, axis, route)]
  transfers between devices with their start and end apart: 3 -> 7, of which waited for: 1 -> 6; matrix products, arithmetic and copies ran while one was open for 5% -> 6% of each run, Pallas kernels for 0% -> 0%
where the time goes in v1:
time: 111 us; the launch traced here: 110 us
  waiting for transfers between devices  58 us (52%)
  starting transfers between devices  22.6 us (20%)
  matrix products  15.4 us (14%)
  other arithmetic  10.9 us (10%)
  local copies, waits for them, and re-layouts  2.19 us (2%)
    ppermute x1, waiting for transfers between devices, from_behind(): return lax.ppermute(block, axis, route)  49.6 us
    ppermute x4, starting transfers between devices, tile_sum(): v = v + lax.ppermute(v, axis, [(i, i ^ step) for i in range(peers)])  14 us
    ppermute x4, waiting for transfers between devices, tile_sum(): v = v + lax.ppermute(v, axis, [(i, i ^ step) for i in range(peers)])  7.91 us
    dot_general x9, matrix products, conv_layers(): jnp.einsum('schw,co->sohw', window, conv2_w[3 * tap_row + tap_col], prefe...  4.86 us
    convert_element_type x1, other arithmetic, conv_layers(): jnp.where(inside[None, None, :, None], jax.nn.relu(layer_one), 0.0)  4.42 us
    ppermute x1, starting transfers between devices, from_behind(): return lax.ppermute(block, axis, route)  4.19 us
    ppermute x1, starting transfers between devices, with_halo(): before = lax.ppermute(last, axis, up)  3.1 us
  transfers between devices with their start and end apart: 7, of which 6 were waited for; matrix products, arithmetic and copies ran while one was open for 6% of the time, Pallas kernels for 0%

profile of v1, /device:TPU:57, one launch (start us, length us, event | category | flops | bytes accessed | tf_op | source)
XLA Modules:
  0.0 110.1 jit_solution(11910021120117141845)
XLA Ops:
  0.6 0.0 copy-start
  0.6 0.7 fusion.152
  1.4 3.1 %collective-permute-start = (bf16[2,2,128]{2,1,0:T(2,128)(2,1)S(1)}, bf16[2,2,128]{2,1,0:T(2,128)(2,1)S(1)}, u32[]{:S(2)}, u32[]{:S(2)}) collective-permute-start(bf16[2,2,128]{2,1,0:T(2,128)(2,1)S(1)} %get-tuple-element.31), channel_id=1, source_target_pairs={{0,1},{1,2},{2,3},{3,4},{4,5},{5,6},{6,7},{7,8},{8,9},{9,10},{10,1... | collective-permute-start | bytes 3080 | tf_op jit(solution)/shard_map/ppermute | solution.py:20
  4.5 1.3 %collective-permute-start.1 = (bf16[2,2,128]{2,1,0:T(2,128)(2,1)S(1)}, bf16[2,2,128]{2,1,0:T(2,128)(2,1)S(1)}, u32[]{:S(2)}, u32[]{:S(2)}) collective-permute-start(bf16[2,2,128]{2,1,0:T(2,128)(2,1)S(1)} %get-tuple-element.32), channel_id=1, source_target_pairs={{1,0},{2,1},{3,2},{4,3},{5,4},{6,5},{7,6},{8,7},{9,8},{10,9},{11,1... | collective-permute-start | bytes 3080 | tf_op jit(solution)/shard_map/ppermute | solution.py:21
  5.8 1.0 bitcast_convert_fusion.8
  6.8 0.7 broadcast_compare_fusion
  7.4 0.1 broadcast_and_fusion
  7.5 0.7 broadcast_multiply_fusion
  8.2 0.0 collective-permute-done
  8.2 0.5 collective-permute-done.1
  8.8 0.9 pad_maximum_fusion.2
  9.7 1.1 fusion.23
  10.8 4.4 %select_convert_fusion = bf16[2,16,130,128]{3,1,2,0:T(8,128)(2,1)S(1)} fusion(f32[2,130,128]{2,1,0:T(8,128)S(1)} %get-tuple-element.27, f32[16]{0:T(128)S(1)} %get-tuple-element.45, f32[2,130,128]{2,1,0:T(8,128)S(1)} %get-tuple-element.55, f32[16]{0:T(128)S(1)} %get-tuple-element.46, f32[2,130,128]{2,1,0:T(8,128)S(1)} %get-tuple-element.26, ...), kind=kLoop, calls=%fused_computation.14 | loop fusion | flops 11182080 | bytes 2263810 | tf_op jit(solution)/shard_map/convert_element_type | solution.py:68
  15.2 0.0 copy-done
  15.2 0.5 fusion.10
  15.7 0.5 fusion.11
  16.2 0.5 fusion.12
  16.7 0.5 fusion.15
  17.1 0.4 fusion.17
  17.6 0.5 fusion.19
  18.0 0.5 fusion.8
  18.5 0.5 fusion.9
  19.0 1.1 fusion.4
  20.1 4.2 %collective-permute-start.2 = (bf16[2,16,128,128]{3,1,2,0:T(8,128)(2,1)S(1)}, bf16[2,16,128,128]{3,1,2,0:T(8,128)(2,1)S(1)}, u32[]{:S(2)}, u32[]{:S(2)}) collective-permute-start(bf16[2,16,128,128]{3,1,2,0:T(8,128)(2,1)S(1)} %fusion.4), channel_id=1, source_target_pairs={{16,0},{32,16},{48,32},{64,48},{80,64},{96,80},{112,96},{128,112},... | collective-permute-start | bytes 3145736 | tf_op jit(solution)/shard_map/ppermute | solution.py:29
  24.3 0.3 copy.123
  24.6 0.7 convolution_convert_fusion.3
  25.2 0.7 fusion.48
  25.9 0.7 convolution_convert_fusion.2
  26.6 0.7 fusion.38
  27.3 0.7 subtract_convert_fusion.1
  28.0 0.7 negate_convert_fusion.1
  28.7 49.6 %collective-permute-done.2 = bf16[2,16,128,128]{3,1,2,0:T(8,128)(2,1)S(1)} collective-permute-done((bf16[2,16,128,128]{3,1,2,0:T(8,128)(2,1)S(1)}, bf16[2,16,128,128]{3,1,2,0:T(8,128)(2,1)S(1)}, u32[]{:S(2)}, u32[]{:S(2)}) %collective-permute-start.2) | collective-permute-done | bytes 1048608 | tf_op jit(solution)/shard_map/ppermute | solution.py:29
  78.2 0.3 copy.126
  78.5 0.7 convolution_convert_fusion.1
  79.2 0.7 convolution_convert_fusion
  79.8 0.7 fusion.46
  80.5 0.7 fusion.36
  81.2 0.7 subtract_convert_fusion
  81.9 0.7 negate_convert_fusion
  82.6 1.1 fusion.3
  83.6 0.1 copy.133
  83.8 0.1 copy.134
  83.9 0.4 fusion.51
  84.3 0.4 fusion.50
  84.7 0.4 fusion.7
  85.1 0.4 fusion.6
  85.5 0.4 fusion.42
  85.9 0.5 fusion.153
  86.4 0.2 fusion.21
  86.6 0.2 multiply_reduce_fusion.1
  86.9 3.2 %collective-permute-start.3 = (f32[2,7]{0,1:T(8,128)S(1)}, f32[2,7]{0,1:T(8,128)S(1)}, u32[]{:S(2)}, u32[]{:S(2)}) collective-permute-start(f32[2,7]{0,1:T(8,128)S(1)} %concatenate.27), channel_id=1, source_target_pairs={{0,1},{1,0},{2,3},{3,2},{4,5},{5,4},{6,7},{7,6},{8,9},{9,8},{10,11... | collective-permute-start | bytes 176 | tf_op jit(solution)/shard_map/ppermute | solution.py:38
  90.1 1.2 %collective-permute-done.3 = f32[2,7]{0,1:T(8,128)S(1)} collective-permute-done((f32[2,7]{0,1:T(8,128)S(1)}, f32[2,7]{0,1:T(8,128)S(1)}, u32[]{:S(2)}, u32[]{:S(2)}) %collective-permute-start.3) | collective-permute-done | bytes 88 | tf_op jit(solution)/shard_map/ppermute | solution.py:38
  91.2 7.0 %collective-permute-start.4 = (f32[2,7]{0,1:T(8,128)S(1)}, f32[2,7]{0,1:T(8,128)S(1)}, u32[]{:S(2)}, u32[]{:S(2)}) collective-permute-start(f32[2,7]{0,1:T(8,128)S(1)} %add.228), channel_id=1, source_target_pairs={{0,2},{1,3},{2,0},{3,1},{4,6},{5,7},{6,4},{7,5},{8,10},{9,11},{10,... | collective-permute-start | bytes 176 | tf_op jit(solution)/shard_map/ppermute | solution.py:38
  98.3 1.0 collective-permute-done.4
  99.3 1.9 %collective-permute-start.5 = (f32[2,7]{0,1:T(8,128)S(1)}, f32[2,7]{0,1:T(8,128)S(1)}, u32[]{:S(2)}, u32[]{:S(2)}) collective-permute-start(f32[2,7]{0,1:T(8,128)S(1)} %add.229), channel_id=1, source_target_pairs={{0,4},{1,5},{2,6},{3,7},{4,0},{5,1},{6,2},{7,3},{8,12},{9,13},{10,... | collective-permute-start | bytes 176 | tf_op jit(solution)/shard_map/ppermute | solution.py:38
  101.2 2.4 %collective-permute-done.5 = f32[2,7]{0,1:T(8,128)S(1)} collective-permute-done((f32[2,7]{0,1:T(8,128)S(1)}, f32[2,7]{0,1:T(8,128)S(1)}, u32[]{:S(2)}, u32[]{:S(2)}) %collective-permute-start.5) | collective-permute-done | bytes 88 | tf_op jit(solution)/shard_map/ppermute | solution.py:38
  103.6 1.9 %collective-permute-start.6 = (f32[2,7]{0,1:T(8,128)S(1)}, f32[2,7]{0,1:T(8,128)S(1)}, u32[]{:S(2)}, u32[]{:S(2)}) collective-permute-start(f32[2,7]{0,1:T(8,128)S(1)} %add.230), channel_id=1, source_target_pairs={{0,8},{1,9},{2,10},{3,11},{4,12},{5,13},{6,14},{7,15},{8,0},{9,1},... | collective-permute-start | bytes 176 | tf_op jit(solution)/shard_map/ppermute | solution.py:38
  105.5 3.3 %collective-permute-done.6 = f32[2,7]{0,1:T(8,128)S(1)} collective-permute-done((f32[2,7]{0,1:T(8,128)S(1)}, f32[2,7]{0,1:T(8,128)S(1)}, u32[]{:S(2)}, u32[]{:S(2)}) %collective-permute-start.6) | collective-permute-done | bytes 88 | tf_op jit(solution)/shard_map/ppermute | solution.py:38
  108.9 0.6 subtract_multiply_fusion
  109.5 0.7 copy.138
  (17 shorter events, 0.1 us)
Async XLA Ops:
  0.6 14.6 %copy-start = (bf16[9,16,16]{2,1,0:T(8,128)(2,1)S(1)}, bf16[9,16,16]{2,1,0:T(8,128)(2,1)}, u32[]{:S(2)}) copy-start(bf16[9,16,16]{2,1,0:T(8,128)(2,1)} %param.11) | copy-start | bytes 13828
  1.4 6.9 %collective-permute-start = (bf16[2,2,128]{2,1,0:T(2,128)(2,1)S(1)}, bf16[2,2,128]{2,1,0:T(2,128)(2,1)S(1)}, u32[]{:S(2)}, u32[]{:S(2)}) collective-permute-start(bf16[2,2,128]{2,1,0:T(2,128)(2,1)S(1)} %get-tuple-element.31), channel_id=1, source_target_pairs={{0,1},{1,2},{2,3},{3,4},{4,5},{5,6},{6,7},{7,8},{8,9},{9,10},{10,1... | collective-permute-start | bytes 3080 | tf_op jit(solution)/shard_map/ppermute | solution.py:20
  4.5 4.3 %collective-permute-start.1 = (bf16[2,2,128]{2,1,0:T(2,128)(2,1)S(1)}, bf16[2,2,128]{2,1,0:T(2,128)(2,1)S(1)}, u32[]{:S(2)}, u32[]{:S(2)}) collective-permute-start(bf16[2,2,128]{2,1,0:T(2,128)(2,1)S(1)} %get-tuple-element.32), channel_id=1, source_target_pairs={{1,0},{2,1},{3,2},{4,3},{5,4},{6,5},{7,6},{8,7},{9,8},{10,9},{11,1... | collective-permute-start | bytes 3080 | tf_op jit(solution)/shard_map/ppermute | solution.py:21
  20.1 58.1 %collective-permute-start.2 = (bf16[2,16,128,128]{3,1,2,0:T(8,128)(2,1)S(1)}, bf16[2,16,128,128]{3,1,2,0:T(8,128)(2,1)S(1)}, u32[]{:S(2)}, u32[]{:S(2)}) collective-permute-start(bf16[2,16,128,128]{3,1,2,0:T(8,128)(2,1)S(1)} %fusion.4), channel_id=1, source_target_pairs={{16,0},{32,16},{48,32},{64,48},{80,64},{96,80},{112,96},{128,112},... | collective-permute-start | bytes 3145736 | tf_op jit(solution)/shard_map/ppermute | solution.py:29
  86.9 4.3 %collective-permute-start.3 = (f32[2,7]{0,1:T(8,128)S(1)}, f32[2,7]{0,1:T(8,128)S(1)}, u32[]{:S(2)}, u32[]{:S(2)}) collective-permute-start(f32[2,7]{0,1:T(8,128)S(1)} %concatenate.27), channel_id=1, source_target_pairs={{0,1},{1,0},{2,3},{3,2},{4,5},{5,4},{6,7},{7,6},{8,9},{9,8},{10,11... | collective-permute-start | bytes 176 | tf_op jit(solution)/shard_map/ppermute | solution.py:38
  91.2 8.0 %collective-permute-start.4 = (f32[2,7]{0,1:T(8,128)S(1)}, f32[2,7]{0,1:T(8,128)S(1)}, u32[]{:S(2)}, u32[]{:S(2)}) collective-permute-start(f32[2,7]{0,1:T(8,128)S(1)} %add.228), channel_id=1, source_target_pairs={{0,2},{1,3},{2,0},{3,1},{4,6},{5,7},{6,4},{7,5},{8,10},{9,11},{10,... | collective-permute-start | bytes 176 | tf_op jit(solution)/shard_map/ppermute | solution.py:38
  99.3 4.3 %collective-permute-start.5 = (f32[2,7]{0,1:T(8,128)S(1)}, f32[2,7]{0,1:T(8,128)S(1)}, u32[]{:S(2)}, u32[]{:S(2)}) collective-permute-start(f32[2,7]{0,1:T(8,128)S(1)} %add.229), channel_id=1, source_target_pairs={{0,4},{1,5},{2,6},{3,7},{4,0},{5,1},{6,2},{7,3},{8,12},{9,13},{10,... | collective-permute-start | bytes 176 | tf_op jit(solution)/shard_map/ppermute | solution.py:38
  103.6 5.2 %collective-permute-start.6 = (f32[2,7]{0,1:T(8,128)S(1)}, f32[2,7]{0,1:T(8,128)S(1)}, u32[]{:S(2)}, u32[]{:S(2)}) collective-permute-start(f32[2,7]{0,1:T(8,128)S(1)} %add.230), channel_id=1, source_target_pairs={{0,8},{1,9},{2,10},{3,11},{4,12},{5,13},{6,14},{7,15},{8,0},{9,1},... | collective-permute-start | bytes 176 | tf_op jit(solution)/shard_map/ppermute | solution.py:38

commit v2 on v1

--- a/solution.py
+++ b/solution.py
@@ -111,7 +111,7 @@
     )
 
 
-def correlate(own_real, own_imag, part_real, part_imag, cosine, sin_table):
+def correlate(own_real, own_imag, part_real, part_imag, pair_valid, cosine, sin_table):
     patch_len = own_real.shape[-1]
     channels = own_real.shape[2]
     own_re32 = own_real.astype(jnp.float32)
@@ -122,8 +122,9 @@
     zero_freq = (freq_index[:, None] == 0) & (freq_index[None, :] == 0)
     cross_real = jnp.sum(own_re32 * part_re32 + own_im32 * part_im32, axis=2).astype(jnp.bfloat16)
     cross_imag = jnp.sum(own_re32 * part_im32 - own_im32 * part_re32, axis=2).astype(jnp.bfloat16)
-    cross_real = jnp.where(zero_freq[None, None], jnp.zeros_like(cross_real), cross_real)
-    cross_imag = jnp.where(zero_freq[None, None], jnp.zeros_like(cross_imag), cross_imag)
+    drop = zero_freq[None, None] | ~pair_valid[:, None, None, None]
+    cross_real = jnp.where(drop, jnp.zeros_like(cross_real), cross_real)
+    cross_imag = jnp.where(drop, jnp.zeros_like(cross_imag), cross_imag)
     flat_real = cross_real.reshape(-1, patch_len)
     flat_imag = cross_imag.reshape(-1, patch_len)
     back_real = (
@@ -164,14 +165,13 @@
     tile_pos = lax.axis_index("tile")
     cosine, sin_table = dft_tables(patch_len)
     padded_rows = with_halo(sections, (("tile", 1),), 2)
+    next_rows = from_behind(padded_rows, "sec", -1)
     row_global = tile_pos * strip_rows - 1 + jnp.arange(strip_rows + 2, dtype=jnp.int32)
     inside = (row_global >= 0) & (row_global < strip_rows * tile_count)
-    own_feats = conv_layers(padded_rows, inside, conv1_w, conv1_b, conv2_w)
-    own_real, own_imag = patch_spectra(own_feats, cosine, sin_table, rows_per)
-    next_feats = from_behind(own_feats, "sec", -1)
-    next_real, next_imag = patch_spectra(next_feats, cosine, sin_table, rows_per)
-    combined_real = jnp.concatenate([own_real, next_real], axis=0)
-    combined_imag = jnp.concatenate([own_imag, next_imag], axis=0)
+    all_rows = jnp.concatenate([padded_rows, next_rows], axis=0)
+    all_feats = conv_layers(all_rows, inside, conv1_w, conv1_b, conv2_w)
+    combined_real, combined_imag = patch_spectra(all_feats, cosine, sin_table, rows_per)
+    own_real, own_imag = combined_real[:sec_here], combined_imag[:sec_here]
     use_first = (offsets == 1)[:, None, None, None, None]
     part_real = jnp.where(
         use_first, combined_real[1 : sec_here + 1], combined_real[2 : sec_here + 2]
@@ -179,12 +179,13 @@
     part_imag = jnp.where(
         use_first, combined_imag[1 : sec_here + 1], combined_imag[2 : sec_here + 2]
     )
-    flow_est = correlate(own_real, own_imag, part_real, part_imag, cosine, sin_table).reshape(
-        2, sec_here, rows_per
-    )
     section_ids = lax.axis_index("sec") * sec_here + jnp.arange(sec_here, dtype=jnp.int32)
     total_sections = sec_here * lax.axis_size("sec")
-    pair_ok = jnp.where(section_ids + offsets < total_sections, 1.0, 0.0).astype(jnp.float32)
+    pair_valid = section_ids + offsets < total_sections
+    flow_est = correlate(
+        own_real, own_imag, part_real, part_imag, pair_valid, cosine, sin_table
+    ).reshape(2, sec_here, rows_per)
+    pair_ok = jnp.where(pair_valid, 1.0, 0.0).astype(jnp.float32)
     weights = valid_mask.astype(jnp.float32) * pair_ok[:, None]
     rows_all = rows_per * tile_count
     grid_y = (

time: 111 us -> 94.7 us (0.85)
  waiting for transfers between devices: 58 us -> 14.4 us
  matrix products: 15.4 us -> 35.4 us
  starting transfers between devices: 22.6 us -> 27.9 us
  local copies, waits for them, and re-layouts: 2.19 us -> 4.02 us
    ppermute x1, waiting for transfers between devices: 49.6 us -> 9.78 us  [from_behind(): return lax.ppermute(block, axis, route)]
    dot_general x9, matrix products: 4.86 us -> 27.2 us  [conv_layers(): jnp.einsum('schw,co->sohw', window, conv2_w[3 * tap_row + tap_col], prefe...]
    ppermute x4, starting transfers between devices: 14 us -> 19.5 us  [tile_sum(): v = v + lax.ppermute(v, axis, [(i, i ^ step) for i in range(peers)])]
    ppermute x4, waiting for transfers between devices: 7.91 us -> 4.17 us  [tile_sum(): v = v + lax.ppermute(v, axis, [(i, i ^ step) for i in range(peers)])]
    slice x0 -> x2, local copies, waits for them, and re-layouts: none -> 1.75 us  [the longest x1 0.88 us: local(): combined_imag[2:sec_here + 2]]
  transfers between devices with their start and end apart: 7 -> 7, of which waited for: 6 -> 6; matrix products, arithmetic and copies ran while one was open for 6% -> 3% of each run, Pallas kernels for 0% -> 0%
where the time goes in v2:
time: 94.7 us; the launch traced here: 93.9 us
  matrix products  35.4 us (37%)
  starting transfers between devices  27.9 us (29%)
  waiting for transfers between devices  14.4 us (15%)
  other arithmetic  11.2 us (12%)
  local copies, waits for them, and re-layouts  4.02 us (4%)
    dot_general x9, matrix products, conv_layers(): jnp.einsum('schw,co->sohw', window, conv2_w[3 * tap_row + tap_col], prefe...  27.2 us
    ppermute x4, starting transfers between devices, tile_sum(): v = v + lax.ppermute(v, axis, [(i, i ^ step) for i in range(peers)])  19.5 us
    ppermute x1, waiting for transfers between devices, from_behind(): return lax.ppermute(block, axis, route)  9.78 us
    ppermute x4, waiting for transfers between devices, tile_sum(): v = v + lax.ppermute(v, axis, [(i, i ^ step) for i in range(peers)])  4.17 us
    convert_element_type x1, other arithmetic, conv_layers(): jnp.where(inside[None, None, :, None], jax.nn.relu(layer_one), 0.0)  4.11 us
    ppermute x1, starting transfers between devices, from_behind(): return lax.ppermute(block, axis, route)  4.01 us
    ppermute x1, starting transfers between devices, with_halo(): before = lax.ppermute(last, axis, up)  3.1 us
  transfers between devices with their start and end apart: 7, of which 6 were waited for; matrix products, arithmetic and copies ran while one was open for 3% of the time, Pallas kernels for 0%

profile of v2, /device:TPU:57, one launch (start us, length us, event | category | flops | bytes accessed | tf_op | source)
XLA Modules:
  0.0 93.9 jit_solution(11357919694491281782)
XLA Ops:
  0.6 0.0 copy-start
  0.6 0.7 fusion.126
  1.4 3.1 %collective-permute-start = (bf16[2,2,128]{2,1,0:T(2,128)(2,1)S(1)}, bf16[2,2,128]{2,1,0:T(2,128)(2,1)S(1)}, u32[]{:S(2)}, u32[]{:S(2)}) collective-permute-start(bf16[2,2,128]{2,1,0:T(2,128)(2,1)S(1)} %get-tuple-element.37), channel_id=1, source_target_pairs={{0,1},{1,2},{2,3},{3,4},{4,5},{5,6},{6,7},{7,8},{8,9},{9,10},{10,1... | collective-permute-start | bytes 3080 | tf_op jit(solution)/shard_map/ppermute | solution.py:20
  4.5 1.3 %collective-permute-start.1 = (bf16[2,2,128]{2,1,0:T(2,128)(2,1)S(1)}, bf16[2,2,128]{2,1,0:T(2,128)(2,1)S(1)}, u32[]{:S(2)}, u32[]{:S(2)}) collective-permute-start(bf16[2,2,128]{2,1,0:T(2,128)(2,1)S(1)} %get-tuple-element.38), channel_id=1, source_target_pairs={{1,0},{2,1},{3,2},{4,3},{5,4},{6,5},{7,6},{8,7},{9,8},{10,9},{11,1... | collective-permute-start | bytes 3080 | tf_op jit(solution)/shard_map/ppermute | solution.py:21
  5.8 1.0 %bitcast_convert_fusion.8 = (f32[16]{0:T(128)S(1)}, f32[16]{0:T(128)S(1)}, f32[16]{0:T(128)S(1)}, f32[16]{0:T(128)S(1)}, f32[16]{0:T(128)S(1)}, /*index=5*/f32[1...) fusion(bf16[9,16]{1,0:T(8,128)(2,1)} %param.9), kind=kLoop, calls=%fused_computation.131 | loop fusion | flops 144 | bytes 864 | tf_op jit(solution)/shard_map/convert_element_type | solution.py:63
  6.8 0.7 compare_not_fusion
  7.4 0.1 broadcast_bitcast_fusion
  7.5 0.1 broadcast_and_fusion
  7.6 0.7 broadcast_multiply_fusion
  8.3 0.0 collective-permute-done
  8.3 0.5 collective-permute-done.1
  8.8 0.9 pad_maximum_fusion.1
  9.7 4.0 %collective-permute-start.2 = (bf16[2,132,128]{2,1,0:T(8,128)(2,1)S(1)}, bf16[2,132,128]{2,1,0:T(8,128)(2,1)S(1)}, u32[]{:S(2)}, u32[]{:S(2)}) collective-permute-start(bf16[2,132,128]{2,1,0:T(8,128)(2,1)S(1)} %pad_maximum_fusion.1), channel_id=1, source_target_pairs={{16,0},{32,16},{48,32},{64,48},{80,64},{96,80},{112,96},{128,112},... | collective-permute-start | bytes 202760 | tf_op jit(solution)/shard_map/ppermute | solution.py:29
  13.7 9.8 %collective-permute-done.2 = bf16[2,132,128]{2,1,0:T(8,128)(2,1)S(1)} collective-permute-done((bf16[2,132,128]{2,1,0:T(8,128)(2,1)S(1)}, bf16[2,132,128]{2,1,0:T(8,128)(2,1)S(1)}, u32[]{:S(2)}, u32[]{:S(2)}) %collective-permute-start.2) | collective-permute-done | bytes 67616 | tf_op jit(solution)/shard_map/ppermute | solution.py:29
  23.5 0.9 pad_maximum_fusion
  24.3 0.3 fusion.21
  24.7 4.1 %select_convert_fusion = bf16[4,16,130,128]{3,1,2,0:T(8,128)(2,1)S(1)} fusion(f32[4,130,128]{2,1,0:T(8,128)S(1)} %get-tuple-element.33, f32[16]{0:T(128)S(1)} %get-tuple-element.51, f32[4,130,128]{2,1,0:T(8,128)S(1)} %get-tuple-element.34, f32[16]{0:T(128)S(1)} %get-tuple-element.52, f32[4,130,128]{2,1,0:T(8,128)S(1)} %get-tuple-element.32, ...), kind=kLoop, calls=%fused_computation.8 | loop fusion | flops 22364160 | bytes 4526850 | tf_op jit(solution)/shard_map/convert_element_type | solution.py:68
  28.8 0.0 copy-done
  28.8 0.7 fusion.11
  29.5 0.7 fusion.13
  30.2 2.7 %fusion.4 = f32[4,128,128,16]{2,3,1,0:T(8,128)} fusion(bf16[4,16,130,128]{3,1,2,0:T(8,128)(2,1)S(1)} %select_convert_fusion, bf16[9,16,16]{2,1,0:T(8,128)(2,1)S(1)} %copy-done), kind=kOutput, calls=%fused_computation.20 | convolution fusion | flops 33554432 | bytes 6328320 | tf_op jit(solution)/shard_map/schw,co->sohw/dot_general | solution.py:76
  33.0 2.7 %fusion.5 = f32[4,128,128,16]{2,3,1,0:T(8,128)} fusion(bf16[4,16,130,128]{3,1,2,0:T(8,128)(2,1)S(1)} %select_convert_fusion, bf16[9,16,16]{2,1,0:T(8,128)(2,1)S(1)} %copy-done), kind=kOutput, calls=%fused_computation.21 | convolution fusion | flops 33554432 | bytes 6328320 | tf_op jit(solution)/shard_map/schw,co->sohw/dot_general | solution.py:76
  35.7 2.7 %fusion.6 = f32[4,128,128,16]{2,3,1,0:T(8,128)} fusion(bf16[4,16,130,128]{3,1,2,0:T(8,128)(2,1)S(1)} %select_convert_fusion, bf16[9,16,16]{2,1,0:T(8,128)(2,1)S(1)} %copy-done), kind=kOutput, calls=%fused_computation.22 | convolution fusion | flops 33554432 | bytes 6328320 | tf_op jit(solution)/shard_map/schw,co->sohw/dot_general | solution.py:76
  38.4 2.7 %fusion.7 = f32[4,128,128,16]{2,3,1,0:T(8,128)} fusion(bf16[4,16,130,128]{3,1,2,0:T(8,128)(2,1)S(1)} %select_convert_fusion, bf16[9,16,16]{2,1,0:T(8,128)(2,1)S(1)} %copy-done), kind=kOutput, calls=%fused_computation.23 | convolution fusion | flops 33554432 | bytes 6328320 | tf_op jit(solution)/shard_map/schw,co->sohw/dot_general | solution.py:76
  41.1 2.7 %fusion.8 = f32[4,128,128,16]{2,3,1,0:T(8,128)} fusion(bf16[4,16,130,128]{3,1,2,0:T(8,128)(2,1)S(1)} %select_convert_fusion, bf16[9,16,16]{2,1,0:T(8,128)(2,1)S(1)} %copy-done), kind=kOutput, calls=%fused_computation.24 | convolution fusion | flops 33554432 | bytes 6328320 | tf_op jit(solution)/shard_map/schw,co->sohw/dot_general | solution.py:76
  43.9 2.7 %fusion.9 = f32[4,128,128,16]{2,3,1,0:T(8,128)} fusion(bf16[4,16,130,128]{3,1,2,0:T(8,128)(2,1)S(1)} %select_convert_fusion, bf16[9,16,16]{2,1,0:T(8,128)(2,1)S(1)} %copy-done), kind=kOutput, calls=%fused_computation.25 | convolution fusion | flops 33554432 | bytes 6295552 | tf_op jit(solution)/shard_map/schw,co->sohw/dot_general | solution.py:76
  46.5 9.5 %fusion.17 = bf16[4,16,128,128]{3,1,2,0:T(8,128)(2,1)S(1)} fusion(bf16[4,16,130,128]{3,1,2,0:T(8,128)(2,1)S(1)} %select_convert_fusion, f32[4,128,128,16]{2,3,1,0:T(8,128)} %fusion.9, f32[4,128,128,16]{2,3,1,0:T(8,128)} %fusion.8, f32[4,128,128,16]{2,3,1,0:T(8,128)} %fusion.7, f32[4,128,128,16]{2,3,1,0:T(8,128)S(1)} %fusion.11, ...), kind=kOutput, calls=%fused_computation.33 | convolution fusion | flops 42991616 | bytes 37785600 | tf_op jit(solution)/shard_map/schw,co->sohw/dot_general | solution.py:76
  56.0 0.5 copy.104
  56.6 0.9 convolution_convert_fusion.1
  57.5 0.9 convolution_convert_fusion
  58.4 1.0 %fusion.38 = f32[64,128,128]{2,1,0:T(8,128)S(1)} fusion(bf16[64,128,128]{2,1,0:T(8,128)(2,1)S(1)} %bitcast.204), kind=kOutput, calls=%fused_computation.79 | convolution fusion | flops 268681216 | bytes 6291456 | tf_op jit(solution)/shard_map/uy,byk->buk/dot_general | solution.py:104
  59.4 1.0 %fusion.44 = f32[64,128,128]{2,1,0:T(8,128)S(1)} fusion(bf16[64,128,128]{2,1,0:T(8,128)(2,1)S(1)} %bitcast.205), kind=kOutput, calls=%fused_computation.85 | convolution fusion | flops 268681216 | bytes 6291456 | tf_op jit(solution)/shard_map/uy,byk->buk/dot_general | solution.py:100
  60.4 1.0 %fusion.16 = bf16[64,128,128]{1,2,0:T(8,128)(2,1)S(1)} fusion(f32[64,128,128]{2,1,0:T(8,128)S(1)} %fusion.38, bf16[64,128,128]{2,1,0:T(8,128)(2,1)S(1)} %bitcast.206), kind=kOutput, calls=%fused_computation.32 | convolution fusion | flops 271826944 | bytes 8388608 | tf_op jit(solution)/shard_map/uy,byk->buk/dot_general | solution.py:105
  61.3 0.9 fusion.124
  62.2 1.0 %fusion.15 = bf16[64,128,128]{1,2,0:T(8,128)(2,1)S(1)} fusion(f32[64,128,128]{2,1,0:T(8,128)S(1)} %fusion.44, bf16[64,128,128]{2,1,0:T(8,128)(2,1)S(1)} %bitcast.207), kind=kOutput, calls=%fused_computation.31 | convolution fusion | flops 270778368 | bytes 8388608 | tf_op jit(solution)/shard_map/uy,byk->buk/dot_general | solution.py:102
  63.2 0.9 fusion.125
  64.1 1.5 %fusion.3 = (bf16[2,128,128]{1,2,0:T(8,128)(2,1)S(1)}, bf16[2,128,128]{1,2,0:T(8,128)(2,1)S(1)}) fusion(bf16[2,1,16,128,128]{3,4,2,0,1:T(8,128)(2,1)S(1)} %bitcast.213, bf16[2,1,16,128,128]{3,4,2,0,1:T(8,128)(2,1)S(1)} %bitcast.210, bf16[2,1,16,128,128]{3,4,2,0,1:T(8,128)(2,1)S(1)} %bitcast.212, bf16[2,1,16,128,128]{3,4,2,0,1:T(8,128)(2,1)S(1)} %bitcast.211, ...), kind=kLoop, calls=%fused_computation.19 | loop fusion | flops 7274496 | bytes 6422530 | tf_op jit(solution)/shard_map/reduce_sum | solution.py:124
  65.5 0.1 copy.109
  65.7 0.1 copy.110
  65.8 0.1 fusion.27
  65.9 0.4 fusion.47
  66.3 0.4 fusion.46
  66.7 0.4 fusion.20
  67.1 0.4 fusion.19
  67.5 0.4 fusion.41
  67.9 0.5 fusion.127
  68.4 0.2 fusion.29
  68.6 0.2 multiply_reduce_fusion.1
  68.9 3.1 %collective-permute-start.3 = (f32[2,7]{0,1:T(8,128)S(1)}, f32[2,7]{0,1:T(8,128)S(1)}, u32[]{:S(2)}, u32[]{:S(2)}) collective-permute-start(f32[2,7]{0,1:T(8,128)S(1)} %concatenate.15), channel_id=1, source_target_pairs={{0,1},{1,0},{2,3},{3,2},{4,5},{5,4},{6,7},{7,6},{8,9},{9,8},{10,11... | collective-permute-start | bytes 176 | tf_op jit(solution)/shard_map/ppermute | solution.py:38
  72.0 1.2 %collective-permute-done.3 = f32[2,7]{0,1:T(8,128)S(1)} collective-permute-done((f32[2,7]{0,1:T(8,128)S(1)}, f32[2,7]{0,1:T(8,128)S(1)}, u32[]{:S(2)}, u32[]{:S(2)}) %collective-permute-start.3) | collective-permute-done | bytes 88 | tf_op jit(solution)/shard_map/ppermute | solution.py:38
  73.2 7.0 %collective-permute-start.4 = (f32[2,7]{0,1:T(8,128)S(1)}, f32[2,7]{0,1:T(8,128)S(1)}, u32[]{:S(2)}, u32[]{:S(2)}) collective-permute-start(f32[2,7]{0,1:T(8,128)S(1)} %add.219), channel_id=1, source_target_pairs={{0,2},{1,3},{2,0},{3,1},{4,6},{5,7},{6,4},{7,5},{8,10},{9,11},{10,... | collective-permute-start | bytes 176 | tf_op jit(solution)/shard_map/ppermute | solution.py:38
  80.2 1.0 %collective-permute-done.4 = f32[2,7]{0,1:T(8,128)S(1)} collective-permute-done((f32[2,7]{0,1:T(8,128)S(1)}, f32[2,7]{0,1:T(8,128)S(1)}, u32[]{:S(2)}, u32[]{:S(2)}) %collective-permute-start.4) | collective-permute-done | bytes 88 | tf_op jit(solution)/shard_map/ppermute | solution.py:38
  81.2 4.7 %collective-permute-start.5 = (f32[2,7]{0,1:T(8,128)S(1)}, f32[2,7]{0,1:T(8,128)S(1)}, u32[]{:S(2)}, u32[]{:S(2)}) collective-permute-start(f32[2,7]{0,1:T(8,128)S(1)} %add.220), channel_id=1, source_target_pairs={{0,4},{1,5},{2,6},{3,7},{4,0},{5,1},{6,2},{7,3},{8,12},{9,13},{10,... | collective-permute-start | bytes 176 | tf_op jit(solution)/shard_map/ppermute | solution.py:38
  85.9 1.0 %collective-permute-done.5 = f32[2,7]{0,1:T(8,128)S(1)} collective-permute-done((f32[2,7]{0,1:T(8,128)S(1)}, f32[2,7]{0,1:T(8,128)S(1)}, u32[]{:S(2)}, u32[]{:S(2)}) %collective-permute-start.5) | collective-permute-done | bytes 88 | tf_op jit(solution)/shard_map/ppermute | solution.py:38
  86.9 4.7 %collective-permute-start.6 = (f32[2,7]{0,1:T(8,128)S(1)}, f32[2,7]{0,1:T(8,128)S(1)}, u32[]{:S(2)}, u32[]{:S(2)}) collective-permute-start(f32[2,7]{0,1:T(8,128)S(1)} %add.221), channel_id=1, source_target_pairs={{0,8},{1,9},{2,10},{3,11},{4,12},{5,13},{6,14},{7,15},{8,0},{9,1},... | collective-permute-start | bytes 176 | tf_op jit(solution)/shard_map/ppermute | solution.py:38
  91.6 1.0 %collective-permute-done.6 = f32[2,7]{0,1:T(8,128)S(1)} collective-permute-done((f32[2,7]{0,1:T(8,128)S(1)}, f32[2,7]{0,1:T(8,128)S(1)}, u32[]{:S(2)}, u32[]{:S(2)}) %collective-permute-start.6) | collective-permute-done | bytes 88 | tf_op jit(solution)/shard_map/ppermute | solution.py:38
  92.6 0.6 subtract_multiply_fusion
  93.2 0.7 copy.114
  (15 shorter events, 0.1 us)
Async XLA Ops:
  0.6 28.1 %copy-start = (bf16[9,16,16]{2,1,0:T(8,128)(2,1)S(1)}, bf16[9,16,16]{2,1,0:T(8,128)(2,1)}, u32[]{:S(2)}) copy-start(bf16[9,16,16]{2,1,0:T(8,128)(2,1)} %param.11) | copy-start | bytes 13828
  1.4 6.9 %collective-permute-start = (bf16[2,2,128]{2,1,0:T(2,128)(2,1)S(1)}, bf16[2,2,128]{2,1,0:T(2,128)(2,1)S(1)}, u32[]{:S(2)}, u32[]{:S(2)}) collective-permute-start(bf16[2,2,128]{2,1,0:T(2,128)(2,1)S(1)} %get-tuple-element.37), channel_id=1, source_target_pairs={{0,1},{1,2},{2,3},{3,4},{4,5},{5,6},{6,7},{7,8},{8,9},{9,10},{10,1... | collective-permute-start | bytes 3080 | tf_op jit(solution)/shard_map/ppermute | solution.py:20
  4.5 4.3 %collective-permute-start.1 = (bf16[2,2,128]{2,1,0:T(2,128)(2,1)S(1)}, bf16[2,2,128]{2,1,0:T(2,128)(2,1)S(1)}, u32[]{:S(2)}, u32[]{:S(2)}) collective-permute-start(bf16[2,2,128]{2,1,0:T(2,128)(2,1)S(1)} %get-tuple-element.38), channel_id=1, source_target_pairs={{1,0},{2,1},{3,2},{4,3},{5,4},{6,5},{7,6},{8,7},{9,8},{10,9},{11,1... | collective-permute-start | bytes 3080 | tf_op jit(solution)/shard_map/ppermute | solution.py:21
  9.7 13.8 %collective-permute-start.2 = (bf16[2,132,128]{2,1,0:T(8,128)(2,1)S(1)}, bf16[2,132,128]{2,1,0:T(8,128)(2,1)S(1)}, u32[]{:S(2)}, u32[]{:S(2)}) collective-permute-start(bf16[2,132,128]{2,1,0:T(8,128)(2,1)S(1)} %pad_maximum_fusion.1), channel_id=1, source_target_pairs={{16,0},{32,16},{48,32},{64,48},{80,64},{96,80},{112,96},{128,112},... | collective-permute-start | bytes 202760 | tf_op jit(solution)/shard_map/ppermute | solution.py:29
  68.9 4.3 %collective-permute-start.3 = (f32[2,7]{0,1:T(8,128)S(1)}, f32[2,7]{0,1:T(8,128)S(1)}, u32[]{:S(2)}, u32[]{:S(2)}) collective-permute-start(f32[2,7]{0,1:T(8,128)S(1)} %concatenate.15), channel_id=1, source_target_pairs={{0,1},{1,0},{2,3},{3,2},{4,5},{5,4},{6,7},{7,6},{8,9},{9,8},{10,11... | collective-permute-start | bytes 176 | tf_op jit(solution)/shard_map/ppermute | solution.py:38
  73.2 8.0 %collective-permute-start.4 = (f32[2,7]{0,1:T(8,128)S(1)}, f32[2,7]{0,1:T(8,128)S(1)}, u32[]{:S(2)}, u32[]{:S(2)}) collective-permute-start(f32[2,7]{0,1:T(8,128)S(1)} %add.219), channel_id=1, source_target_pairs={{0,2},{1,3},{2,0},{3,1},{4,6},{5,7},{6,4},{7,5},{8,10},{9,11},{10,... | collective-permute-start | bytes 176 | tf_op jit(solution)/shard_map/ppermute | solution.py:38
  81.2 5.7 %collective-permute-start.5 = (f32[2,7]{0,1:T(8,128)S(1)}, f32[2,7]{0,1:T(8,128)S(1)}, u32[]{:S(2)}, u32[]{:S(2)}) collective-permute-start(f32[2,7]{0,1:T(8,128)S(1)} %add.220), channel_id=1, source_target_pairs={{0,4},{1,5},{2,6},{3,7},{4,0},{5,1},{6,2},{7,3},{8,12},{9,13},{10,... | collective-permute-start | bytes 176 | tf_op jit(solution)/shard_map/ppermute | solution.py:38
  86.9 5.7 %collective-permute-start.6 = (f32[2,7]{0,1:T(8,128)S(1)}, f32[2,7]{0,1:T(8,128)S(1)}, u32[]{:S(2)}, u32[]{:S(2)}) collective-permute-start(f32[2,7]{0,1:T(8,128)S(1)} %add.221), channel_id=1, source_target_pairs={{0,8},{1,9},{2,10},{3,11},{4,12},{5,13},{6,14},{7,15},{8,0},{9,1},... | collective-permute-start | bytes 176 | tf_op jit(solution)/shard_map/ppermute | solution.py:38

commit v3 on v2

--- a/solution.py
+++ b/solution.py
@@ -168,10 +168,12 @@
     next_rows = from_behind(padded_rows, "sec", -1)
     row_global = tile_pos * strip_rows - 1 + jnp.arange(strip_rows + 2, dtype=jnp.int32)
     inside = (row_global >= 0) & (row_global < strip_rows * tile_count)
-    all_rows = jnp.concatenate([padded_rows, next_rows], axis=0)
-    all_feats = conv_layers(all_rows, inside, conv1_w, conv1_b, conv2_w)
-    combined_real, combined_imag = patch_spectra(all_feats, cosine, sin_table, rows_per)
-    own_real, own_imag = combined_real[:sec_here], combined_imag[:sec_here]
+    own_feats = conv_layers(padded_rows, inside, conv1_w, conv1_b, conv2_w)
+    own_real, own_imag = patch_spectra(own_feats, cosine, sin_table, rows_per)
+    next_feats = conv_layers(next_rows, inside, conv1_w, conv1_b, conv2_w)
+    next_real, next_imag = patch_spectra(next_feats, cosine, sin_table, rows_per)
+    combined_real = jnp.concatenate([own_real, next_real], axis=0)
+    combined_imag = jnp.concatenate([own_imag, next_imag], axis=0)
     use_first = (offsets == 1)[:, None, None, None, None]
     part_real = jnp.where(
         use_first, combined_real[1 : sec_here + 1], combined_real[2 : sec_here + 2]

time: 94.7 us -> 77.5 us (0.82)
  the two profiles are of different devices: /device:TPU:57 before, /device:TPU:2 now
where the time goes in v3:
time: 77.5 us; the launch traced here: 77 us
  starting transfers between devices  22.6 us (29%)
  matrix products  20.3 us (26%)
  waiting for transfers between devices  15.7 us (20%)
  other arithmetic  15 us (19%)
  local copies, waits for them, and re-layouts  2.27 us (3%)
  between operations  1.03 us (1%)
    ppermute x4, waiting for transfers between devices, tile_sum(): v = v + lax.ppermute(v, axis, [(i, i ^ step) for i in range(peers)])  15.7 us
    dot_general x18, matrix products, conv_layers(): jnp.einsum('schw,co->sohw', window, conv2_w[3 * tap_row + tap_col], prefe...  9.71 us
    ppermute x1, starting transfers between devices, with_halo(): after = lax.ppermute(initial, axis, down)  9.32 us
    ppermute x4, starting transfers between devices, tile_sum(): v = v + lax.ppermute(v, axis, [(i, i ^ step) for i in range(peers)])  8.62 us
    convert_element_type x2, other arithmetic, conv_layers(): jnp.where(inside[None, None, :, None], jax.nn.relu(layer_one), 0.0)  8.24 us
    ppermute x1, starting transfers between devices, with_halo(): before = lax.ppermute(last, axis, up)  3.39 us
  transfers between devices with their start and end apart: 7, of which 4 were waited for; matrix products, arithmetic and copies ran while one was open for 22% of the time, Pallas kernels for 0%

profile of v3, /device:TPU:2, one launch (start us, length us, event | category | flops | bytes accessed | tf_op | source)
XLA Modules:
  0.0 77.0 jit_solution(14776744389421846338)
XLA Ops:
  0.6 0.7 fusion.196
  1.4 3.4 %collective-permute-start = (bf16[2,2,128]{2,1,0:T(2,128)(2,1)S(1)}, bf16[2,2,128]{2,1,0:T(2,128)(2,1)S(1)}, u32[]{:S(2)}, u32[]{:S(2)}) collective-permute-start(bf16[2,2,128]{2,1,0:T(2,128)(2,1)S(1)} %get-tuple-element.40), channel_id=1, source_target_pairs={{0,1},{1,2},{2,3},{3,4},{4,5},{5,6},{6,7},{7,8},{8,9},{9,10},{10,1... | collective-permute-start | bytes 3080 | tf_op jit(solution)/shard_map/ppermute | solution.py:20
  4.8 9.3 %collective-permute-start.1 = (bf16[2,2,128]{2,1,0:T(2,128)(2,1)S(1)}, bf16[2,2,128]{2,1,0:T(2,128)(2,1)S(1)}, u32[]{:S(2)}, u32[]{:S(2)}) collective-permute-start(bf16[2,2,128]{2,1,0:T(2,128)(2,1)S(1)} %get-tuple-element.41), channel_id=1, source_target_pairs={{1,0},{2,1},{3,2},{4,3},{5,4},{6,5},{7,6},{8,7},{9,8},{10,9},{11,1... | collective-permute-start | bytes 3080 | tf_op jit(solution)/shard_map/ppermute | solution.py:21
  14.1 1.0 %bitcast_convert_fusion.8 = (f32[16]{0:T(128)S(1)}, f32[16]{0:T(128)S(1)}, f32[16]{0:T(128)S(1)}, f32[16]{0:T(128)S(1)}, f32[16]{0:T(128)S(1)}, /*index=5*/f32[1...) fusion(bf16[9,16]{1,0:T(8,128)(2,1)} %param.9), kind=kLoop, calls=%fused_computation.193 | loop fusion | flops 144 | bytes 864 | tf_op jit(solution)/shard_map/convert_element_type | solution.py:63
  15.1 0.7 compare_not_fusion
  15.9 0.7 broadcast_multiply_fusion
  16.6 0.9 %pad_maximum_fusion.2 = bf16[2,132,128]{2,1,0:T(8,128)(2,1)S(1)} fusion(bf16[2,2,128]{2,1,0:T(2,128)(2,1)S(1)} %collective-permute-done.1, bf16[2,128,128]{2,1,0:T(8,128)(2,1)} %param.6, bf16[2,2,128]{2,1,0:T(2,128)(2,1)S(1)} %collective-permute-done), kind=kLoop, calls=%fused_computation.105 | loop fusion | flops 202752 | bytes 135168 | tf_op jit(solution)/shard_map/concatenate | solution.py:22
  17.5 1.3 %collective-permute-start.2 = (bf16[2,132,128]{2,1,0:T(8,128)(2,1)S(1)}, bf16[2,132,128]{2,1,0:T(8,128)(2,1)S(1)}, u32[]{:S(2)}, u32[]{:S(2)}) collective-permute-start(bf16[2,132,128]{2,1,0:T(8,128)(2,1)S(1)} %pad_maximum_fusion.2), channel_id=1, source_target_pairs={{16,0},{32,16},{48,32},{64,48},{80,64},{96,80},{112,96},{128,112},... | collective-permute-start | bytes 202760 | tf_op jit(solution)/shard_map/ppermute | solution.py:29
  18.8 1.1 %fusion.37 = (f32[2,130,128]{2,1,0:T(8,128)S(1)}, f32[2,130,128]{2,1,0:T(8,128)S(1)}, f32[2,130,128]{2,1,0:T(8,128)S(1)}, f32[2,130,128]{2,1,0:T(8,128)S(1)}, f3...) fusion(bf16[2,132,128]{2,1,0:T(8,128)(2,1)S(1)} %pad_maximum_fu, ...), kind=kLoop, calls=%fused_computation.89 | loop fusion | flops 499200 | bytes 1404928 | tf_op jit(solution)/shard_map/convert_element_type | solution.py:64
  19.9 4.4 %select_convert_fusion.1 = bf16[2,16,130,128]{3,1,2,0:T(8,128)(2,1)S(1)} fusion(f32[2,130,128]{2,1,0:T(8,128)S(1)} %get-tuple-element.36, f32[16]{0:T(128)S(1)} %get-tuple-element.54, f32[2,130,128]{2,1,0:T(8,128)S(1)} %get-tuple-element.66, f32[16]{0:T(128)S(1)} %get-tuple-element.55, f32[2,130,128]{2,1,0:T(8,128)S(1)} %get-tuple-element.35, ...), kind=kLoop, calls=%fused_computation.21 | loop fusion | flops 11182080 | bytes 2263810 | tf_op jit(solution)/shard_map/convert_element_type | solution.py:68
  24.4 0.5 fusion.10
  24.8 0.5 fusion.11
  25.3 0.5 fusion.12
  25.8 0.5 fusion.13
  26.3 0.4 fusion.27
  26.8 0.5 fusion.29
  27.2 0.5 fusion.31
  27.7 0.5 fusion.9
  28.2 1.1 %fusion.4 = bf16[2,16,128,128]{3,1,2,0:T(8,128)(2,1)S(1)} fusion(f32[2,128,128,16]{2,3,1,0:T(8,128)S(1)} %fusion.27, f32[2,128,128,16]{2,3,1,0:T(8,128)S(1)} %fusion.13, f32[2,128,128,16]{2,3,1,0:T(8,128)S(1)} %fusion.12, f32[2,128,128,16]{2,3,1,0:T(8,128)S(1)} %fusion.29, f32[2,128,128,16]{2,3,1,0:T(8,128)S(1)} %fusion.11, ...), kind=kOutput, calls=%fused_computation.32 | convolution fusion | flops 21495808 | bytes 18894848 | tf_op jit(solution)/shard_map/schw,co->sohw/dot_general | solution.py:76
  29.2 0.3 copy.123
  29.5 0.7 convolution_convert_fusion.3
  30.2 0.7 convolution_convert_fusion.2
  30.9 0.7 fusion.68
  31.5 0.7 fusion.58
  32.2 0.7 subtract_convert_fusion.1
  32.9 0.7 negate_convert_fusion.1
  33.6 0.2 fusion.43
  33.8 3.8 %select_convert_fusion = bf16[2,16,130,128]{3,1,2,0:T(8,128)(2,1)S(1)} fusion(f32[2,130,128]{2,1,0:T(8,128)S(1)} %get-tuple-element.27, f32[2,130,128]{2,1,0:T(8,128)S(1)} %get-tuple-element.28, f32[2,130,128]{2,1,0:T(8,128)S(1)} %get-tuple-element.26, f32[2,130,128]{2,1,0:T(8,128)S(1)} %get-tuple-element.25, f32[2,130,128]{2,1,0:T(8,128)S(1)} %get-tuple-element.29, ...), kind=kLoop, calls=%fused_computation.20 | loop fusion | flops 11182080 | bytes 2263810 | tf_op jit(solution)/shard_map/convert_element_type | solution.py:68
  37.7 0.5 fusion.14
  38.1 0.5 fusion.15
  38.6 0.5 fusion.16
  39.1 0.5 fusion.17
  39.6 0.5 fusion.18
  40.1 0.4 fusion.21
  40.5 0.5 fusion.23
  41.0 0.5 fusion.25
  41.5 1.1 %fusion.5 = bf16[2,16,128,128]{3,1,2,0:T(8,128)(2,1)S(1)} fusion(f32[2,128,128,16]{2,3,1,0:T(8,128)S(1)} %fusion.21, f32[2,128,128,16]{2,3,1,0:T(8,128)S(1)} %fusion.18, f32[2,128,128,16]{2,3,1,0:T(8,128)S(1)} %fusion.17, f32[2,128,128,16]{2,3,1,0:T(8,128)S(1)} %fusion.23, f32[2,128,128,16]{2,3,1,0:T(8,128)S(1)} %fusion.16, ...), kind=kOutput, calls=%fused_computation.33 | convolution fusion | flops 21495808 | bytes 18894848 | tf_op jit(solution)/shard_map/schw,co->sohw/dot_general | solution.py:76
  42.5 0.3 copy.126
  42.8 0.7 convolution_convert_fusion.1
  43.5 0.7 convolution_convert_fusion
  44.2 0.7 fusion.66
  44.8 0.7 fusion.56
  45.5 0.7 subtract_convert_fusion
  46.2 0.7 negate_convert_fusion
  46.9 1.1 %fusion.3 = (bf16[2,128,128]{1,2,0:T(8,128)(2,1)S(1)}, bf16[2,128,128]{1,2,0:T(8,128)(2,1)S(1)}) fusion(bf16[2,1,16,128,128]{3,4,2,0,1:T(8,128)(2,1)S(1)} %bitcast.261, bf16[2,1,16,128,128]{3,4,2,0,1:T(8,128)(2,1)S(1)} %bitcast.260, bf16[2,1,16,128,128]{3,4,2,0,1:T(8,128)(2,1)S(1)} %bitcast.263, bf16[2,1,16,128,128]{3,4,2,0,1:T(8,128)(2,1)S(1)} %bitcast.262, ...), kind=kLoop, calls=%fused_computation.25 | loop fusion | flops 11468800 | bytes 4325378 | tf_op jit(solution)/shard_map/reduce_sum | solution.py:124
  48.1 0.1 copy.134
  48.4 0.4 fusion.71
  48.7 0.4 fusion.70
  49.1 0.4 fusion.8
  49.5 0.4 fusion.7
  49.9 0.4 fusion.62
  50.3 0.5 fusion.197
  50.9 0.2 fusion.35
  51.0 0.2 multiply_reduce_fusion.1
  51.3 2.9 %collective-permute-start.3 = (f32[2,7]{0,1:T(8,128)S(1)}, f32[2,7]{0,1:T(8,128)S(1)}, u32[]{:S(2)}, u32[]{:S(2)}) collective-permute-start(f32[2,7]{0,1:T(8,128)S(1)} %concatenate.27), channel_id=1, source_target_pairs={{0,1},{1,0},{2,3},{3,2},{4,5},{5,4},{6,7},{7,6},{8,9},{9,8},{10,11... | collective-permute-start | bytes 176 | tf_op jit(solution)/shard_map/ppermute | solution.py:38
  54.2 2.6 %collective-permute-done.3 = f32[2,7]{0,1:T(8,128)S(1)} collective-permute-done((f32[2,7]{0,1:T(8,128)S(1)}, f32[2,7]{0,1:T(8,128)S(1)}, u32[]{:S(2)}, u32[]{:S(2)}) %collective-permute-start.3) | collective-permute-done | bytes 88 | tf_op jit(solution)/shard_map/ppermute | solution.py:38
  56.8 1.9 %collective-permute-start.4 = (f32[2,7]{0,1:T(8,128)S(1)}, f32[2,7]{0,1:T(8,128)S(1)}, u32[]{:S(2)}, u32[]{:S(2)}) collective-permute-start(f32[2,7]{0,1:T(8,128)S(1)} %add.310), channel_id=1, source_target_pairs={{0,2},{1,3},{2,0},{3,1},{4,6},{5,7},{6,4},{7,5},{8,10},{9,11},{10,... | collective-permute-start | bytes 176 | tf_op jit(solution)/shard_map/ppermute | solution.py:38
  58.7 5.1 %collective-permute-done.4 = f32[2,7]{0,1:T(8,128)S(1)} collective-permute-done((f32[2,7]{0,1:T(8,128)S(1)}, f32[2,7]{0,1:T(8,128)S(1)}, u32[]{:S(2)}, u32[]{:S(2)}) %collective-permute-start.4) | collective-permute-done | bytes 88 | tf_op jit(solution)/shard_map/ppermute | solution.py:38
  63.8 1.9 %collective-permute-start.5 = (f32[2,7]{0,1:T(8,128)S(1)}, f32[2,7]{0,1:T(8,128)S(1)}, u32[]{:S(2)}, u32[]{:S(2)}) collective-permute-start(f32[2,7]{0,1:T(8,128)S(1)} %add.311), channel_id=1, source_target_pairs={{0,4},{1,5},{2,6},{3,7},{4,0},{5,1},{6,2},{7,3},{8,12},{9,13},{10,... | collective-permute-start | bytes 176 | tf_op jit(solution)/shard_map/ppermute | solution.py:38
  65.7 3.6 %collective-permute-done.5 = f32[2,7]{0,1:T(8,128)S(1)} collective-permute-done((f32[2,7]{0,1:T(8,128)S(1)}, f32[2,7]{0,1:T(8,128)S(1)}, u32[]{:S(2)}, u32[]{:S(2)}) %collective-permute-start.5) | collective-permute-done | bytes 88 | tf_op jit(solution)/shard_map/ppermute | solution.py:38
  69.3 1.9 %collective-permute-start.6 = (f32[2,7]{0,1:T(8,128)S(1)}, f32[2,7]{0,1:T(8,128)S(1)}, u32[]{:S(2)}, u32[]{:S(2)}) collective-permute-start(f32[2,7]{0,1:T(8,128)S(1)} %add.312), channel_id=1, source_target_pairs={{0,8},{1,9},{2,10},{3,11},{4,12},{5,13},{6,14},{7,15},{8,0},{9,1},... | collective-permute-start | bytes 176 | tf_op jit(solution)/shard_map/ppermute | solution.py:38
  71.2 4.5 %collective-permute-done.6 = f32[2,7]{0,1:T(8,128)S(1)} collective-permute-done((f32[2,7]{0,1:T(8,128)S(1)}, f32[2,7]{0,1:T(8,128)S(1)}, u32[]{:S(2)}, u32[]{:S(2)}) %collective-permute-start.6) | collective-permute-done | bytes 88 | tf_op jit(solution)/shard_map/ppermute | solution.py:38
  75.7 0.6 subtract_multiply_fusion
  76.3 0.7 copy.138
  (27 shorter events, 0.5 us)
Async XLA Ops:
  0.6 23.7 %copy-start = (bf16[9,16,16]{2,1,0:T(8,128)(2,1)S(1)}, bf16[9,16,16]{2,1,0:T(8,128)(2,1)}, u32[]{:S(2)}) copy-start(bf16[9,16,16]{2,1,0:T(8,128)(2,1)} %param.11) | copy-start | bytes 13828
  1.4 15.3 %collective-permute-start = (bf16[2,2,128]{2,1,0:T(2,128)(2,1)S(1)}, bf16[2,2,128]{2,1,0:T(2,128)(2,1)S(1)}, u32[]{:S(2)}, u32[]{:S(2)}) collective-permute-start(bf16[2,2,128]{2,1,0:T(2,128)(2,1)S(1)} %get-tuple-element.40), channel_id=1, source_target_pairs={{0,1},{1,2},{2,3},{3,4},{4,5},{5,6},{6,7},{7,8},{8,9},{9,10},{10,1... | collective-permute-start | bytes 3080 | tf_op jit(solution)/shard_map/ppermute | solution.py:20
  4.8 11.9 %collective-permute-start.1 = (bf16[2,2,128]{2,1,0:T(2,128)(2,1)S(1)}, bf16[2,2,128]{2,1,0:T(2,128)(2,1)S(1)}, u32[]{:S(2)}, u32[]{:S(2)}) collective-permute-start(bf16[2,2,128]{2,1,0:T(2,128)(2,1)S(1)} %get-tuple-element.41), channel_id=1, source_target_pairs={{1,0},{2,1},{3,2},{4,3},{5,4},{6,5},{7,6},{8,7},{9,8},{10,9},{11,1... | collective-permute-start | bytes 3080 | tf_op jit(solution)/shard_map/ppermute | solution.py:21
  17.5 16.1 %collective-permute-start.2 = (bf16[2,132,128]{2,1,0:T(8,128)(2,1)S(1)}, bf16[2,132,128]{2,1,0:T(8,128)(2,1)S(1)}, u32[]{:S(2)}, u32[]{:S(2)}) collective-permute-start(bf16[2,132,128]{2,1,0:T(8,128)(2,1)S(1)} %pad_maximum_fusion.2), channel_id=1, source_target_pairs={{16,0},{32,16},{48,32},{64,48},{80,64},{96,80},{112,96},{128,112},... | collective-permute-start | bytes 202760 | tf_op jit(solution)/shard_map/ppermute | solution.py:29
  32.9 0.9 %copy-start.1 = (f32[16]{0:T(128)S(1)}, f32[16]{0:T(128)}, u32[]{:S(2)}) copy-start(f32[16]{0:T(128)} %param.10) | copy-start | bytes 196
  51.3 5.5 %collective-permute-start.3 = (f32[2,7]{0,1:T(8,128)S(1)}, f32[2,7]{0,1:T(8,128)S(1)}, u32[]{:S(2)}, u32[]{:S(2)}) collective-permute-start(f32[2,7]{0,1:T(8,128)S(1)} %concatenate.27), channel_id=1, source_target_pairs={{0,1},{1,0},{2,3},{3,2},{4,5},{5,4},{6,7},{7,6},{8,9},{9,8},{10,11... | collective-permute-start | bytes 176 | tf_op jit(solution)/shard_map/ppermute | solution.py:38
  56.8 7.0 %collective-permute-start.4 = (f32[2,7]{0,1:T(8,128)S(1)}, f32[2,7]{0,1:T(8,128)S(1)}, u32[]{:S(2)}, u32[]{:S(2)}) collective-permute-start(f32[2,7]{0,1:T(8,128)S(1)} %add.310), channel_id=1, source_target_pairs={{0,2},{1,3},{2,0},{3,1},{4,6},{5,7},{6,4},{7,5},{8,10},{9,11},{10,... | collective-permute-start | bytes 176 | tf_op jit(solution)/shard_map/ppermute | solution.py:38
  63.8 5.5 %collective-permute-start.5 = (f32[2,7]{0,1:T(8,128)S(1)}, f32[2,7]{0,1:T(8,128)S(1)}, u32[]{:S(2)}, u32[]{:S(2)}) collective-permute-start(f32[2,7]{0,1:T(8,128)S(1)} %add.311), channel_id=1, source_target_pairs={{0,4},{1,5},{2,6},{3,7},{4,0},{5,1},{6,2},{7,3},{8,12},{9,13},{10,... | collective-permute-start | bytes 176 | tf_op jit(solution)/shard_map/ppermute | solution.py:38
  69.3 6.4 %collective-permute-start.6 = (f32[2,7]{0,1:T(8,128)S(1)}, f32[2,7]{0,1:T(8,128)S(1)}, u32[]{:S(2)}, u32[]{:S(2)}) collective-permute-start(f32[2,7]{0,1:T(8,128)S(1)} %add.312), channel_id=1, source_target_pairs={{0,8},{1,9},{2,10},{3,11},{4,12},{5,13},{6,14},{7,15},{8,0},{9,1},... | collective-permute-start | bytes 176 | tf_op jit(solution)/shard_map/ppermute | solution.py:38

commit v4 on v3

--- a/solution.py
+++ b/solution.py
@@ -31,14 +31,8 @@
 
 def tile_sum(v, axis):
     peers = lax.axis_size(axis)
-    if peers & (peers - 1):
-        return lax.psum(v, axis)
-    step = 1
-    while step < peers:
-        v = v + lax.ppermute(v, axis, [(i, i ^ step) for i in range(peers)])
-        step *= 2
-    return v
-
+    copies = jnp.broadcast_to(v[None], (peers,) + v.shape)
+    return jnp.sum(lax.all_to_all(copies, axis, 0, 0, tiled=False), axis=0)
 
 def dft_tables(patch_len):
     index_row = jnp.arange(patch_len, dtype=jnp.int32)

time: 77.5 us -> 66.6 us (0.86)
  the two profiles are of different devices: /device:TPU:2 before, /device:TPU:57 now
where the time goes in v4:
time: 66.6 us; the launch traced here: 65.4 us
  matrix products  20.3 us (30%)
  blocking collectives  17.1 us (26%)
  other arithmetic  15.1 us (23%)
  starting transfers between devices  8.41 us (13%)
  local copies, waits for them, and re-layouts  3.35 us (5%)
  between operations  0.99 us (1%)
    all_to_all x1, blocking collectives, tile_sum(): return jnp.sum(lax.all_to_all(copies, axis, 0, 0, tiled=False), axis=0)  17.1 us
    dot_general x18, matrix products, conv_layers(): jnp.einsum('schw,co->sohw', window, conv2_w[3 * tap_row + tap_col], prefe...  9.71 us
    convert_element_type x2, other arithmetic, conv_layers(): jnp.where(inside[None, None, :, None], jax.nn.relu(layer_one), 0.0)  8.24 us
    ppermute x1, starting transfers between devices, from_behind(): return lax.ppermute(block, axis, route)  4.01 us
    ppermute x1, starting transfers between devices, with_halo(): before = lax.ppermute(last, axis, up)  3.1 us
    dot_general x2, matrix products, patch_spectra(): jnp.einsum('uy,byk->buk', sin_table, half_sin, preferred_element_type=jnp...  1.38 us
    dot_general x2, matrix products, patch_spectra(): jnp.einsum('uy,byk->buk', sin_table, half_cos, preferred_element_type=jnp...  1.37 us
    dot_general x2, matrix products, patch_spectra(): jnp.einsum('uy,byk->buk', cosine, half_sin, preferred_element_type=jnp.fl...  1.37 us
  transfers between devices with their start and end apart: 3, of which 1 were waited for; matrix products, arithmetic and copies ran while one was open for 27% of the time, Pallas kernels for 0%

profile of v4, /device:TPU:57, one launch (start us, length us, event | category | flops | bytes accessed | tf_op | source)
XLA Modules:
  0.0 65.4 jit_solution(6436726437153054412)
XLA Ops:
  0.6 0.7 %fusion.196 = (bf16[2,2,128]{2,1,0:T(2,128)(2,1)S(1)}, bf16[2,2,128]{2,1,0:T(2,128)(2,1)S(1)}) fusion(bf16[2,128,128]{2,1,0:T(8,128)(2,1)} %param.6), kind=kLoop, calls=%fused_computation.292 | loop fusion | bytes 4096 | tf_op jit(solution)/shard_map/slice | solution.py:18
  1.4 3.1 %collective-permute-start = (bf16[2,2,128]{2,1,0:T(2,128)(2,1)S(1)}, bf16[2,2,128]{2,1,0:T(2,128)(2,1)S(1)}, u32[]{:S(2)}, u32[]{:S(2)}) collective-permute-start(bf16[2,2,128]{2,1,0:T(2,128)(2,1)S(1)} %get-tuple-element.44), channel_id=1, source_target_pairs={{0,1},{1,2},{2,3},{3,4},{4,5},{5,6},{6,7},{7,8},{8,9},{9,10},{10,1... | collective-permute-start | bytes 3080 | tf_op jit(solution)/shard_map/ppermute | solution.py:20
  4.5 1.3 %collective-permute-start.1 = (bf16[2,2,128]{2,1,0:T(2,128)(2,1)S(1)}, bf16[2,2,128]{2,1,0:T(2,128)(2,1)S(1)}, u32[]{:S(2)}, u32[]{:S(2)}) collective-permute-start(bf16[2,2,128]{2,1,0:T(2,128)(2,1)S(1)} %get-tuple-element.45), channel_id=1, source_target_pairs={{1,0},{2,1},{3,2},{4,3},{5,4},{6,5},{7,6},{8,7},{9,8},{10,9},{11,1... | collective-permute-start | bytes 3080 | tf_op jit(solution)/shard_map/ppermute | solution.py:21
  5.8 1.0 %bitcast_convert_fusion.8 = (f32[16]{0:T(128)S(1)}, f32[16]{0:T(128)S(1)}, f32[16]{0:T(128)S(1)}, f32[16]{0:T(128)S(1)}, f32[16]{0:T(128)S(1)}, /*index=5*/f32[1...) fusion(bf16[9,16]{1,0:T(8,128)(2,1)} %param.9), kind=kLoop, calls=%fused_computation.195 | loop fusion | flops 144 | bytes 864 | tf_op jit(solution)/shard_map/convert_element_type | solution.py:57
  6.8 0.7 %compare_not_fusion = (pred[2]{0:T(512)(128)(4,1)S(1)}, pred[2]{0:T(512)(128)(4,1)S(1)}) fusion(s32[2]{0:T(128)} %param.7, s32[]{:T(128)S(6)} %mul.529), kind=kLoop, calls=%fused_computation.174 | loop fusion | flops 10 | bytes 16 | tf_op jit(solution)/shard_map/not | solution.py:119
  7.6 0.7 %broadcast_multiply_fusion = (f32[2,1]{0,1:T(1,128)S(1)}, f32[2,1]{0,1:T(1,128)S(1)}, f32[2,1]{0,1:T(1,128)S(1)}) fusion(f32[]{:T(128)S(6)} %sub.70, s32[2]{0:T(128)} %param.7, s32[]{:T(128)S(6)} %mul.529, s32[2,1]{0,1:T(1,128)} %param.8), kind=kLoop, calls=%fused_computation.205 | loop fusion | flops 16 | bytes 48 | tf_op jit(solution)/shard_map/mul | solution.py:195
  8.3 0.1 copy.198
  8.6 0.2 collective-permute-done.1
  8.8 0.9 %pad_maximum_fusion.2 = bf16[2,132,128]{2,1,0:T(8,128)(2,1)S(1)} fusion(bf16[2,2,128]{2,1,0:T(2,128)(2,1)S(1)} %collective-permute-done.1, bf16[2,128,128]{2,1,0:T(8,128)(2,1)} %param.6, bf16[2,2,128]{2,1,0:T(2,128)(2,1)S(1)} %collective-permute-done), kind=kLoop, calls=%fused_computation.105 | loop fusion | flops 202752 | bytes 135168 | tf_op jit(solution)/shard_map/concatenate | solution.py:22
  9.7 4.0 %collective-permute-start.2 = (bf16[2,132,128]{2,1,0:T(8,128)(2,1)S(1)}, bf16[2,132,128]{2,1,0:T(8,128)(2,1)S(1)}, u32[]{:S(2)}, u32[]{:S(2)}) collective-permute-start(bf16[2,132,128]{2,1,0:T(8,128)(2,1)S(1)} %pad_maximum_fusion.2), channel_id=1, source_target_pairs={{16,0},{32,16},{48,32},{64,48},{80,64},{96,80},{112,96},{128,112},... | collective-permute-start | bytes 202760 | tf_op jit(solution)/shard_map/ppermute | solution.py:29
  13.7 1.1 %fusion.37 = (f32[2,130,128]{2,1,0:T(8,128)S(1)}, f32[2,130,128]{2,1,0:T(8,128)S(1)}, f32[2,130,128]{2,1,0:T(8,128)S(1)}, f32[2,130,128]{2,1,0:T(8,128)S(1)}, f3...) fusion(bf16[2,132,128]{2,1,0:T(8,128)(2,1)S(1)} %pad_maximum_fu, ...), kind=kLoop, calls=%fused_computation.89 | loop fusion | flops 499200 | bytes 1404928 | tf_op jit(solution)/shard_map/convert_element_type | solution.py:58
  14.8 4.4 %select_convert_fusion.1 = bf16[2,16,130,128]{3,1,2,0:T(8,128)(2,1)S(1)} fusion(f32[2,130,128]{2,1,0:T(8,128)S(1)} %get-tuple-element.40, f32[16]{0:T(128)S(1)} %get-tuple-element.55, f32[2,130,128]{2,1,0:T(8,128)S(1)} %get-tuple-element.72, f32[16]{0:T(128)S(1)} %get-tuple-element.56, f32[2,130,128]{2,1,0:T(8,128)S(1)} %get-tuple-element.39, ...), kind=kLoop, calls=%fused_computation.21 | loop fusion | flops 11182080 | bytes 2263810 | tf_op jit(solution)/shard_map/convert_element_type | solution.py:62
  19.2 0.5 fusion.10
  19.7 0.5 fusion.11
  20.2 0.5 fusion.12
  20.7 0.5 fusion.13
  21.2 0.4 fusion.27
  21.6 0.5 fusion.29
  22.1 0.5 fusion.31
  22.5 0.5 fusion.9
  23.0 1.1 %fusion.4 = bf16[2,16,128,128]{3,1,2,0:T(8,128)(2,1)S(1)} fusion(f32[2,128,128,16]{2,3,1,0:T(8,128)S(1)} %fusion.27, f32[2,128,128,16]{2,3,1,0:T(8,128)S(1)} %fusion.13, f32[2,128,128,16]{2,3,1,0:T(8,128)S(1)} %fusion.12, f32[2,128,128,16]{2,3,1,0:T(8,128)S(1)} %fusion.29, f32[2,128,128,16]{2,3,1,0:T(8,128)S(1)} %fusion.11, ...), kind=kOutput, calls=%fused_computation.32 | convolution fusion | flops 21495808 | bytes 18894848 | tf_op jit(solution)/shard_map/schw,co->sohw/dot_general | solution.py:70
  24.1 0.3 copy.184
  24.4 0.7 %convolution_convert_fusion.3 = bf16[4096,128]{1,0:T(8,128)(2,1)S(1)} fusion(bf16[4096,128]{1,0:T(8,128)(2,1)S(1)} %bitcast.246), kind=kOutput, calls=%fused_computation.3 | convolution fusion | flops 134987776 | bytes 2097152 | tf_op jit(solution)/shard_map/dot_general | solution.py:85
  25.0 0.7 %convolution_convert_fusion.2 = bf16[4096,128]{1,0:T(8,128)(2,1)S(1)} fusion(bf16[4096,128]{1,0:T(8,128)(2,1)S(1)} %bitcast.247), kind=kOutput, calls=%fused_computation.2 | convolution fusion | flops 134987776 | bytes 2097152 | tf_op jit(solution)/shard_map/dot_general | solution.py:90
  25.7 0.7 %fusion.68 = f32[32,128,128]{2,1,0:T(8,128)S(1)} fusion(bf16[32,128,128]{2,1,0:T(8,128)(2,1)S(1)} %bitcast.242), kind=kOutput, calls=%fused_computation.129 | convolution fusion | flops 134463488 | bytes 3145728 | tf_op jit(solution)/shard_map/uy,byk->buk/dot_general | solution.py:94
  26.4 0.7 %fusion.58 = f32[32,128,128]{2,1,0:T(8,128)S(1)} fusion(bf16[32,128,128]{2,1,0:T(8,128)(2,1)S(1)} %bitcast.243), kind=kOutput, calls=%fused_computation.119 | convolution fusion | flops 134463488 | bytes 3145728 | tf_op jit(solution)/shard_map/uy,byk->buk/dot_general | solution.py:98
  27.1 0.7 %subtract_convert_fusion.1 = bf16[32,128,128]{2,1,0:T(8,128)(2,1)S(1)} fusion(f32[32,128,128]{2,1,0:T(8,128)S(1)} %fusion.68, bf16[32,128,128]{2,1,0:T(8,128)(2,1)S(1)} %bitcast.250), kind=kOutput, calls=%fused_computation.31 | convolution fusion | flops 135512064 | bytes 4194304 | tf_op jit(solution)/shard_map/uy,byk->buk/dot_general | solution.py:96
  27.8 0.7 %negate_convert_fusion.1 = bf16[32,128,128]{2,1,0:T(8,128)(2,1)S(1)} fusion(f32[32,128,128]{2,1,0:T(8,128)S(1)} %fusion.58, bf16[32,128,128]{2,1,0:T(8,128)(2,1)S(1)} %bitcast.251), kind=kOutput, calls=%fused_computation.29 | convolution fusion | flops 136036352 | bytes 4194304 | tf_op jit(solution)/shard_map/uy,byk->buk/dot_general | solution.py:99
  28.5 0.2 fusion.43
  28.7 3.8 %select_convert_fusion = bf16[2,16,130,128]{3,1,2,0:T(8,128)(2,1)S(1)} fusion(f32[2,130,128]{2,1,0:T(8,128)S(1)} %get-tuple-element.31, f32[2,130,128]{2,1,0:T(8,128)S(1)} %get-tuple-element.32, f32[2,130,128]{2,1,0:T(8,128)S(1)} %get-tuple-element.30, f32[2,130,128]{2,1,0:T(8,128)S(1)} %get-tuple-element.29, f32[2,130,128]{2,1,0:T(8,128)S(1)} %get-tuple-element.33, ...), kind=kLoop, calls=%fused_computation.20 | loop fusion | flops 11182080 | bytes 2263810 | tf_op jit(solution)/shard_map/convert_element_type | solution.py:62
  32.5 0.5 fusion.14
  33.0 0.5 fusion.15
  33.5 0.5 fusion.16
  34.0 0.5 fusion.17
  34.5 0.5 fusion.18
  35.0 0.4 fusion.21
  35.4 0.5 fusion.23
  35.9 0.5 fusion.25
  36.3 1.1 %fusion.5 = bf16[2,16,128,128]{3,1,2,0:T(8,128)(2,1)S(1)} fusion(f32[2,128,128,16]{2,3,1,0:T(8,128)S(1)} %fusion.21, f32[2,128,128,16]{2,3,1,0:T(8,128)S(1)} %fusion.18, f32[2,128,128,16]{2,3,1,0:T(8,128)S(1)} %fusion.17, f32[2,128,128,16]{2,3,1,0:T(8,128)S(1)} %fusion.23, f32[2,128,128,16]{2,3,1,0:T(8,128)S(1)} %fusion.16, ...), kind=kOutput, calls=%fused_computation.33 | convolution fusion | flops 21495808 | bytes 18894848 | tf_op jit(solution)/shard_map/schw,co->sohw/dot_general | solution.py:70
  37.4 0.3 copy.187
  37.7 0.7 convolution_convert_fusion.1
  38.3 0.7 %convolution_convert_fusion = bf16[4096,128]{1,0:T(8,128)(2,1)S(1)} fusion(bf16[4096,128]{1,0:T(8,128)(2,1)S(1)} %bitcast.249), kind=kOutput, calls=%fused_computation | convolution fusion | flops 134987776 | bytes 2097152 | tf_op jit(solution)/shard_map/dot_general | solution.py:90
  39.0 0.7 %fusion.66 = f32[32,128,128]{2,1,0:T(8,128)S(1)} fusion(bf16[32,128,128]{2,1,0:T(8,128)(2,1)S(1)} %bitcast.244), kind=kOutput, calls=%fused_computation.127 | convolution fusion | flops 134463488 | bytes 3145728 | tf_op jit(solution)/shard_map/uy,byk->buk/dot_general | solution.py:94
  39.7 0.7 %fusion.56 = f32[32,128,128]{2,1,0:T(8,128)S(1)} fusion(bf16[32,128,128]{2,1,0:T(8,128)(2,1)S(1)} %bitcast.245), kind=kOutput, calls=%fused_computation.117 | convolution fusion | flops 134463488 | bytes 3145728 | tf_op jit(solution)/shard_map/uy,byk->buk/dot_general | solution.py:98
  40.4 0.7 %subtract_convert_fusion = bf16[32,128,128]{2,1,0:T(8,128)(2,1)S(1)} fusion(f32[32,128,128]{2,1,0:T(8,128)S(1)} %fusion.66, bf16[32,128,128]{2,1,0:T(8,128)(2,1)S(1)} %bitcast.252), kind=kOutput, calls=%fused_computation.30 | convolution fusion | flops 135512064 | bytes 4194304 | tf_op jit(solution)/shard_map/uy,byk->buk/dot_general | solution.py:96
  41.1 0.7 %negate_convert_fusion = bf16[32,128,128]{2,1,0:T(8,128)(2,1)S(1)} fusion(f32[32,128,128]{2,1,0:T(8,128)S(1)} %fusion.56, bf16[32,128,128]{2,1,0:T(8,128)(2,1)S(1)} %bitcast.253), kind=kOutput, calls=%fused_computation.28 | convolution fusion | flops 136036352 | bytes 4194304 | tf_op jit(solution)/shard_map/uy,byk->buk/dot_general | solution.py:99
  41.8 1.1 %fusion.3 = (bf16[2,128,128]{1,2,0:T(8,128)(2,1)S(1)}, bf16[2,128,128]{1,2,0:T(8,128)(2,1)S(1)}) fusion(bf16[2,1,16,128,128]{3,4,2,0,1:T(8,128)(2,1)S(1)} %bitcast.255, bf16[2,1,16,128,128]{3,4,2,0,1:T(8,128)(2,1)S(1)} %bitcast.254, bf16[2,1,16,128,128]{3,4,2,0,1:T(8,128)(2,1)S(1)} %bitcast.257, bf16[2,1,16,128,128]{3,4,2,0,1:T(8,128)(2,1)S(1)} %bitcast.256, ...), kind=kLoop, calls=%fused_computation.25 | loop fusion | flops 11468800 | bytes 4325378 | tf_op jit(solution)/shard_map/reduce_sum | solution.py:118
  42.8 0.1 copy.194
  43.0 0.1 copy.195
  43.1 0.1 fusion.33
  43.2 0.4 fusion.71
  43.6 0.4 fusion.70
  44.0 0.4 fusion.8
  44.4 0.4 fusion.7
  44.8 0.4 fusion.62
  45.2 0.5 fusion.198
  45.7 0.2 fusion.35
  45.9 0.2 multiply_reduce_fusion.1
  46.1 0.1 copy.201
  46.2 0.1 copy.202
  46.3 0.1 concatenate.27
  46.4 17.1 %all_to_all.5 = f32[16,2,7]{2,1,0:T(2,128)S(1)} all-to-all(f32[16,2,7]{2,1,0:T(2,128)S(1)} %broadcast_in_dim.39), channel_id=1, replica_groups=mesh['sec'=48,'tile'=16] {'tile'}, dimensions={0} | all-to-all | bytes 1792 | tf_op jit(solution)/shard_map/all_to_all | solution.py:35
  64.1 0.6 subtract_multiply_fusion
  64.7 0.7 copy.205
  (29 shorter events, 1.1 us)
Async XLA Ops:
  0.6 18.6 %copy-start = (bf16[9,16,16]{2,1,0:T(8,128)(2,1)S(1)}, bf16[9,16,16]{2,1,0:T(8,128)(2,1)}, u32[]{:S(2)}) copy-start(bf16[9,16,16]{2,1,0:T(8,128)(2,1)} %param.11) | copy-start | bytes 13828
  1.4 7.2 %collective-permute-start = (bf16[2,2,128]{2,1,0:T(2,128)(2,1)S(1)}, bf16[2,2,128]{2,1,0:T(2,128)(2,1)S(1)}, u32[]{:S(2)}, u32[]{:S(2)}) collective-permute-start(bf16[2,2,128]{2,1,0:T(2,128)(2,1)S(1)} %get-tuple-element.44), channel_id=1, source_target_pairs={{0,1},{1,2},{2,3},{3,4},{4,5},{5,6},{6,7},{7,8},{8,9},{9,10},{10,1... | collective-permute-start | bytes 3080 | tf_op jit(solution)/shard_map/ppermute | solution.py:20
  4.5 4.3 %collective-permute-start.1 = (bf16[2,2,128]{2,1,0:T(2,128)(2,1)S(1)}, bf16[2,2,128]{2,1,0:T(2,128)(2,1)S(1)}, u32[]{:S(2)}, u32[]{:S(2)}) collective-permute-start(bf16[2,2,128]{2,1,0:T(2,128)(2,1)S(1)} %get-tuple-element.45), channel_id=1, source_target_pairs={{1,0},{2,1},{3,2},{4,3},{5,4},{6,5},{7,6},{8,7},{9,8},{10,9},{11,1... | collective-permute-start | bytes 3080 | tf_op jit(solution)/shard_map/ppermute | solution.py:21
  9.7 18.8 %collective-permute-start.2 = (bf16[2,132,128]{2,1,0:T(8,128)(2,1)S(1)}, bf16[2,132,128]{2,1,0:T(8,128)(2,1)S(1)}, u32[]{:S(2)}, u32[]{:S(2)}) collective-permute-start(bf16[2,132,128]{2,1,0:T(8,128)(2,1)S(1)} %pad_maximum_fusion.2), channel_id=1, source_target_pairs={{16,0},{32,16},{48,32},{64,48},{80,64},{96,80},{112,96},{128,112},... | collective-permute-start | bytes 202760 | tf_op jit(solution)/shard_map/ppermute | solution.py:29
  27.8 0.9 %copy-start.1 = (f32[16]{0:T(128)S(1)}, f32[16]{0:T(128)}, u32[]{:S(2)}) copy-start(f32[16]{0:T(128)} %param.10) | copy-start | bytes 196

commit v5 on v4

--- a/solution.py
+++ b/solution.py
@@ -81,27 +81,23 @@
     patches = features.reshape(sec_count, channels, rows_per, patch_len, patch_len)
     patches = patches.transpose(0, 2, 1, 3, 4).reshape(-1, patch_len, patch_len)
     flat_rows = patches.reshape(-1, patch_len)
-    half_cos = (
-        jnp.dot(flat_rows, cosine, preferred_element_type=jnp.float32)
-        .astype(jnp.bfloat16)
-        .reshape(patches.shape)
-    )
-    half_sin = (
-        jnp.dot(flat_rows, sin_table, preferred_element_type=jnp.float32)
-        .astype(jnp.bfloat16)
-        .reshape(patches.shape)
-    )
-    spec_real = jnp.einsum(
-        "uy,byk->buk", cosine, half_cos, preferred_element_type=jnp.float32
-    ) - jnp.einsum("uy,byk->buk", sin_table, half_sin, preferred_element_type=jnp.float32)
-    spec_imag = -(
-        jnp.einsum("uy,byk->buk", sin_table, half_cos, preferred_element_type=jnp.float32)
-        + jnp.einsum("uy,byk->buk", cosine, half_sin, preferred_element_type=jnp.float32)
-    )
+    half_both = jnp.dot(
+        flat_rows, jnp.concatenate([cosine, sin_table], axis=1), preferred_element_type=jnp.float32
+    ).astype(jnp.bfloat16)
+    half_cos = half_both[:, :patch_len].reshape(patches.shape)
+    half_sin = half_both[:, patch_len:].reshape(patches.shape)
+    left_cos = jnp.concatenate([cosine, -sin_table], axis=0)
+    left_sin = jnp.concatenate([-sin_table, -cosine], axis=0)
+    spec_both = jnp.einsum(
+        "uy,byk->buk", left_cos, half_cos, preferred_element_type=jnp.float32
+    ) + jnp.einsum("uy,byk->buk", left_sin, half_sin, preferred_element_type=jnp.float32)
+    spec_both = spec_both.astype(jnp.bfloat16)
+    spec_real = spec_both[:, :patch_len]
+    spec_imag = spec_both[:, patch_len:]
     out_shape = (sec_count, rows_per, channels, patch_len, patch_len)
     return (
-        spec_real.astype(jnp.bfloat16).reshape(out_shape),
-        spec_imag.astype(jnp.bfloat16).reshape(out_shape),
+        spec_real.reshape(out_shape),
+        spec_imag.reshape(out_shape),
     )
 
 
@@ -121,14 +117,20 @@
     cross_imag = jnp.where(drop, jnp.zeros_like(cross_imag), cross_imag)
     flat_real = cross_real.reshape(-1, patch_len)
     flat_imag = cross_imag.reshape(-1, patch_len)
-    back_real = (
-        jnp.dot(flat_real, cosine, preferred_element_type=jnp.float32)
-        - jnp.dot(flat_imag, sin_table, preferred_element_type=jnp.float32)
+    back_both = (
+        jnp.dot(
+            flat_real,
+            jnp.concatenate([cosine, sin_table], axis=1),
+            preferred_element_type=jnp.float32,
+        )
+        + jnp.dot(
+            flat_imag,
+            jnp.concatenate([-sin_table, cosine], axis=1),
+            preferred_element_type=jnp.float32,
+        )
     ).astype(jnp.bfloat16)
-    back_imag = (
-        jnp.dot(flat_real, sin_table, preferred_element_type=jnp.float32)
-        + jnp.dot(flat_imag, cosine, preferred_element_type=jnp.float32)
-    ).astype(jnp.bfloat16)
+    back_real = back_both[:, :patch_len]
+    back_imag = back_both[:, patch_len:]
     back_real = back_real.reshape(-1, patch_len, patch_len)
     back_imag = back_imag.reshape(-1, patch_len, patch_len)
     raw_corr = jnp.einsum(

time: 66.6 us -> 63.4 us (0.952)
  the two profiles are of different devices: /device:TPU:57 before, /device:TPU:512 now
where the time goes in v5:
time: 63.4 us; the launch traced here: 63 us
  blocking collectives  18.2 us (29%)
  other arithmetic  15.7 us (25%)
  matrix products  15.3 us (24%)
  starting transfers between devices  7.21 us (11%)
  local copies, waits for them, and re-layouts  4.82 us (8%)
  between operations  0.99 us (2%)
  waiting for transfers between devices  0.78 us (1%)
    all_to_all x1, blocking collectives, tile_sum(): return jnp.sum(lax.all_to_all(copies, axis, 0, 0, tiled=False), axis=0)  18.2 us
    dot_general x18, matrix products, conv_layers(): jnp.einsum('schw,co->sohw', window, conv2_w[3 * tap_row + tap_col], prefe...  9.71 us
    convert_element_type x2, other arithmetic, conv_layers(): jnp.where(inside[None, None, :, None], jax.nn.relu(layer_one), 0.0)  8.23 us
    ppermute x1, starting transfers between devices, with_halo(): before = lax.ppermute(last, axis, up)  3.38 us
    ppermute x1, starting transfers between devices, from_behind(): return lax.ppermute(block, axis, route)  2.53 us
    dot_general x2, matrix products, patch_spectra(): jnp.einsum('uy,byk->buk', left_sin, half_sin, preferred_element_type=jnp....  1.49 us
    dot_general x2, matrix products, patch_spectra(): jnp.einsum('uy,byk->buk', left_cos, half_cos, preferred_element_type=jnp....  1.49 us
    dot_general x2, matrix products, patch_spectra(): jnp.dot(flat_rows, jnp.concatenate([cosine, sin_table], axis=1), preferre...  1.36 us
  transfers between devices with their start and end apart: 3, of which 1 were waited for; matrix products, arithmetic and copies ran while one was open for 27% of the time, Pallas kernels for 0%

profile of v5, /device:TPU:512, one launch (start us, length us, event | category | flops | bytes accessed | tf_op | source)
XLA Modules:
  0.0 63.0 jit_solution(16450555333532983575)
XLA Ops:
  0.6 0.7 %fusion.140 = (bf16[2,2,128]{2,1,0:T(2,128)(2,1)S(1)}, bf16[2,2,128]{2,1,0:T(2,128)(2,1)S(1)}) fusion(bf16[2,128,128]{2,1,0:T(8,128)(2,1)} %param.6), kind=kLoop, calls=%fused_computation.234 | loop fusion | bytes 4096 | tf_op jit(solution)/shard_map/slice | solution.py:18
  1.4 3.4 %collective-permute-start = (bf16[2,2,128]{2,1,0:T(2,128)(2,1)S(1)}, bf16[2,2,128]{2,1,0:T(2,128)(2,1)S(1)}, u32[]{:S(2)}, u32[]{:S(2)}) collective-permute-start(bf16[2,2,128]{2,1,0:T(2,128)(2,1)S(1)} %get-tuple-element.54), channel_id=1, source_target_pairs={{0,1},{1,2},{2,3},{3,4},{4,5},{5,6},{6,7},{7,8},{8,9},{9,10},{10,1... | collective-permute-start | bytes 3080 | tf_op jit(solution)/shard_map/ppermute | solution.py:20
  4.7 1.3 %collective-permute-start.1 = (bf16[2,2,128]{2,1,0:T(2,128)(2,1)S(1)}, bf16[2,2,128]{2,1,0:T(2,128)(2,1)S(1)}, u32[]{:S(2)}, u32[]{:S(2)}) collective-permute-start(bf16[2,2,128]{2,1,0:T(2,128)(2,1)S(1)} %get-tuple-element.55), channel_id=1, source_target_pairs={{1,0},{2,1},{3,2},{4,3},{5,4},{6,5},{7,6},{8,7},{9,8},{10,9},{11,1... | collective-permute-start | bytes 3080 | tf_op jit(solution)/shard_map/ppermute | solution.py:21
  6.0 0.3 sine_convert_fusion
  6.3 0.3 fusion.64
  6.6 1.0 %bitcast_convert_fusion.8 = (f32[16]{0:T(128)S(1)}, f32[16]{0:T(128)S(1)}, f32[16]{0:T(128)S(1)}, f32[16]{0:T(128)S(1)}, f32[16]{0:T(128)S(1)}, /*index=5*/f32[1...) fusion(bf16[9,16]{1,0:T(8,128)(2,1)} %param.9), kind=kLoop, calls=%fused_computation.188 | loop fusion | flops 144 | bytes 864 | tf_op jit(solution)/shard_map/convert_element_type | solution.py:57
  7.6 0.7 %compare_not_fusion = (pred[2]{0:T(512)(128)(4,1)S(1)}, pred[2]{0:T(512)(128)(4,1)S(1)}) fusion(s32[2]{0:T(128)} %param.7, s32[]{:T(128)S(6)} %mul.465), kind=kLoop, calls=%fused_computation.167 | loop fusion | flops 10 | bytes 16 | tf_op jit(solution)/shard_map/not | solution.py:115
  8.5 0.7 %broadcast_multiply_fusion = (f32[2,1]{0,1:T(1,128)S(1)}, f32[2,1]{0,1:T(1,128)S(1)}, f32[2,1]{0,1:T(1,128)S(1)}) fusion(f32[]{:T(128)S(6)} %sub.56, s32[2]{0:T(128)} %param.7, s32[]{:T(128)S(6)} %mul.465, s32[2,1]{0,1:T(1,128)} %param.8), kind=kLoop, calls=%fused_computation.198 | loop fusion | flops 16 | bytes 48 | tf_op jit(solution)/shard_map/mul | solution.py:197
  9.2 0.1 copy.170
  9.3 0.1 copy.171
  9.3 0.1 copy.172
  9.4 0.8 %collective-permute-done.1 = bf16[2,2,128]{2,1,0:T(2,128)(2,1)S(1)} collective-permute-done((bf16[2,2,128]{2,1,0:T(2,128)(2,1)S(1)}, bf16[2,2,128]{2,1,0:T(2,128)(2,1)S(1)}, u32[]{:S(2)}, u32[]{:S(2)}) %collective-permute-start.1) | collective-permute-done | bytes 1056 | tf_op jit(solution)/shard_map/ppermute | solution.py:21
  10.2 0.9 %pad_maximum_fusion.2 = bf16[2,132,128]{2,1,0:T(8,128)(2,1)S(1)} fusion(bf16[2,2,128]{2,1,0:T(2,128)(2,1)S(1)} %collective-permute-done.1, bf16[2,128,128]{2,1,0:T(8,128)(2,1)} %param.6, bf16[2,2,128]{2,1,0:T(2,128)(2,1)S(1)} %collective-permute-done), kind=kLoop, calls=%fused_computation.101 | loop fusion | flops 202752 | bytes 135168 | tf_op jit(solution)/shard_map/concatenate | solution.py:22
  11.1 2.5 %collective-permute-start.2 = (bf16[2,132,128]{2,1,0:T(8,128)(2,1)S(1)}, bf16[2,132,128]{2,1,0:T(8,128)(2,1)S(1)}, u32[]{:S(2)}, u32[]{:S(2)}) collective-permute-start(bf16[2,132,128]{2,1,0:T(8,128)(2,1)S(1)} %pad_maximum_fusion.2), channel_id=1, source_target_pairs={{16,0},{32,16},{48,32},{64,48},{80,64},{96,80},{112,96},{128,112},... | collective-permute-start | bytes 202760 | tf_op jit(solution)/shard_map/ppermute | solution.py:29
  13.6 1.1 %fusion.38 = (f32[2,130,128]{2,1,0:T(8,128)S(1)}, f32[2,130,128]{2,1,0:T(8,128)S(1)}, f32[2,130,128]{2,1,0:T(8,128)S(1)}, f32[2,130,128]{2,1,0:T(8,128)S(1)}, f3...) fusion(bf16[2,132,128]{2,1,0:T(8,128)(2,1)S(1)} %pad_maximum_fu, ...), kind=kLoop, calls=%fused_computation.85 | loop fusion | flops 499200 | bytes 1404928 | tf_op jit(solution)/shard_map/convert_element_type | solution.py:58
  14.7 4.4 %select_convert_fusion.1 = bf16[2,16,130,128]{3,1,2,0:T(8,128)(2,1)S(1)} fusion(f32[2,130,128]{2,1,0:T(8,128)S(1)} %get-tuple-element.50, f32[16]{0:T(128)S(1)} %get-tuple-element.65, f32[2,130,128]{2,1,0:T(8,128)S(1)} %get-tuple-element.82, f32[16]{0:T(128)S(1)} %get-tuple-element.66, f32[2,130,128]{2,1,0:T(8,128)S(1)} %get-tuple-element.49, ...), kind=kLoop, calls=%fused_computation.21 | loop fusion | flops 11182080 | bytes 2263810 | tf_op jit(solution)/shard_map/convert_element_type | solution.py:62
  19.2 0.5 fusion.10
  19.6 0.5 fusion.11
  20.1 0.5 fusion.12
  20.6 0.5 fusion.13
  21.1 0.5 fusion.14
  21.6 0.4 fusion.28
  22.0 0.5 fusion.30
  22.5 0.5 fusion.32
  22.9 1.1 %fusion.6 = bf16[2,16,128,128]{3,1,2,0:T(8,128)(2,1)S(1)} fusion(f32[2,128,128,16]{2,3,1,0:T(8,128)S(1)} %fusion.28, f32[2,128,128,16]{2,3,1,0:T(8,128)S(1)} %fusion.14, f32[2,128,128,16]{2,3,1,0:T(8,128)S(1)} %fusion.13, f32[2,128,128,16]{2,3,1,0:T(8,128)S(1)} %fusion.30, f32[2,128,128,16]{2,3,1,0:T(8,128)S(1)} %fusion.12, ...), kind=kOutput, calls=%fused_computation.30 | convolution fusion | flops 21495808 | bytes 18894848 | tf_op jit(solution)/shard_map/schw,co->sohw/dot_general | solution.py:70
  24.0 0.3 copy.160
  24.3 0.7 %convolution_convert_fusion.1 = bf16[4096,256]{1,0:T(8,128)(2,1)S(1)} fusion(bf16[4096,128]{1,0:T(8,128)(2,1)S(1)} %bitcast.222, bf16[128,128]{1,0:T(8,128)(2,1)S(1)} %get-tuple-element.84, bf16[128,128]{1,0:T(8,128)(2,1)S(1)} %get-tuple-element.85), kind=kOutput, calls=%fused_computation.1 | convolution fusion | flops 269615104 | bytes 3211264 | tf_op jit(solution)/shard_map/dot_general | solution.py:84
  25.0 0.1 fusion.138
  25.2 0.7 %fusion.60 = f32[32,128,256]{2,1,0:T(8,128)S(1)} fusion(bf16[32,128,128]{2,1,0:T(8,128)(2,1)S(1)} %bitcast.230, bf16[128,128]{1,0:T(8,128)(2,1)S(1)} %get-tuple-element.87, bf16[128,128]{1,0:T(8,128)(2,1)S(1)} %get-tuple-element.85), kind=kOutput, calls=%fused_computation.119 | convolution fusion | flops 268566528 | bytes 5308416 | tf_op jit(solution)/shard_map/uy,byk->buk/dot_general | solution.py:91
  25.9 0.7 %fusion.4 = bf16[32,256,128]{1,2,0:T(8,128)(2,1)S(1)} fusion(f32[32,128,256]{2,1,0:T(8,128)S(1)} %fusion.60, bf16[32,128,128]{2,1,0:T(8,128)(2,1)S(1)} %bitcast.228, bf16[128,128]{1,0:T(8,128)(2,1)S(1)} %get-tuple-element.86, bf16[128,128]{1,0:T(8,128)(2,1)S(1)} %get-tuple-element.87), kind=kOutput, calls=%fused_computation.28 | convolution fusion | flops 270663680 | bytes 7405568 | tf_op jit(solution)/shard_map/uy,byk->buk/dot_general | solution.py:93
  26.7 0.6 fusion.137
  27.3 0.2 fusion.44
  27.5 3.8 %select_convert_fusion = bf16[2,16,130,128]{3,1,2,0:T(8,128)(2,1)S(1)} fusion(f32[2,130,128]{2,1,0:T(8,128)S(1)} %get-tuple-element.41, f32[2,130,128]{2,1,0:T(8,128)S(1)} %get-tuple-element.42, f32[2,130,128]{2,1,0:T(8,128)S(1)} %get-tuple-element.40, f32[2,130,128]{2,1,0:T(8,128)S(1)} %get-tuple-element.39, f32[2,130,128]{2,1,0:T(8,128)S(1)} %get-tuple-element.43, ...), kind=kLoop, calls=%fused_computation.20 | loop fusion | flops 11182080 | bytes 2263810 | tf_op jit(solution)/shard_map/convert_element_type | solution.py:62
  31.3 0.5 fusion.15
  31.8 0.5 fusion.16
  32.3 0.5 fusion.17
  32.8 0.5 fusion.18
  33.2 0.5 fusion.19
  33.7 0.5 fusion.22
  34.2 0.4 fusion.24
  34.7 0.5 fusion.26
  35.1 1.1 %fusion.7 = bf16[2,16,128,128]{3,1,2,0:T(8,128)(2,1)S(1)} fusion(f32[2,128,128,16]{2,3,1,0:T(8,128)S(1)} %fusion.22, f32[2,128,128,16]{2,3,1,0:T(8,128)S(1)} %fusion.19, f32[2,128,128,16]{2,3,1,0:T(8,128)S(1)} %fusion.18, f32[2,128,128,16]{2,3,1,0:T(8,128)S(1)} %fusion.24, f32[2,128,128,16]{2,3,1,0:T(8,128)S(1)} %fusion.17, ...), kind=kOutput, calls=%fused_computation.31 | convolution fusion | flops 21495808 | bytes 18894848 | tf_op jit(solution)/shard_map/schw,co->sohw/dot_general | solution.py:70
  36.2 0.3 copy.163
  36.5 0.7 %convolution_convert_fusion = bf16[4096,256]{1,0:T(8,128)(2,1)S(1)} fusion(bf16[4096,128]{1,0:T(8,128)(2,1)S(1)} %bitcast.223, bf16[128,128]{1,0:T(8,128)(2,1)S(1)} %get-tuple-element.84, bf16[128,128]{1,0:T(8,128)(2,1)S(1)} %get-tuple-element.85), kind=kOutput, calls=%fused_computation | convolution fusion | flops 269615104 | bytes 3211264 | tf_op jit(solution)/shard_map/dot_general | solution.py:84
  37.2 0.1 fusion.136
  37.3 0.7 %fusion.59 = f32[32,128,256]{2,1,0:T(8,128)S(1)} fusion(bf16[32,128,128]{2,1,0:T(8,128)(2,1)S(1)} %bitcast.231, bf16[128,128]{1,0:T(8,128)(2,1)S(1)} %get-tuple-element.87, bf16[128,128]{1,0:T(8,128)(2,1)S(1)} %get-tuple-element.85), kind=kOutput, calls=%fused_computation.118 | convolution fusion | flops 268566528 | bytes 5308416 | tf_op jit(solution)/shard_map/uy,byk->buk/dot_general | solution.py:91
  38.1 0.7 %fusion.5 = bf16[32,256,128]{1,2,0:T(8,128)(2,1)S(1)} fusion(f32[32,128,256]{2,1,0:T(8,128)S(1)} %fusion.59, bf16[32,128,128]{2,1,0:T(8,128)(2,1)S(1)} %bitcast.229, bf16[128,128]{1,0:T(8,128)(2,1)S(1)} %get-tuple-element.86, bf16[128,128]{1,0:T(8,128)(2,1)S(1)} %get-tuple-element.87), kind=kOutput, calls=%fused_computation.29 | convolution fusion | flops 270663680 | bytes 7405568 | tf_op jit(solution)/shard_map/uy,byk->buk/dot_general | solution.py:93
  38.8 0.6 fusion.135
  39.4 1.1 %fusion.3 = (bf16[2,128,128]{1,2,0:T(8,128)(2,1)S(1)}, bf16[2,128,128]{1,2,0:T(8,128)(2,1)S(1)}) fusion(bf16[2,1,16,128,128]{3,4,2,0,1:T(8,128)(2,1)S(1)} %bitcast.225, bf16[2,1,16,128,128]{3,4,2,0,1:T(8,128)(2,1)S(1)} %bitcast.224, bf16[2,1,16,128,128]{3,4,2,0,1:T(8,128)(2,1)S(1)} %bitcast.227, bf16[2,1,16,128,128]{3,4,2,0,1:T(8,128)(2,1)S(1)} %bitcast.226, ...), kind=kLoop, calls=%fused_computation.25 | loop fusion | flops 11468800 | bytes 4325378 | tf_op jit(solution)/shard_map/reduce_sum | solution.py:114
  40.5 0.1 copy.166
  40.6 0.1 copy.167
  40.7 0.1 fusion.34
  40.9 0.2 fusion.66
  41.0 0.2 fusion.8
  41.2 0.4 fusion.62
  41.6 0.5 fusion.142
  42.1 0.2 fusion.36
  42.3 0.2 multiply_reduce_fusion.1
  42.6 0.1 copy.173
  42.7 0.1 concatenate.47
  42.8 18.2 %all_to_all.5 = f32[16,2,7]{2,1,0:T(2,128)S(1)} all-to-all(f32[16,2,7]{2,1,0:T(2,128)S(1)} %broadcast_in_dim.39), channel_id=1, replica_groups=mesh['sec'=48,'tile'=16] {'tile'}, dimensions={0} | all-to-all | bytes 1792 | tf_op jit(solution)/shard_map/all_to_all | solution.py:35
  61.4 0.1 copy.209
  61.7 0.6 subtract_multiply_fusion
  62.3 0.7 %copy.177 = f32[2,4]{1,0:T(2,128)} copy(f32[2,4]{0,1:T(4,128)S(1)} %pad_maximum_fusion.7) | data formatting | bytes 64
  (28 shorter events, 0.9 us)
Async XLA Ops:
  0.6 18.5 %copy-start = (bf16[9,16,16]{2,1,0:T(8,128)(2,1)S(1)}, bf16[9,16,16]{2,1,0:T(8,128)(2,1)}, u32[]{:S(2)}) copy-start(bf16[9,16,16]{2,1,0:T(8,128)(2,1)} %param.11) | copy-start | bytes 13828
  1.4 8.1 %collective-permute-start = (bf16[2,2,128]{2,1,0:T(2,128)(2,1)S(1)}, bf16[2,2,128]{2,1,0:T(2,128)(2,1)S(1)}, u32[]{:S(2)}, u32[]{:S(2)}) collective-permute-start(bf16[2,2,128]{2,1,0:T(2,128)(2,1)S(1)} %get-tuple-element.54), channel_id=1, source_target_pairs={{0,1},{1,2},{2,3},{3,4},{4,5},{5,6},{6,7},{7,8},{8,9},{9,10},{10,1... | collective-permute-start | bytes 3080 | tf_op jit(solution)/shard_map/ppermute | solution.py:20
  4.7 5.5 %collective-permute-start.1 = (bf16[2,2,128]{2,1,0:T(2,128)(2,1)S(1)}, bf16[2,2,128]{2,1,0:T(2,128)(2,1)S(1)}, u32[]{:S(2)}, u32[]{:S(2)}) collective-permute-start(bf16[2,2,128]{2,1,0:T(2,128)(2,1)S(1)} %get-tuple-element.55), channel_id=1, source_target_pairs={{1,0},{2,1},{3,2},{4,3},{5,4},{6,5},{7,6},{8,7},{9,8},{10,9},{11,1... | collective-permute-start | bytes 3080 | tf_op jit(solution)/shard_map/ppermute | solution.py:21
  11.1 16.2 %collective-permute-start.2 = (bf16[2,132,128]{2,1,0:T(8,128)(2,1)S(1)}, bf16[2,132,128]{2,1,0:T(8,128)(2,1)S(1)}, u32[]{:S(2)}, u32[]{:S(2)}) collective-permute-start(bf16[2,132,128]{2,1,0:T(8,128)(2,1)S(1)} %pad_maximum_fusion.2), channel_id=1, source_target_pairs={{16,0},{32,16},{48,32},{64,48},{80,64},{96,80},{112,96},{128,112},... | collective-permute-start | bytes 202760 | tf_op jit(solution)/shard_map/ppermute | solution.py:29
  26.7 0.8 %copy-start.1 = (f32[16]{0:T(128)S(1)}, f32[16]{0:T(128)}, u32[]{:S(2)}) copy-start(f32[16]{0:T(128)} %param.10) | copy-start | bytes 196

commit v6 on v5

--- a/solution.py
+++ b/solution.py
@@ -161,10 +161,11 @@
     tile_pos = lax.axis_index("tile")
     cosine, sin_table = dft_tables(patch_len)
     padded_rows = with_halo(sections, (("tile", 1),), 2)
-    next_rows = from_behind(padded_rows, "sec", -1)
     row_global = tile_pos * strip_rows - 1 + jnp.arange(strip_rows + 2, dtype=jnp.int32)
     inside = (row_global >= 0) & (row_global < strip_rows * tile_count)
     own_feats = conv_layers(padded_rows, inside, conv1_w, conv1_b, conv2_w)
+    own_feats, rows_out = lax.optimization_barrier((own_feats, padded_rows))
+    next_rows = from_behind(rows_out, "sec", -1)
     own_real, own_imag = patch_spectra(own_feats, cosine, sin_table, rows_per)
     next_feats = conv_layers(next_rows, inside, conv1_w, conv1_b, conv2_w)
     next_real, next_imag = patch_spectra(next_feats, cosine, sin_table, rows_per)

time: 63.4 us -> 68.5 us (1.080)
  the two profiles are of different devices: /device:TPU:512 before, /device:TPU:57 now
where the time goes in v6:
time: 68.5 us; the launch traced here: 68.1 us
  blocking collectives  16.8 us (25%)
  other arithmetic  15.7 us (23%)
  matrix products  15.3 us (22%)
  starting transfers between devices  8.04 us (12%)
  waiting for transfers between devices  6.56 us (10%)
  local copies, waits for them, and re-layouts  4.82 us (7%)
  between operations  0.98 us (1%)
    all_to_all x1, blocking collectives, tile_sum(): return jnp.sum(lax.all_to_all(copies, axis, 0, 0, tiled=False), axis=0)  16.8 us
    dot_general x18, matrix products, conv_layers(): jnp.einsum('schw,co->sohw', window, conv2_w[3 * tap_row + tap_col], prefe...  9.71 us
    convert_element_type x2, other arithmetic, conv_layers(): jnp.where(inside[None, None, :, None], jax.nn.relu(layer_one), 0.0)  8.23 us
    ppermute x1, waiting for transfers between devices, from_behind(): return lax.ppermute(block, axis, route)  6.56 us
    ppermute x1, starting transfers between devices, from_behind(): return lax.ppermute(block, axis, route)  3.64 us
    ppermute x1, starting transfers between devices, with_halo(): before = lax.ppermute(last, axis, up)  3.1 us
    dot_general x2, matrix products, patch_spectra(): jnp.einsum('uy,byk->buk', left_sin, half_sin, preferred_element_type=jnp....  1.5 us
    dot_general x2, matrix products, patch_spectra(): jnp.einsum('uy,byk->buk', left_cos, half_cos, preferred_element_type=jnp....  1.49 us
  transfers between devices with their start and end apart: 3, of which 1 were waited for; matrix products, arithmetic and copies ran while one was open for 10% of the time, Pallas kernels for 0%

profile of v6, /device:TPU:57, one launch (start us, length us, event | category | flops | bytes accessed | tf_op | source)
XLA Modules:
  0.0 68.1 jit_solution(1513860348212705915)
XLA Ops:
  0.6 0.7 %fusion.140 = (bf16[2,2,128]{2,1,0:T(2,128)(2,1)S(1)}, bf16[2,2,128]{2,1,0:T(2,128)(2,1)S(1)}) fusion(bf16[2,128,128]{2,1,0:T(8,128)(2,1)} %param.6), kind=kLoop, calls=%fused_computation.234 | loop fusion | bytes 4096 | tf_op jit(solution)/shard_map/slice | solution.py:18
  1.4 3.1 %collective-permute-start = (bf16[2,2,128]{2,1,0:T(2,128)(2,1)S(1)}, bf16[2,2,128]{2,1,0:T(2,128)(2,1)S(1)}, u32[]{:S(2)}, u32[]{:S(2)}) collective-permute-start(bf16[2,2,128]{2,1,0:T(2,128)(2,1)S(1)} %get-tuple-element.58), channel_id=1, source_target_pairs={{0,1},{1,2},{2,3},{3,4},{4,5},{5,6},{6,7},{7,8},{8,9},{9,10},{10,1... | collective-permute-start | bytes 3080 | tf_op jit(solution)/shard_map/ppermute | solution.py:20
  4.5 1.3 %collective-permute-start.1 = (bf16[2,2,128]{2,1,0:T(2,128)(2,1)S(1)}, bf16[2,2,128]{2,1,0:T(2,128)(2,1)S(1)}, u32[]{:S(2)}, u32[]{:S(2)}) collective-permute-start(bf16[2,2,128]{2,1,0:T(2,128)(2,1)S(1)} %get-tuple-element.59), channel_id=1, source_target_pairs={{1,0},{2,1},{3,2},{4,3},{5,4},{6,5},{7,6},{8,7},{9,8},{10,9},{11,1... | collective-permute-start | bytes 3080 | tf_op jit(solution)/shard_map/ppermute | solution.py:21
  5.8 0.3 sine_convert_fusion
  6.1 0.3 fusion.64
  6.4 1.0 %bitcast_convert_fusion.8 = (f32[16]{0:T(128)S(1)}, f32[16]{0:T(128)S(1)}, f32[16]{0:T(128)S(1)}, f32[16]{0:T(128)S(1)}, f32[16]{0:T(128)S(1)}, /*index=5*/f32[1...) fusion(bf16[9,16]{1,0:T(8,128)(2,1)} %param.9), kind=kLoop, calls=%fused_computation.188 | loop fusion | flops 144 | bytes 864 | tf_op jit(solution)/shard_map/convert_element_type | solution.py:57
  7.4 0.7 compare_not_fusion
  8.2 0.7 %broadcast_multiply_fusion = (f32[2,1]{0,1:T(1,128)S(1)}, f32[2,1]{0,1:T(1,128)S(1)}, f32[2,1]{0,1:T(1,128)S(1)}) fusion(f32[]{:T(128)S(6)} %sub.56, s32[2]{0:T(128)} %param.7, s32[]{:T(128)S(6)} %mul.465, s32[2,1]{0,1:T(1,128)} %param.8), kind=kLoop, calls=%fused_computation.198 | loop fusion | flops 16 | bytes 48 | tf_op jit(solution)/shard_map/mul | solution.py:198
  8.9 0.1 copy.170
  9.0 0.1 copy.171
  9.1 0.1 copy.172
  9.2 0.9 %pad_maximum_fusion.2 = bf16[2,132,128]{2,1,0:T(8,128)(2,1)S(1)} fusion(bf16[2,2,128]{2,1,0:T(2,128)(2,1)S(1)} %collective-permute-done.1, bf16[2,128,128]{2,1,0:T(8,128)(2,1)} %param.6, bf16[2,2,128]{2,1,0:T(2,128)(2,1)S(1)} %collective-permute-done), kind=kLoop, calls=%fused_computation.101 | loop fusion | flops 202752 | bytes 135168 | tf_op jit(solution)/shard_map/concatenate | solution.py:22
  10.0 1.1 %fusion.38 = (f32[2,130,128]{2,1,0:T(8,128)S(1)}, f32[2,130,128]{2,1,0:T(8,128)S(1)}, f32[2,130,128]{2,1,0:T(8,128)S(1)}, f32[2,130,128]{2,1,0:T(8,128)S(1)}, f3...) fusion(bf16[2,132,128]{2,1,0:T(8,128)(2,1)S(1)} %pad_maximum_fu, ...), kind=kLoop, calls=%fused_computation.85 | loop fusion | flops 499200 | bytes 1404928 | tf_op jit(solution)/shard_map/convert_element_type | solution.py:58
  11.1 4.4 %select_convert_fusion.1 = bf16[2,16,130,128]{3,1,2,0:T(8,128)(2,1)S(1)} fusion(f32[2,130,128]{2,1,0:T(8,128)S(1)} %get-tuple-element.54, f32[16]{0:T(128)S(1)} %get-tuple-element.69, f32[2,130,128]{2,1,0:T(8,128)S(1)} %get-tuple-element.86, f32[16]{0:T(128)S(1)} %get-tuple-element.70, f32[2,130,128]{2,1,0:T(8,128)S(1)} %get-tuple-element.53, ...), kind=kLoop, calls=%fused_computation.21 | loop fusion | flops 11182080 | bytes 2263810 | tf_op jit(solution)/shard_map/convert_element_type | solution.py:62
  15.6 0.5 fusion.10
  16.0 0.5 fusion.11
  16.5 0.5 fusion.12
  17.0 0.5 fusion.13
  17.5 0.5 fusion.14
  18.0 0.4 fusion.28
  18.4 0.5 fusion.30
  18.9 0.5 fusion.32
  19.4 1.1 %fusion.6 = bf16[2,16,128,128]{3,1,2,0:T(8,128)(2,1)S(1)} fusion(f32[2,128,128,16]{2,3,1,0:T(8,128)S(1)} %fusion.28, f32[2,128,128,16]{2,3,1,0:T(8,128)S(1)} %fusion.14, f32[2,128,128,16]{2,3,1,0:T(8,128)S(1)} %fusion.13, f32[2,128,128,16]{2,3,1,0:T(8,128)S(1)} %fusion.30, f32[2,128,128,16]{2,3,1,0:T(8,128)S(1)} %fusion.12, ...), kind=kOutput, calls=%fused_computation.30 | convolution fusion | flops 21495808 | bytes 18894848 | tf_op jit(solution)/shard_map/schw,co->sohw/dot_general | solution.py:70
  20.5 3.6 %collective-permute-start.2 = (bf16[2,132,128]{2,1,0:T(8,128)(2,1)S(1)}, bf16[2,132,128]{2,1,0:T(8,128)(2,1)S(1)}, u32[]{:S(2)}, u32[]{:S(2)}) collective-permute-start(bf16[2,132,128]{2,1,0:T(8,128)(2,1)S(1)} %pad_maximum_fusion.2), channel_id=1, source_target_pairs={{16,0},{32,16},{48,32},{64,48},{80,64},{96,80},{112,96},{128,112},... | collective-permute-start | bytes 202760 | tf_op jit(solution)/shard_map/ppermute | solution.py:29
  24.1 0.3 copy.160
  24.4 0.7 %convolution_convert_fusion.1 = bf16[4096,256]{1,0:T(8,128)(2,1)S(1)} fusion(bf16[4096,128]{1,0:T(8,128)(2,1)S(1)} %bitcast.222, bf16[128,128]{1,0:T(8,128)(2,1)S(1)} %get-tuple-element.88, bf16[128,128]{1,0:T(8,128)(2,1)S(1)} %get-tuple-element.89), kind=kOutput, calls=%fused_computation.1 | convolution fusion | flops 269615104 | bytes 3211264 | tf_op jit(solution)/shard_map/dot_general | solution.py:84
  25.1 0.1 fusion.138
  25.2 0.7 %fusion.60 = f32[32,128,256]{2,1,0:T(8,128)S(1)} fusion(bf16[32,128,128]{2,1,0:T(8,128)(2,1)S(1)} %bitcast.230, bf16[128,128]{1,0:T(8,128)(2,1)S(1)} %get-tuple-element.91, bf16[128,128]{1,0:T(8,128)(2,1)S(1)} %get-tuple-element.89), kind=kOutput, calls=%fused_computation.119 | convolution fusion | flops 268566528 | bytes 5308416 | tf_op jit(solution)/shard_map/uy,byk->buk/dot_general | solution.py:91
  26.0 0.7 %fusion.4 = bf16[32,256,128]{1,2,0:T(8,128)(2,1)S(1)} fusion(f32[32,128,256]{2,1,0:T(8,128)S(1)} %fusion.60, bf16[32,128,128]{2,1,0:T(8,128)(2,1)S(1)} %bitcast.228, bf16[128,128]{1,0:T(8,128)(2,1)S(1)} %get-tuple-element.90, bf16[128,128]{1,0:T(8,128)(2,1)S(1)} %get-tuple-element.91), kind=kOutput, calls=%fused_computation.28 | convolution fusion | flops 270663680 | bytes 7405568 | tf_op jit(solution)/shard_map/uy,byk->buk/dot_general | solution.py:93
  26.7 0.6 fusion.137
  27.3 6.6 %collective-permute-done.2 = bf16[2,132,128]{2,1,0:T(8,128)(2,1)S(1)} collective-permute-done((bf16[2,132,128]{2,1,0:T(8,128)(2,1)S(1)}, bf16[2,132,128]{2,1,0:T(8,128)(2,1)S(1)}, u32[]{:S(2)}, u32[]{:S(2)}) %collective-permute-start.2) | collective-permute-done | bytes 67616 | tf_op jit(solution)/shard_map/ppermute | solution.py:29
  33.9 0.2 fusion.44
  34.1 3.8 %select_convert_fusion = bf16[2,16,130,128]{3,1,2,0:T(8,128)(2,1)S(1)} fusion(f32[2,130,128]{2,1,0:T(8,128)S(1)} %get-tuple-element.45, f32[2,130,128]{2,1,0:T(8,128)S(1)} %get-tuple-element.46, f32[2,130,128]{2,1,0:T(8,128)S(1)} %get-tuple-element.44, f32[2,130,128]{2,1,0:T(8,128)S(1)} %get-tuple-element.43, f32[2,130,128]{2,1,0:T(8,128)S(1)} %get-tuple-element.47, ...), kind=kLoop, calls=%fused_computation.20 | loop fusion | flops 11182080 | bytes 2263810 | tf_op jit(solution)/shard_map/convert_element_type | solution.py:62
  37.9 0.5 fusion.15
  38.4 0.5 fusion.16
  38.9 0.5 fusion.17
  39.4 0.5 fusion.18
  39.9 0.5 fusion.19
  40.3 0.4 fusion.22
  40.8 0.5 fusion.24
  41.3 0.5 fusion.26
  41.7 1.1 %fusion.7 = bf16[2,16,128,128]{3,1,2,0:T(8,128)(2,1)S(1)} fusion(f32[2,128,128,16]{2,3,1,0:T(8,128)S(1)} %fusion.22, f32[2,128,128,16]{2,3,1,0:T(8,128)S(1)} %fusion.19, f32[2,128,128,16]{2,3,1,0:T(8,128)S(1)} %fusion.18, f32[2,128,128,16]{2,3,1,0:T(8,128)S(1)} %fusion.24, f32[2,128,128,16]{2,3,1,0:T(8,128)S(1)} %fusion.17, ...), kind=kOutput, calls=%fused_computation.31 | convolution fusion | flops 21495808 | bytes 18894848 | tf_op jit(solution)/shard_map/schw,co->sohw/dot_general | solution.py:70
  42.8 0.3 copy.163
  43.1 0.7 %convolution_convert_fusion = bf16[4096,256]{1,0:T(8,128)(2,1)S(1)} fusion(bf16[4096,128]{1,0:T(8,128)(2,1)S(1)} %bitcast.223, bf16[128,128]{1,0:T(8,128)(2,1)S(1)} %get-tuple-element.88, bf16[128,128]{1,0:T(8,128)(2,1)S(1)} %get-tuple-element.89), kind=kOutput, calls=%fused_computation | convolution fusion | flops 269615104 | bytes 3211264 | tf_op jit(solution)/shard_map/dot_general | solution.py:84
  43.8 0.1 fusion.136
  43.9 0.7 %fusion.59 = f32[32,128,256]{2,1,0:T(8,128)S(1)} fusion(bf16[32,128,128]{2,1,0:T(8,128)(2,1)S(1)} %bitcast.231, bf16[128,128]{1,0:T(8,128)(2,1)S(1)} %get-tuple-element.91, bf16[128,128]{1,0:T(8,128)(2,1)S(1)} %get-tuple-element.89), kind=kOutput, calls=%fused_computation.118 | convolution fusion | flops 268566528 | bytes 5308416 | tf_op jit(solution)/shard_map/uy,byk->buk/dot_general | solution.py:91
  44.7 0.7 %fusion.5 = bf16[32,256,128]{1,2,0:T(8,128)(2,1)S(1)} fusion(f32[32,128,256]{2,1,0:T(8,128)S(1)} %fusion.59, bf16[32,128,128]{2,1,0:T(8,128)(2,1)S(1)} %bitcast.229, bf16[128,128]{1,0:T(8,128)(2,1)S(1)} %get-tuple-element.90, bf16[128,128]{1,0:T(8,128)(2,1)S(1)} %get-tuple-element.91), kind=kOutput, calls=%fused_computation.29 | convolution fusion | flops 270663680 | bytes 7405568 | tf_op jit(solution)/shard_map/uy,byk->buk/dot_general | solution.py:93
  45.4 0.6 fusion.135
  46.0 1.1 %fusion.3 = (bf16[2,128,128]{1,2,0:T(8,128)(2,1)S(1)}, bf16[2,128,128]{1,2,0:T(8,128)(2,1)S(1)}) fusion(bf16[2,1,16,128,128]{3,4,2,0,1:T(8,128)(2,1)S(1)} %bitcast.225, bf16[2,1,16,128,128]{3,4,2,0,1:T(8,128)(2,1)S(1)} %bitcast.224, bf16[2,1,16,128,128]{3,4,2,0,1:T(8,128)(2,1)S(1)} %bitcast.227, bf16[2,1,16,128,128]{3,4,2,0,1:T(8,128)(2,1)S(1)} %bitcast.226, ...), kind=kLoop, calls=%fused_computation.25 | loop fusion | flops 11468800 | bytes 4325378 | tf_op jit(solution)/shard_map/reduce_sum | solution.py:114
  47.1 0.1 copy.166
  47.2 0.1 copy.167
  47.3 0.1 fusion.34
  47.5 0.2 fusion.66
  47.6 0.2 fusion.8
  47.8 0.4 fusion.62
  48.2 0.5 fusion.142
  48.7 0.2 fusion.36
  48.9 0.2 multiply_reduce_fusion.1
  49.2 0.1 copy.173
  49.3 0.1 concatenate.47
  49.4 16.8 %all_to_all.5 = f32[16,2,7]{2,1,0:T(2,128)S(1)} all-to-all(f32[16,2,7]{2,1,0:T(2,128)S(1)} %broadcast_in_dim.39), channel_id=1, replica_groups=mesh['sec'=48,'tile'=16] {'tile'}, dimensions={0} | all-to-all | bytes 1792 | tf_op jit(solution)/shard_map/all_to_all | solution.py:35
  66.8 0.1 copy.206
  66.9 0.6 subtract_multiply_fusion
  67.5 0.7 copy.177
  (28 shorter events, 0.9 us)
Async XLA Ops:
  0.6 14.9 %copy-start = (bf16[9,16,16]{2,1,0:T(8,128)(2,1)S(1)}, bf16[9,16,16]{2,1,0:T(8,128)(2,1)}, u32[]{:S(2)}) copy-start(bf16[9,16,16]{2,1,0:T(8,128)(2,1)} %param.11) | copy-start | bytes 13828
  1.4 7.8 %collective-permute-start = (bf16[2,2,128]{2,1,0:T(2,128)(2,1)S(1)}, bf16[2,2,128]{2,1,0:T(2,128)(2,1)S(1)}, u32[]{:S(2)}, u32[]{:S(2)}) collective-permute-start(bf16[2,2,128]{2,1,0:T(2,128)(2,1)S(1)} %get-tuple-element.58), channel_id=1, source_target_pairs={{0,1},{1,2},{2,3},{3,4},{4,5},{5,6},{6,7},{7,8},{8,9},{9,10},{10,1... | collective-permute-start | bytes 3080 | tf_op jit(solution)/shard_map/ppermute | solution.py:20
  4.5 4.7 %collective-permute-start.1 = (bf16[2,2,128]{2,1,0:T(2,128)(2,1)S(1)}, bf16[2,2,128]{2,1,0:T(2,128)(2,1)S(1)}, u32[]{:S(2)}, u32[]{:S(2)}) collective-permute-start(bf16[2,2,128]{2,1,0:T(2,128)(2,1)S(1)} %get-tuple-element.59), channel_id=1, source_target_pairs={{1,0},{2,1},{3,2},{4,3},{5,4},{6,5},{7,6},{8,7},{9,8},{10,9},{11,1... | collective-permute-start | bytes 3080 | tf_op jit(solution)/shard_map/ppermute | solution.py:21
  20.5 13.4 %collective-permute-start.2 = (bf16[2,132,128]{2,1,0:T(8,128)(2,1)S(1)}, bf16[2,132,128]{2,1,0:T(8,128)(2,1)S(1)}, u32[]{:S(2)}, u32[]{:S(2)}) collective-permute-start(bf16[2,132,128]{2,1,0:T(8,128)(2,1)S(1)} %pad_maximum_fusion.2), channel_id=1, source_target_pairs={{16,0},{32,16},{48,32},{64,48},{80,64},{96,80},{112,96},{128,112},... | collective-permute-start | bytes 202760 | tf_op jit(solution)/shard_map/ppermute | solution.py:29
  26.7 7.4 %copy-start.1 = (f32[16]{0:T(128)S(1)}, f32[16]{0:T(128)}, u32[]{:S(2)}) copy-start(f32[16]{0:T(128)} %param.10) | copy-start | bytes 196

commit v7 on v5

--- a/solution.py
+++ b/solution.py
@@ -41,7 +41,7 @@
     return (jnp.cos(phase_angle).astype(jnp.bfloat16), jnp.sin(phase_angle).astype(jnp.bfloat16))
 
 
-def conv_layers(rows_in, inside, conv1_w, conv1_b, conv2_w):
+def conv_one(rows_in, inside, conv1_w, conv1_b):
     sec_count = rows_in.shape[0]
     wide_rows = rows_in.shape[1] - 2
     strip_rows = wide_rows - 2
@@ -62,6 +62,12 @@
     hidden = jnp.where(inside[None, None, :, None], jax.nn.relu(layer_one), 0.0).astype(
         jnp.bfloat16
     )
+    return hidden
+
+
+def conv_two(hidden, conv2_w):
+    sec_count, channels, wide_rows, patch_len = hidden.shape
+    strip_rows = wide_rows - 2
     hidden_pad = jnp.pad(hidden, ((0, 0), (0, 0), (0, 0), (1, 1)))
     layer_two = jnp.zeros((sec_count, channels, strip_rows, patch_len), jnp.float32)
     for tap_row in range(3):
@@ -160,13 +166,14 @@
     tile_count = lax.axis_size("tile")
     tile_pos = lax.axis_index("tile")
     cosine, sin_table = dft_tables(patch_len)
-    padded_rows = with_halo(sections, (("tile", 1),), 2)
-    next_rows = from_behind(padded_rows, "sec", -1)
+    next_raw = from_behind(sections, "sec", -1)
+    padded_rows = with_halo(jnp.concatenate([sections, next_raw], axis=0), (("tile", 1),), 2)
     row_global = tile_pos * strip_rows - 1 + jnp.arange(strip_rows + 2, dtype=jnp.int32)
     inside = (row_global >= 0) & (row_global < strip_rows * tile_count)
-    own_feats = conv_layers(padded_rows, inside, conv1_w, conv1_b, conv2_w)
+    hidden_all = conv_one(padded_rows, inside, conv1_w, conv1_b)
+    own_feats = conv_two(hidden_all[:sec_here], conv2_w)
     own_real, own_imag = patch_spectra(own_feats, cosine, sin_table, rows_per)
-    next_feats = conv_layers(next_rows, inside, conv1_w, conv1_b, conv2_w)
+    next_feats = conv_two(hidden_all[sec_here:], conv2_w)
     next_real, next_imag = patch_spectra(next_feats, cosine, sin_table, rows_per)
     combined_real = jnp.concatenate([own_real, next_real], axis=0)
     combined_imag = jnp.concatenate([own_imag, next_imag], axis=0)

time: 63.4 us -> 67.6 us (1.066)
  the two profiles are of different devices: /device:TPU:512 before, /device:TPU:57 now
where the time goes in v7:
time: 67.6 us; the launch traced here: 67.2 us
  matrix products  18.6 us (28%)
  blocking collectives  16.8 us (25%)
  other arithmetic  9.44 us (14%)
  waiting for transfers between devices  8.76 us (13%)
  starting transfers between devices  6.99 us (10%)
  local copies, waits for them, and re-layouts  5.72 us (8%)
  between operations  0.98 us (1%)
    all_to_all x1, blocking collectives, tile_sum(): return jnp.sum(lax.all_to_all(copies, axis, 0, 0, tiled=False), axis=0)  16.8 us
    dot_general x18, matrix products, conv_two(): jnp.einsum('schw,co->sohw', window, conv2_w[3 * tap_row + tap_col], prefe...  12.8 us
    ppermute x1, waiting for transfers between devices, from_behind(): return lax.ppermute(block, axis, route)  6.02 us
    convert_element_type x1, other arithmetic, conv_one(): jnp.where(inside[None, None, :, None], jax.nn.relu(layer_one), 0.0)  3.79 us
    ppermute x1, starting transfers between devices, with_halo(): before = lax.ppermute(last, axis, up)  3.12 us
    ppermute x1, waiting for transfers between devices, with_halo(): after = lax.ppermute(initial, axis, down)  2.73 us
    ppermute x1, starting transfers between devices, from_behind(): return lax.ppermute(block, axis, route)  2.58 us
    unnamed x11, local copies, waits for them, and re-layouts  2.35 us
  transfers between devices with their start and end apart: 3, of which 2 were waited for; matrix products, arithmetic and copies ran while one was open for 6% of the time, Pallas kernels for 0%

profile of v7, /device:TPU:57, one launch (start us, length us, event | category | flops | bytes accessed | tf_op | source)
XLA Modules:
  0.0 67.2 jit_solution(11295263338679745458)
XLA Ops:
  0.6 2.6 %collective-permute-start = (bf16[2,128,128]{2,1,0:T(8,128)(2,1)}, bf16[2,128,128]{2,1,0:T(8,128)(2,1)S(1)}, u32[]{:S(2)}, u32[]{:S(2)}) collective-permute-start(bf16[2,128,128]{2,1,0:T(8,128)(2,1)} %param.6), channel_id=1, source_target_pairs={{16,0},{32,16},{48,32},{64,48},{80,64},{96,80},{112,96},{128,112},... | collective-permute-start | bytes 196616 | tf_op jit(solution)/shard_map/ppermute | solution.py:29
  3.2 0.8 %constant_dynamic-update-slice_fusion.1 = bf16[4,128,128]{2,1,0:T(8,128)(2,1)S(1)} fusion(bf16[2,128,128]{2,1,0:T(8,128)(2,1)} %param.6), kind=kLoop, calls=%fused_computation.112 | loop fusion | bytes 131072
  4.1 0.3 sine_convert_fusion
  4.4 0.3 fusion.58
  4.7 1.0 %bitcast_convert_fusion.8 = (f32[16]{0:T(128)S(1)}, f32[16]{0:T(128)S(1)}, f32[16]{0:T(128)S(1)}, f32[16]{0:T(128)S(1)}, f32[16]{0:T(128)S(1)}, /*index=5*/f32[1...) fusion(bf16[9,16]{1,0:T(8,128)(2,1)} %param.9), kind=kLoop, calls=%fused_computation.174 | loop fusion | flops 144 | bytes 864 | tf_op jit(solution)/shard_map/convert_element_type | solution.py:57
  5.6 0.7 compare_not_fusion
  6.5 0.7 %broadcast_multiply_fusion = (f32[2,1]{0,1:T(1,128)S(1)}, f32[2,1]{0,1:T(1,128)S(1)}, f32[2,1]{0,1:T(1,128)S(1)}) fusion(f32[]{:T(128)S(6)} %sub.56, s32[2]{0:T(128)} %param.7, s32[]{:T(128)S(6)} %mul.366, s32[2,1]{0,1:T(1,128)} %param.8), kind=kLoop, calls=%fused_computation.184 | loop fusion | flops 16 | bytes 48 | tf_op jit(solution)/shard_map/mul | solution.py:204
  7.2 6.0 %collective-permute-done = bf16[2,128,128]{2,1,0:T(8,128)(2,1)S(1)} collective-permute-done((bf16[2,128,128]{2,1,0:T(8,128)(2,1)}, bf16[2,128,128]{2,1,0:T(8,128)(2,1)S(1)}, u32[]{:S(2)}, u32[]{:S(2)}) %collective-permute-start) | collective-permute-done | bytes 65568 | tf_op jit(solution)/shard_map/ppermute | solution.py:29
  13.2 3.1 %collective-permute-start.1 = (bf16[4,2,128]{2,1,0:T(2,128)(2,1)S(1)}, bf16[4,2,128]{2,1,0:T(2,128)(2,1)S(1)}, u32[]{:S(2)}, u32[]{:S(2)}) collective-permute-start(bf16[4,2,128]{2,1,0:T(2,128)(2,1)S(1)} %get-tuple-element.47), channel_id=1, source_target_pairs={{0,1},{1,2},{2,3},{3,4},{4,5},{5,6},{6,7},{7,8},{8,9},{9,10},{10,1... | collective-permute-start | bytes 6152 | tf_op jit(solution)/shard_map/ppermute | solution.py:20
  16.3 1.3 %collective-permute-start.2 = (bf16[4,2,128]{2,1,0:T(2,128)(2,1)S(1)}, bf16[4,2,128]{2,1,0:T(2,128)(2,1)S(1)}, u32[]{:S(2)}, u32[]{:S(2)}) collective-permute-start(bf16[4,2,128]{2,1,0:T(2,128)(2,1)S(1)} %get-tuple-element.48), channel_id=1, source_target_pairs={{1,0},{2,1},{3,2},{4,3},{5,4},{6,5},{7,6},{8,7},{9,8},{10,9},{11,1... | collective-permute-start | bytes 6152 | tf_op jit(solution)/shard_map/ppermute | solution.py:21
  17.7 0.1 copy.170
  17.8 0.1 copy.171
  17.9 2.7 %collective-permute-done.2 = bf16[4,2,128]{2,1,0:T(2,128)(2,1)S(1)} collective-permute-done((bf16[4,2,128]{2,1,0:T(2,128)(2,1)S(1)}, bf16[4,2,128]{2,1,0:T(2,128)(2,1)S(1)}, u32[]{:S(2)}, u32[]{:S(2)}) %collective-permute-start.2) | collective-permute-done | bytes 2080 | tf_op jit(solution)/shard_map/ppermute | solution.py:21
  20.7 0.3 fusion.34
  21.1 3.8 %select_convert_fusion = bf16[4,16,130,128]{3,1,2,0:T(8,128)(2,1)S(1)} fusion(f32[4,130,128]{2,1,0:T(8,128)S(1)} %get-tuple-element.41, f32[16]{0:T(128)S(1)} %get-tuple-element.58, f32[4,130,128]{2,1,0:T(8,128)S(1)} %get-tuple-element.75, f32[16]{0:T(128)S(1)} %get-tuple-element.59, f32[4,130,128]{2,1,0:T(8,128)S(1)} %get-tuple-element.40, ...), kind=kLoop, calls=%fused_computation.2 | loop fusion | flops 22364160 | bytes 4526850 | tf_op jit(solution)/shard_map/convert_element_type | solution.py:62
  24.9 0.4 fusion.129
  25.2 0.4 copy-done
  25.6 0.5 fusion.15
  26.1 0.5 fusion.16
  26.6 0.5 fusion.17
  27.1 0.5 fusion.18
  27.6 0.5 fusion.19
  28.1 0.5 fusion.22
  28.5 0.5 fusion.24
  29.0 1.8 %fusion.26 = f32[2,128,128,16]{2,3,1,0:T(8,128)} fusion(bf16[4,16,130,128]{3,1,2,0:T(8,128)(2,1)S(1)} %select_convert_fusion, bf16[9,16,16]{2,1,0:T(8,128)(2,1)S(1)} %copy-done), kind=kOutput, calls=%fused_computation.53 | convolution fusion | flops 16777216 | bytes 3149824 | tf_op jit(solution)/shard_map/schw,co->sohw/dot_general | solution.py:76
  30.8 0.5 fusion.10
  31.3 0.5 fusion.11
  31.7 0.5 fusion.12
  32.2 0.5 fusion.13
  32.7 0.5 fusion.14
  33.2 0.5 fusion.28
  33.7 0.5 fusion.30
  34.1 0.4 fusion.32
  34.6 2.8 %fusion.7 = bf16[2,16,128,128]{3,1,2,0:T(8,128)(2,1)S(1)} fusion(f32[2,128,128,16]{2,3,1,0:T(8,128)S(1)} %fusion.22, f32[2,128,128,16]{2,3,1,0:T(8,128)S(1)} %fusion.19, f32[2,128,128,16]{2,3,1,0:T(8,128)S(1)} %fusion.18, f32[2,128,128,16]{2,3,1,0:T(8,128)S(1)} %fusion.24, f32[2,128,128,16]{2,3,1,0:T(8,128)S(1)} %fusion.17, ...), kind=kOutput, calls=%fused_computation.30 | convolution fusion | flops 21495808 | bytes 18894848 | tf_op jit(solution)/shard_map/schw,co->sohw/dot_general | solution.py:76
  37.4 0.3 copy.163
  37.7 0.7 %convolution_convert_fusion = bf16[4096,256]{1,0:T(8,128)(2,1)S(1)} fusion(bf16[4096,128]{1,0:T(8,128)(2,1)S(1)} %bitcast.222, bf16[128,128]{1,0:T(8,128)(2,1)S(1)} %get-tuple-element.77, bf16[128,128]{1,0:T(8,128)(2,1)S(1)} %get-tuple-element.78), kind=kOutput, calls=%fused_computation | convolution fusion | flops 269615104 | bytes 3211264 | tf_op jit(solution)/shard_map/dot_general | solution.py:90
  38.4 0.1 fusion.131
  38.5 0.7 %fusion.53 = f32[32,128,256]{2,1,0:T(8,128)S(1)} fusion(bf16[32,128,128]{2,1,0:T(8,128)(2,1)S(1)} %bitcast.230, bf16[128,128]{1,0:T(8,128)(2,1)S(1)} %get-tuple-element.80, bf16[128,128]{1,0:T(8,128)(2,1)S(1)} %get-tuple-element.78), kind=kOutput, calls=%fused_computation.102 | convolution fusion | flops 268566528 | bytes 5308416 | tf_op jit(solution)/shard_map/uy,byk->buk/dot_general | solution.py:97
  39.2 0.7 %fusion.5 = bf16[32,256,128]{1,2,0:T(8,128)(2,1)S(1)} fusion(f32[32,128,256]{2,1,0:T(8,128)S(1)} %fusion.53, bf16[32,128,128]{2,1,0:T(8,128)(2,1)S(1)} %bitcast.228, bf16[128,128]{1,0:T(8,128)(2,1)S(1)} %get-tuple-element.79, bf16[128,128]{1,0:T(8,128)(2,1)S(1)} %get-tuple-element.80), kind=kOutput, calls=%fused_computation.28 | convolution fusion | flops 270663680 | bytes 7405568 | tf_op jit(solution)/shard_map/uy,byk->buk/dot_general | solution.py:99
  40.0 0.6 fusion.130
  40.6 1.1 %fusion.6 = bf16[2,16,128,128]{3,1,2,0:T(8,128)(2,1)S(1)} fusion(f32[2,128,128,16]{2,3,1,0:T(8,128)S(1)} %fusion.28, f32[2,128,128,16]{2,3,1,0:T(8,128)S(1)} %fusion.14, f32[2,128,128,16]{2,3,1,0:T(8,128)S(1)} %fusion.13, f32[2,128,128,16]{2,3,1,0:T(8,128)S(1)} %fusion.30, f32[2,128,128,16]{2,3,1,0:T(8,128)S(1)} %fusion.12, ...), kind=kOutput, calls=%fused_computation.29 | convolution fusion | flops 21495808 | bytes 18894848 | tf_op jit(solution)/shard_map/schw,co->sohw/dot_general | solution.py:76
  41.7 0.3 copy.160
  42.0 0.9 %convolution_convert_fusion.1 = bf16[4096,256]{1,0:T(8,128)(2,1)S(1)} fusion(bf16[4096,128]{1,0:T(8,128)(2,1)S(1)} %bitcast.223, bf16[128,128]{1,0:T(8,128)(2,1)S(1)} %get-tuple-element.77, bf16[128,128]{1,0:T(8,128)(2,1)S(1)} %get-tuple-element.78), kind=kOutput, calls=%fused_computation.1 | convolution fusion | flops 269615104 | bytes 3211264 | tf_op jit(solution)/shard_map/dot_general | solution.py:90
  42.9 0.1 fusion.133
  43.0 0.7 %fusion.54 = f32[32,128,256]{2,1,0:T(8,128)S(1)} fusion(bf16[32,128,128]{2,1,0:T(8,128)(2,1)S(1)} %bitcast.231, bf16[128,128]{1,0:T(8,128)(2,1)S(1)} %get-tuple-element.80, bf16[128,128]{1,0:T(8,128)(2,1)S(1)} %get-tuple-element.78), kind=kOutput, calls=%fused_computation.103 | convolution fusion | flops 268566528 | bytes 5308416 | tf_op jit(solution)/shard_map/uy,byk->buk/dot_general | solution.py:97
  43.8 0.7 %fusion.4 = bf16[32,256,128]{1,2,0:T(8,128)(2,1)S(1)} fusion(f32[32,128,256]{2,1,0:T(8,128)S(1)} %fusion.54, bf16[32,128,128]{2,1,0:T(8,128)(2,1)S(1)} %bitcast.229, bf16[128,128]{1,0:T(8,128)(2,1)S(1)} %get-tuple-element.79, bf16[128,128]{1,0:T(8,128)(2,1)S(1)} %get-tuple-element.80), kind=kOutput, calls=%fused_computation.27 | convolution fusion | flops 270663680 | bytes 7405568 | tf_op jit(solution)/shard_map/uy,byk->buk/dot_general | solution.py:99
  44.5 0.6 fusion.132
  45.1 1.1 %fusion.3 = (bf16[2,128,128]{1,2,0:T(8,128)(2,1)S(1)}, bf16[2,128,128]{1,2,0:T(8,128)(2,1)S(1)}) fusion(bf16[2,1,16,128,128]{3,4,2,0,1:T(8,128)(2,1)S(1)} %bitcast.227, bf16[2,1,16,128,128]{3,4,2,0,1:T(8,128)(2,1)S(1)} %bitcast.226, bf16[2,1,16,128,128]{3,4,2,0,1:T(8,128)(2,1)S(1)} %bitcast.225, bf16[2,1,16,128,128]{3,4,2,0,1:T(8,128)(2,1)S(1)} %bitcast.224, ...), kind=kLoop, calls=%fused_computation.24 | loop fusion | flops 11468800 | bytes 4325378 | tf_op jit(solution)/shard_map/reduce_sum | solution.py:120
  46.2 0.1 copy.166
  46.3 0.1 copy.167
  46.5 0.1 fusion.40
  46.6 0.2 fusion.60
  46.7 0.2 fusion.8
  46.9 0.4 fusion.56
  47.3 0.5 fusion.137
  47.8 0.2 fusion.42
  48.0 0.2 multiply_reduce_fusion.1
  48.3 0.1 copy.173
  48.5 0.1 concatenate.51
  48.6 16.8 %all_to_all.5 = f32[16,2,7]{2,1,0:T(2,128)S(1)} all-to-all(f32[16,2,7]{2,1,0:T(2,128)S(1)} %broadcast_in_dim.38), channel_id=1, replica_groups=mesh['sec'=48,'tile'=16] {'tile'}, dimensions={0} | all-to-all | bytes 1792 | tf_op jit(solution)/shard_map/all_to_all | solution.py:35
  65.6 0.1 copy.208
  65.8 0.1 copy.204
  66.0 0.6 subtract_multiply_fusion
  66.6 0.7 copy.177
  (29 shorter events, 1.0 us)
Async XLA Ops:
  0.6 20.4 %copy-start.1 = (f32[16]{0:T(128)S(1)}, f32[16]{0:T(128)}, u32[]{:S(2)}) copy-start(f32[16]{0:T(128)} %param.10) | copy-start | bytes 196
  0.6 12.6 %collective-permute-start = (bf16[2,128,128]{2,1,0:T(8,128)(2,1)}, bf16[2,128,128]{2,1,0:T(8,128)(2,1)S(1)}, u32[]{:S(2)}, u32[]{:S(2)}) collective-permute-start(bf16[2,128,128]{2,1,0:T(8,128)(2,1)} %param.6), channel_id=1, source_target_pairs={{16,0},{32,16},{48,32},{64,48},{80,64},{96,80},{112,96},{128,112},... | collective-permute-start | bytes 196616 | tf_op jit(solution)/shard_map/ppermute | solution.py:29
  13.2 4.7 %collective-permute-start.1 = (bf16[4,2,128]{2,1,0:T(2,128)(2,1)S(1)}, bf16[4,2,128]{2,1,0:T(2,128)(2,1)S(1)}, u32[]{:S(2)}, u32[]{:S(2)}) collective-permute-start(bf16[4,2,128]{2,1,0:T(2,128)(2,1)S(1)} %get-tuple-element.47), channel_id=1, source_target_pairs={{0,1},{1,2},{2,3},{3,4},{4,5},{5,6},{6,7},{7,8},{8,9},{9,10},{10,1... | collective-permute-start | bytes 6152 | tf_op jit(solution)/shard_map/ppermute | solution.py:20
  16.3 4.3 %collective-permute-start.2 = (bf16[4,2,128]{2,1,0:T(2,128)(2,1)S(1)}, bf16[4,2,128]{2,1,0:T(2,128)(2,1)S(1)}, u32[]{:S(2)}, u32[]{:S(2)}) collective-permute-start(bf16[4,2,128]{2,1,0:T(2,128)(2,1)S(1)} %get-tuple-element.48), channel_id=1, source_target_pairs={{1,0},{2,1},{3,2},{4,3},{5,4},{6,5},{7,6},{8,7},{9,8},{10,9},{11,1... | collective-permute-start | bytes 6152 | tf_op jit(solution)/shard_map/ppermute | solution.py:21
  24.9 0.8 %copy-start = (bf16[9,16,16]{2,1,0:T(8,128)(2,1)S(1)}, bf16[9,16,16]{2,1,0:T(8,128)(2,1)}, u32[]{:S(2)}) copy-start(bf16[9,16,16]{2,1,0:T(8,128)(2,1)} %param.11) | copy-start | bytes 13828

commit v8 on v5

--- a/solution.py
+++ b/solution.py
@@ -4,6 +4,8 @@
 import jax.numpy as jnp
 from jax import lax
 from jax.sharding import PartitionSpec as P
+from jax.experimental import pallas as pl
+from jax.experimental.pallas import tpu as pltpu
 
 RIDGE_TERM = 1.0
 CORR_GAIN = 2.5
@@ -41,27 +43,65 @@
     return (jnp.cos(phase_angle).astype(jnp.bfloat16), jnp.sin(phase_angle).astype(jnp.bfloat16))
 
 
+def conv_one_kernel(w_ref, b_ref, keep_ref, x_ref, o_ref, img_ref):
+    wide_rows = x_ref.shape[1] - 2
+    patch_len = x_ref.shape[2]
+    channels = o_ref.shape[1]
+    out_rows = o_ref.shape[2]
+    img_ref[...] = jnp.zeros_like(img_ref)
+    img_ref[0 : wide_rows + 2, :] = x_ref[0].astype(jnp.float32)
+    lane = lax.broadcasted_iota(jnp.int32, (8, patch_len), 1)
+
+    def block(i, carry):
+        top = pl.multiple_of(i * 8, 8)
+        windows = []
+        for tap_row in range(3):
+            rows = img_ref[pl.ds(top + tap_row, 8), :]
+            left = jnp.where(lane == 0, 0.0, pltpu.roll(rows, 1, 1))
+            right = jnp.where(lane == patch_len - 1, 0.0, pltpu.roll(rows, patch_len - 1, 1))
+            windows.extend([left, rows, right])
+        keep = keep_ref[pl.ds(top, 8), :] > 0
+        for c in range(channels):
+            acc = jnp.zeros((8, patch_len), jnp.float32) + b_ref[c]
+            for t in range(9):
+                acc = acc + w_ref[t, c] * windows[t]
+            acc = jnp.where(keep, jnp.maximum(acc, 0.0), 0.0)
+            o_ref[0, c, pl.ds(top, 8), :] = acc.astype(o_ref.dtype)
+        return carry
+
+    lax.fori_loop(0, out_rows // 8, block, 0)
+
+
+def conv_one(rows_in, inside, conv1_w, conv1_b):
+    sec_count, padded_rows, patch_len = rows_in.shape
+    wide_rows = padded_rows - 2
+    channels = conv1_w.shape[1]
+    out_rows = -(-wide_rows // 8) * 8
+    keep = jnp.zeros((out_rows, patch_len), jnp.int32).at[:wide_rows].set(
+        jnp.broadcast_to(inside.astype(jnp.int32)[:, None], (wide_rows, patch_len))
+    )
+    return pl.pallas_call(
+        conv_one_kernel,
+        grid=(sec_count,),
+        in_specs=[
+            pl.BlockSpec(memory_space=pltpu.SMEM),
+            pl.BlockSpec(memory_space=pltpu.SMEM),
+            pl.BlockSpec((out_rows, patch_len), lambda s: (0, 0)),
+            pl.BlockSpec((1, padded_rows, patch_len), lambda s: (s, 0, 0)),
+        ],
+        out_specs=pl.BlockSpec((1, channels, out_rows, patch_len), lambda s: (s, 0, 0, 0)),
+        out_shape=jax.ShapeDtypeStruct((sec_count, channels, out_rows, patch_len), jnp.bfloat16),
+        scratch_shapes=[pltpu.VMEM((out_rows + 8, patch_len), jnp.float32)],
+    )(conv1_w.astype(jnp.float32), conv1_b, keep, rows_in)
+
+
 def conv_layers(rows_in, inside, conv1_w, conv1_b, conv2_w):
     sec_count = rows_in.shape[0]
     wide_rows = rows_in.shape[1] - 2
     strip_rows = wide_rows - 2
     patch_len = rows_in.shape[2]
     channels = conv1_w.shape[1]
-    padded = jnp.pad(rows_in, ((0, 0), (0, 0), (1, 1)))
-    layer_one = (
-        jnp.zeros((sec_count, channels, wide_rows, patch_len), jnp.float32)
-        + conv1_b[None, :, None, None]
-    )
-    for tap_row in range(3):
-        for tap_col in range(3):
-            weight_tap = conv1_w[3 * tap_row + tap_col].astype(jnp.float32)
-            window = padded[:, tap_row : tap_row + wide_rows, tap_col : tap_col + patch_len].astype(
-                jnp.float32
-            )
-            layer_one = layer_one + weight_tap[None, :, None, None] * window[:, None]
-    hidden = jnp.where(inside[None, None, :, None], jax.nn.relu(layer_one), 0.0).astype(
-        jnp.bfloat16
-    )
+    hidden = conv_one(rows_in, inside, conv1_w, conv1_b)
     hidden_pad = jnp.pad(hidden, ((0, 0), (0, 0), (0, 0), (1, 1)))
     layer_two = jnp.zeros((sec_count, channels, strip_rows, patch_len), jnp.float32)
     for tap_row in range(3):

time: 63.4 us -> 90.2 us (1.42)
  local copies, waits for them, and re-layouts: 4.82 us -> 22.8 us
  Pallas kernels: 0 us -> 13.2 us
  other arithmetic: 15.7 us -> 6.46 us
  matrix products: 15.3 us -> 20.1 us
    slice x0 -> x2, local copies, waits for them, and re-layouts: none -> 16.7 us  [conv_layers(): hidden_pad[:, :, tap_row:tap_row + strip_rows, tap_col:tap_col + patch_len]]
    pallas_call x0 -> x2, Pallas kernels: none -> 13.2 us  [conv_one(): pl.pallas_call(conv_one_kernel, grid=(sec_count,), in_specs=[pl.BlockSpec...]
    convert_element_type x5 -> x1, other arithmetic: 10.5 us -> 1.28 us  [conv_one(): conv1_w.astype(jnp.float32)]
    dot_general x18, matrix products: 9.71 us -> 14.5 us  [conv_layers(): jnp.einsum('schw,co->sohw', window, conv2_w[3 * tap_row + tap_col], prefe...]
  transfers between devices with their start and end apart: 3 -> 3, of which waited for: 1 -> 1; matrix products, arithmetic and copies ran while one was open for 27% -> 26% of each run, Pallas kernels for 0% -> 7%
where the time goes in v8:
time: 90.2 us; the launch traced here: 89.8 us
  local copies, waits for them, and re-layouts  22.8 us (25%)
  matrix products  20.1 us (22%)
  blocking collectives  18.2 us (20%)
  Pallas kernels  13.2 us (15%)
  starting transfers between devices  7.54 us (8%)
  other arithmetic  6.46 us (7%)
  between operations  0.98 us (1%)
    all_to_all x1, blocking collectives, tile_sum(): return jnp.sum(lax.all_to_all(copies, axis, 0, 0, tiled=False), axis=0)  18.2 us
    slice x2, local copies, waits for them, and re-layouts, conv_layers(): hidden_pad[:, :, tap_row:tap_row + strip_rows, tap_col:tap_col + patch_len]  16.7 us
    dot_general x18, matrix products, conv_layers(): jnp.einsum('schw,co->sohw', window, conv2_w[3 * tap_row + tap_col], prefe...  14.5 us
    pallas_call x2, Pallas kernels, conv_one(): pl.pallas_call(conv_one_kernel, grid=(sec_count,), in_specs=[pl.BlockSpec...  13.2 us
    ppermute x1, starting transfers between devices, with_halo(): before = lax.ppermute(last, axis, up)  3.38 us
    ppermute x1, starting transfers between devices, from_behind(): return lax.ppermute(block, axis, route)  2.86 us
  transfers between devices with their start and end apart: 3, of which 1 were waited for; matrix products, arithmetic and copies ran while one was open for 26% of the time, Pallas kernels for 7%

profile of v8, /device:TPU:512, one launch (start us, length us, event | category | flops | bytes accessed | tf_op | source)
XLA Modules:
  0.0 89.8 jit_solution(13195429819054772076)
XLA Ops:
  0.6 0.7 fusion.131
  1.3 3.4 %collective-permute-start = (bf16[2,2,128]{2,1,0:T(2,128)(2,1)S(1)}, bf16[2,2,128]{2,1,0:T(2,128)(2,1)S(1)}, u32[]{:S(2)}, u32[]{:S(2)}) collective-permute-start(bf16[2,2,128]{2,1,0:T(2,128)(2,1)S(1)} %get-tuple-element.74), channel_id=1, source_target_pairs={{0,1},{1,2},{2,3},{3,4},{4,5},{5,6},{6,7},{7,8},{8,9},{9,10},{10,1... | collective-permute-start | bytes 3080 | tf_op jit(solution)/shard_map/ppermute | solution.py:22
  4.7 1.3 %collective-permute-start.1 = (bf16[2,2,128]{2,1,0:T(2,128)(2,1)S(1)}, bf16[2,2,128]{2,1,0:T(2,128)(2,1)S(1)}, u32[]{:S(2)}, u32[]{:S(2)}) collective-permute-start(bf16[2,2,128]{2,1,0:T(2,128)(2,1)S(1)} %get-tuple-element.75), channel_id=1, source_target_pairs={{1,0},{2,1},{3,2},{4,3},{5,4},{6,5},{7,6},{8,7},{9,8},{10,9},{11,1... | collective-permute-start | bytes 3080 | tf_op jit(solution)/shard_map/ppermute | solution.py:23
  6.0 0.3 sine_convert_fusion
  6.3 0.3 fusion.67
  6.7 0.7 compare_not_fusion
  7.5 0.7 broadcast_multiply_fusion
  8.2 1.3 %convert_element_type.149.w_ref = f32[9,16]{1,0:T(8,128)} convert(bf16[9,16]{1,0:T(8,128)(2,1)} %param.13) | non-fusion elementwise | flops 144 | bytes 864 | tf_op jit(solution)/shard_map/convert_element_type | solution.py:95
  9.6 0.1 copy.297
  9.8 0.4 collective-permute-done.1
  10.2 0.9 pad_maximum_fusion.2.x_ref
  11.1 2.9 %collective-permute-start.2 = (bf16[2,132,128]{2,1,0:T(8,128)(2,1)S(1)}, bf16[2,132,128]{2,1,0:T(8,128)(2,1)S(1)}, u32[]{:S(2)}, u32[]{:S(2)}) collective-permute-start(bf16[2,132,128]{2,1,0:T(8,128)(2,1)S(1)} %pad_maximum_fusion.2.x_ref), channel_id=1, source_target_pairs={{16,0},{32,16},{48,32},{64,48},{80,64},{96,80},{112,96},{128,112},... | collective-permute-start | bytes 202760 | tf_op jit(solution)/shard_map/ppermute | solution.py:31
  14.0 0.7 scatter.14.keep_ref
  14.7 6.6 %shard_map.77 = bf16[2,16,136,128]{3,2,1,0:T(8,128)(2,1)} custom-call(f32[9,16]{1,0:T(8,128)} %convert_element_type.149.w_ref, f32[16]{0:T(128)} %b_ref.3, s32[136,128]{1,0:T(8,128)} %scatter.14.keep_ref, bf16[2,132,128]{2,1,0:T(8,128)(2,1)} %copy-done), custom_call_target="tpu_custom_call" | custom-call | tf_op jit(solution)/shard_map/pallas_call | solution.py:83
  21.3 8.3 %pad_slice_fusion.6 = (bf16[2,16,128,128]{3,2,1,0:T(8,128)(2,1)S(1)}, bf16[2,16,128,128]{3,2,1,0:T(8,128)(2,1)S(1)}, bf16[2,16,128,128]{3,2,1,0:T(8,128)(2,1)S(1...) fusion(bf16[2,16,136,128]{3,2,1,0:T(8,128)(2,1)} %shard_map.77), kind=kLoop, calls=%fused_computation.10 | loop fusion | bytes 13697024 | tf_op jit(solution)/shard_map/slice | solution.py:109
  29.6 0.7 fusion.33
  30.4 0.7 fusion.35
  31.1 0.7 fusion.37
  31.8 0.7 fusion.39
  32.5 0.7 fusion.41
  33.3 0.7 fusion.43
  34.0 0.7 fusion.45
  34.7 0.7 fusion.47
  35.5 1.4 %fusion.6 = bf16[2,16,128,128]{3,1,2,0:T(8,128)(2,1)S(1)} fusion(f32[2,128,128,16]{2,3,1,0:T(8,128)S(1)} %fusion.33, f32[2,128,128,16]{2,3,1,0:T(8,128)S(1)} %fusion.35, f32[2,128,128,16]{2,3,1,0:T(8,128)S(1)} %fusion.37, f32[2,128,128,16]{2,3,1,0:T(8,128)S(1)} %fusion.39, f32[2,128,128,16]{2,3,1,0:T(8,128)S(1)} %fusion.41, ...), kind=kOutput, calls=%fused_computation.28 | convolution fusion | flops 21495808 | bytes 18878464 | tf_op jit(solution)/shard_map/schw,co->sohw/dot_general | solution.py:110
  36.9 0.3 copy.277
  37.2 0.7 convolution_convert_fusion.1
  37.9 0.1 fusion.129
  38.0 0.7 fusion.63
  38.8 0.7 fusion.4
  39.5 0.6 fusion.128
  40.2 0.6 copy-done.2
  40.8 6.6 %shard_map.78 = bf16[2,16,136,128]{3,2,1,0:T(8,128)(2,1)} custom-call(f32[9,16]{1,0:T(8,128)} %convert_element_type.149.w_ref, f32[16]{0:T(128)} %b_ref.3, s32[136,128]{1,0:T(8,128)} %scatter.14.keep_ref, bf16[2,132,128]{2,1,0:T(8,128)(2,1)} %copy-done.2), custom_call_target="tpu_custom_call" | custom-call | tf_op jit(solution)/shard_map/pallas_call | solution.py:83
  47.4 8.4 %pad_slice_fusion = (bf16[2,16,128,128]{3,2,1,0:T(8,128)(2,1)S(1)}, bf16[2,16,128,128]{3,2,1,0:T(8,128)(2,1)S(1)}, bf16[2,16,128,128]{3,2,1,0:T(8,128)(2,1)S(1)}...) fusion(bf16[2,16,136,128]{3,2,1,0:T(8,128)(2,1)} %shard_map.78), kind=kLoop, calls=%fused_computation.4 | loop fusion | bytes 13697024 | tf_op jit(solution)/shard_map/slice | solution.py:109
  55.8 0.7 fusion.16
  56.5 0.7 fusion.18
  57.2 0.7 fusion.20
  58.0 0.7 fusion.22
  58.7 0.7 fusion.24
  59.4 0.7 fusion.26
  60.1 0.7 fusion.28
  60.9 0.7 fusion.30
  61.6 1.4 %fusion.9 = bf16[2,16,128,128]{3,1,2,0:T(8,128)(2,1)S(1)} fusion(f32[2,128,128,16]{2,3,1,0:T(8,128)S(1)} %fusion.16, f32[2,128,128,16]{2,3,1,0:T(8,128)S(1)} %fusion.18, f32[2,128,128,16]{2,3,1,0:T(8,128)S(1)} %fusion.20, f32[2,128,128,16]{2,3,1,0:T(8,128)S(1)} %fusion.22, f32[2,128,128,16]{2,3,1,0:T(8,128)S(1)} %fusion.24, ...), kind=kOutput, calls=%fused_computation.33 | convolution fusion | flops 21495808 | bytes 18878464 | tf_op jit(solution)/shard_map/schw,co->sohw/dot_general | solution.py:110
  63.0 0.3 copy.289
  63.3 0.7 convolution_convert_fusion
  64.0 0.1 fusion.127
  64.2 0.7 fusion.62
  64.9 0.7 fusion.5
  65.7 0.6 fusion.126
  66.3 1.1 %fusion.3 = (bf16[2,128,128]{1,2,0:T(8,128)(2,1)S(1)}, bf16[2,128,128]{1,2,0:T(8,128)(2,1)S(1)}) fusion(bf16[2,1,16,128,128]{3,4,2,0,1:T(8,128)(2,1)S(1)} %bitcast.198, bf16[2,1,16,128,128]{3,4,2,0,1:T(8,128)(2,1)S(1)} %bitcast.197, bf16[2,1,16,128,128]{3,4,2,0,1:T(8,128)(2,1)S(1)} %bitcast.200, bf16[2,1,16,128,128]{3,4,2,0,1:T(8,128)(2,1)S(1)} %bitcast.199, ...), kind=kLoop, calls=%fused_computation.23 | loop fusion | flops 11468800 | bytes 4325378 | tf_op jit(solution)/shard_map/reduce_sum | solution.py:154
  67.3 0.1 copy.292
  67.5 0.1 copy.293
  67.6 0.1 fusion.49
  67.7 0.2 fusion.69
  67.9 0.2 fusion.7
  68.1 0.4 fusion.65
  68.5 0.5 fusion.133
  69.0 0.2 fusion.51
  69.2 0.2 multiply_reduce_fusion.1
  69.4 0.1 copy.299
  69.6 0.1 concatenate.42
  69.7 18.2 %all_to_all.5 = f32[16,2,7]{2,1,0:T(2,128)S(1)} all-to-all(f32[16,2,7]{2,1,0:T(2,128)S(1)} %broadcast_in_dim.27), channel_id=1, replica_groups=mesh['sec'=48,'tile'=16] {'tile'}, dimensions={0} | all-to-all | bytes 1792 | tf_op jit(solution)/shard_map/all_to_all | solution.py:37
  88.3 0.1 copy.335
  88.6 0.6 subtract_multiply_fusion
  89.2 0.7 copy.303
  (32 shorter events, 1.1 us)
Async XLA Ops:
  1.3 8.4 %collective-permute-start = (bf16[2,2,128]{2,1,0:T(2,128)(2,1)S(1)}, bf16[2,2,128]{2,1,0:T(2,128)(2,1)S(1)}, u32[]{:S(2)}, u32[]{:S(2)}) collective-permute-start(bf16[2,2,128]{2,1,0:T(2,128)(2,1)S(1)} %get-tuple-element.74), channel_id=1, source_target_pairs={{0,1},{1,2},{2,3},{3,4},{4,5},{5,6},{6,7},{7,8},{8,9},{9,10},{10,1... | collective-permute-start | bytes 3080 | tf_op jit(solution)/shard_map/ppermute | solution.py:22
  4.7 5.5 %collective-permute-start.1 = (bf16[2,2,128]{2,1,0:T(2,128)(2,1)S(1)}, bf16[2,2,128]{2,1,0:T(2,128)(2,1)S(1)}, u32[]{:S(2)}, u32[]{:S(2)}) collective-permute-start(bf16[2,2,128]{2,1,0:T(2,128)(2,1)S(1)} %get-tuple-element.75), channel_id=1, source_target_pairs={{1,0},{2,1},{3,2},{4,3},{5,4},{6,5},{7,6},{8,7},{9,8},{10,9},{11,1... | collective-permute-start | bytes 3080 | tf_op jit(solution)/shard_map/ppermute | solution.py:23
  11.1 3.6 %copy-start = (bf16[2,132,128]{2,1,0:T(8,128)(2,1)}, bf16[2,132,128]{2,1,0:T(8,128)(2,1)S(1)}, u32[]{:S(2)}) copy-start(bf16[2,132,128]{2,1,0:T(8,128)(2,1)S(1)} %pad_maximum_fusion.2.x_ref) | copy-start | bytes 202756
  11.1 29.1 %collective-permute-start.2 = (bf16[2,132,128]{2,1,0:T(8,128)(2,1)S(1)}, bf16[2,132,128]{2,1,0:T(8,128)(2,1)S(1)}, u32[]{:S(2)}, u32[]{:S(2)}) collective-permute-start(bf16[2,132,128]{2,1,0:T(8,128)(2,1)S(1)} %pad_maximum_fusion.2.x_ref), channel_id=1, source_target_pairs={{16,0},{32,16},{48,32},{64,48},{80,64},{96,80},{112,96},{128,112},... | collective-permute-start | bytes 202760 | tf_op jit(solution)/shard_map/ppermute | solution.py:31
  21.3 8.3 %copy-start.1 = (bf16[9,16,16]{2,1,0:T(8,128)(2,1)S(1)}, bf16[9,16,16]{2,1,0:T(8,128)(2,1)}, u32[]{:S(2)}) copy-start(bf16[9,16,16]{2,1,0:T(8,128)(2,1)} %param.15) | copy-start | bytes 13828
  40.1 0.6 copy-start.2

commit v9 on v5

--- a/solution.py
+++ b/solution.py
@@ -201,16 +201,16 @@
         axis=1,
     )
     totals = tile_sum(partial, "tile")
-    weight_sum, weighted_y, weighted_yy = totals[:, 0], totals[:, 1], totals[:, 2]
-    flow_sum = totals[:, 3:5].T
-    flow_y_sum = totals[:, 5:7].T
-    m_zero = weight_sum + RIDGE_TERM
-    m_two = weighted_yy + RIDGE_TERM
+    weighted_y = totals[:, 1:2]
+    m_zero = totals[:, 0:1] + RIDGE_TERM
+    m_two = totals[:, 2:3] + RIDGE_TERM
     determinant = m_zero * m_two - weighted_y * weighted_y
-    offset_coef = (m_two[None] * flow_sum - weighted_y[None] * flow_y_sum) / determinant[None]
-    slope_coef = (m_zero[None] * flow_y_sum - weighted_y[None] * flow_sum) / determinant[None]
-    affine = jnp.stack([offset_coef[0], slope_coef[0], offset_coef[1], slope_coef[1]], axis=1)
-    fitted = offset_coef[:, :, None] + slope_coef[:, :, None] * grid_y[None, None, :]
+    flow_sum = totals[:, 3:5]
+    flow_y_sum = totals[:, 5:7]
+    offset_coef = (m_two * flow_sum - weighted_y * flow_y_sum) / determinant
+    slope_coef = (m_zero * flow_y_sum - weighted_y * flow_sum) / determinant
+    affine = jnp.stack([offset_coef, slope_coef], axis=2).reshape(sec_here, 4)
+    fitted = offset_coef.T[:, :, None] + slope_coef.T[:, :, None] * grid_y[None, None, :]
     residual = (flow_est - fitted) * weights[None]
     return (residual, affine)
 

time: 63.4 us -> 63.6 us (level)
    unnamed x10 -> x9, local copies, waits for them, and re-layouts: 1.12 us -> 0.47 us
    reshape x0 -> x1, local copies, waits for them, and re-layouts: none -> 0.64 us  [local(): affine = jnp.stack([offset_coef, slope_coef], axis=2).reshape(sec_here, 4)]
where the time goes in v9:
time: 63.6 us; the launch traced here: 63.2 us
  blocking collectives  18.2 us (29%)
  other arithmetic  15.6 us (25%)
  matrix products  15.3 us (24%)
  starting transfers between devices  7.21 us (11%)
  local copies, waits for them, and re-layouts  5.17 us (8%)
  between operations  0.99 us (2%)
  waiting for transfers between devices  0.78 us (1%)
    all_to_all x1, blocking collectives, tile_sum(): return jnp.sum(lax.all_to_all(copies, axis, 0, 0, tiled=False), axis=0)  18.2 us
    dot_general x18, matrix products, conv_layers(): jnp.einsum('schw,co->sohw', window, conv2_w[3 * tap_row + tap_col], prefe...  9.71 us
    convert_element_type x2, other arithmetic, conv_layers(): jnp.where(inside[None, None, :, None], jax.nn.relu(layer_one), 0.0)  8.23 us
    ppermute x1, starting transfers between devices, with_halo(): before = lax.ppermute(last, axis, up)  3.38 us
    ppermute x1, starting transfers between devices, from_behind(): return lax.ppermute(block, axis, route)  2.53 us
    dot_general x2, matrix products, patch_spectra(): jnp.einsum('uy,byk->buk', left_sin, half_sin, preferred_element_type=jnp....  1.49 us
    dot_general x2, matrix products, patch_spectra(): jnp.einsum('uy,byk->buk', left_cos, half_cos, preferred_element_type=jnp....  1.49 us
    dot_general x2, matrix products, patch_spectra(): jnp.dot(flat_rows, jnp.concatenate([cosine, sin_table], axis=1), preferre...  1.36 us
  transfers between devices with their start and end apart: 3, of which 1 were waited for; matrix products, arithmetic and copies ran while one was open for 27% of the time, Pallas kernels for 0%

profile of v9, /device:TPU:512, one launch (start us, length us, event | category | flops | bytes accessed | tf_op | source)
XLA Modules:
  0.0 63.2 jit_solution(14450657604467682543)
XLA Ops:
  0.6 0.7 %fusion.141 = (bf16[2,2,128]{2,1,0:T(2,128)(2,1)S(1)}, bf16[2,2,128]{2,1,0:T(2,128)(2,1)S(1)}) fusion(bf16[2,128,128]{2,1,0:T(8,128)(2,1)} %param.6), kind=kLoop, calls=%fused_computation.231 | loop fusion | bytes 4096 | tf_op jit(solution)/shard_map/slice | solution.py:18
  1.4 3.4 %collective-permute-start = (bf16[2,2,128]{2,1,0:T(2,128)(2,1)S(1)}, bf16[2,2,128]{2,1,0:T(2,128)(2,1)S(1)}, u32[]{:S(2)}, u32[]{:S(2)}) collective-permute-start(bf16[2,2,128]{2,1,0:T(2,128)(2,1)S(1)} %get-tuple-element.54), channel_id=1, source_target_pairs={{0,1},{1,2},{2,3},{3,4},{4,5},{5,6},{6,7},{7,8},{8,9},{9,10},{10,1... | collective-permute-start | bytes 3080 | tf_op jit(solution)/shard_map/ppermute | solution.py:20
  4.7 1.3 %collective-permute-start.1 = (bf16[2,2,128]{2,1,0:T(2,128)(2,1)S(1)}, bf16[2,2,128]{2,1,0:T(2,128)(2,1)S(1)}, u32[]{:S(2)}, u32[]{:S(2)}) collective-permute-start(bf16[2,2,128]{2,1,0:T(2,128)(2,1)S(1)} %get-tuple-element.55), channel_id=1, source_target_pairs={{1,0},{2,1},{3,2},{4,3},{5,4},{6,5},{7,6},{8,7},{9,8},{10,9},{11,1... | collective-permute-start | bytes 3080 | tf_op jit(solution)/shard_map/ppermute | solution.py:21
  6.0 0.3 sine_convert_fusion
  6.3 0.3 fusion.64
  6.6 1.0 %bitcast_convert_fusion.8 = (f32[16]{0:T(128)S(1)}, f32[16]{0:T(128)S(1)}, f32[16]{0:T(128)S(1)}, f32[16]{0:T(128)S(1)}, f32[16]{0:T(128)S(1)}, /*index=5*/f32[1...) fusion(bf16[9,16]{1,0:T(8,128)(2,1)} %param.9), kind=kLoop, calls=%fused_computation.187 | loop fusion | flops 144 | bytes 864 | tf_op jit(solution)/shard_map/convert_element_type | solution.py:57
  7.6 0.7 %compare_not_fusion = (pred[2]{0:T(512)(128)(4,1)S(1)}, pred[2]{0:T(512)(128)(4,1)S(1)}) fusion(s32[2]{0:T(128)} %param.7, s32[]{:T(128)S(6)} %mul.458), kind=kLoop, calls=%fused_computation.167 | loop fusion | flops 10 | bytes 16 | tf_op jit(solution)/shard_map/not | solution.py:115
  8.5 0.7 %broadcast_multiply_fusion = (f32[2,1]{0,1:T(1,128)S(1)}, f32[2,1]{0,1:T(1,128)S(1)}, f32[2,1]{0,1:T(1,128)S(1)}) fusion(f32[]{:T(128)S(6)} %sub.50, s32[2]{0:T(128)} %param.7, s32[]{:T(128)S(6)} %mul.458, s32[2,1]{0,1:T(1,128)} %param.8), kind=kLoop, calls=%fused_computation.195 | loop fusion | flops 16 | bytes 48 | tf_op jit(solution)/shard_map/mul | solution.py:197
  9.2 0.1 copy.182
  9.3 0.1 copy.183
  9.4 0.8 %collective-permute-done.1 = bf16[2,2,128]{2,1,0:T(2,128)(2,1)S(1)} collective-permute-done((bf16[2,2,128]{2,1,0:T(2,128)(2,1)S(1)}, bf16[2,2,128]{2,1,0:T(2,128)(2,1)S(1)}, u32[]{:S(2)}, u32[]{:S(2)}) %collective-permute-start.1) | collective-permute-done | bytes 1056 | tf_op jit(solution)/shard_map/ppermute | solution.py:21
  10.2 0.9 %pad_maximum_fusion.2 = bf16[2,132,128]{2,1,0:T(8,128)(2,1)S(1)} fusion(bf16[2,2,128]{2,1,0:T(2,128)(2,1)S(1)} %collective-permute-done.1, bf16[2,128,128]{2,1,0:T(8,128)(2,1)} %param.6, bf16[2,2,128]{2,1,0:T(2,128)(2,1)S(1)} %collective-permute-done), kind=kLoop, calls=%fused_computation.101 | loop fusion | flops 202752 | bytes 135168 | tf_op jit(solution)/shard_map/concatenate | solution.py:22
  11.1 2.5 %collective-permute-start.2 = (bf16[2,132,128]{2,1,0:T(8,128)(2,1)S(1)}, bf16[2,132,128]{2,1,0:T(8,128)(2,1)S(1)}, u32[]{:S(2)}, u32[]{:S(2)}) collective-permute-start(bf16[2,132,128]{2,1,0:T(8,128)(2,1)S(1)} %pad_maximum_fusion.2), channel_id=1, source_target_pairs={{16,0},{32,16},{48,32},{64,48},{80,64},{96,80},{112,96},{128,112},... | collective-permute-start | bytes 202760 | tf_op jit(solution)/shard_map/ppermute | solution.py:29
  13.6 1.1 %fusion.38 = (f32[2,130,128]{2,1,0:T(8,128)S(1)}, f32[2,130,128]{2,1,0:T(8,128)S(1)}, f32[2,130,128]{2,1,0:T(8,128)S(1)}, f32[2,130,128]{2,1,0:T(8,128)S(1)}, f3...) fusion(bf16[2,132,128]{2,1,0:T(8,128)(2,1)S(1)} %pad_maximum_fu, ...), kind=kLoop, calls=%fused_computation.85 | loop fusion | flops 499200 | bytes 1404928 | tf_op jit(solution)/shard_map/convert_element_type | solution.py:58
  14.7 4.4 %select_convert_fusion.1 = bf16[2,16,130,128]{3,1,2,0:T(8,128)(2,1)S(1)} fusion(f32[2,130,128]{2,1,0:T(8,128)S(1)} %get-tuple-element.50, f32[16]{0:T(128)S(1)} %get-tuple-element.65, f32[2,130,128]{2,1,0:T(8,128)S(1)} %get-tuple-element.81, f32[16]{0:T(128)S(1)} %get-tuple-element.66, f32[2,130,128]{2,1,0:T(8,128)S(1)} %get-tuple-element.49, ...), kind=kLoop, calls=%fused_computation.21 | loop fusion | flops 11182080 | bytes 2263810 | tf_op jit(solution)/shard_map/convert_element_type | solution.py:62
  19.2 0.5 fusion.10
  19.6 0.5 fusion.11
  20.1 0.5 fusion.12
  20.6 0.5 fusion.13
  21.1 0.5 fusion.14
  21.6 0.4 fusion.28
  22.0 0.5 fusion.30
  22.5 0.5 fusion.32
  22.9 1.1 %fusion.6 = bf16[2,16,128,128]{3,1,2,0:T(8,128)(2,1)S(1)} fusion(f32[2,128,128,16]{2,3,1,0:T(8,128)S(1)} %fusion.28, f32[2,128,128,16]{2,3,1,0:T(8,128)S(1)} %fusion.14, f32[2,128,128,16]{2,3,1,0:T(8,128)S(1)} %fusion.13, f32[2,128,128,16]{2,3,1,0:T(8,128)S(1)} %fusion.30, f32[2,128,128,16]{2,3,1,0:T(8,128)S(1)} %fusion.12, ...), kind=kOutput, calls=%fused_computation.30 | convolution fusion | flops 21495808 | bytes 18894848 | tf_op jit(solution)/shard_map/schw,co->sohw/dot_general | solution.py:70
  24.0 0.3 copy.172
  24.3 0.7 %convolution_convert_fusion.1 = bf16[4096,256]{1,0:T(8,128)(2,1)S(1)} fusion(bf16[4096,128]{1,0:T(8,128)(2,1)S(1)} %bitcast.215, bf16[128,128]{1,0:T(8,128)(2,1)S(1)} %get-tuple-element.83, bf16[128,128]{1,0:T(8,128)(2,1)S(1)} %get-tuple-element.84), kind=kOutput, calls=%fused_computation.1 | convolution fusion | flops 269615104 | bytes 3211264 | tf_op jit(solution)/shard_map/dot_general | solution.py:84
  25.0 0.1 fusion.139
  25.2 0.7 %fusion.60 = f32[32,128,256]{2,1,0:T(8,128)S(1)} fusion(bf16[32,128,128]{2,1,0:T(8,128)(2,1)S(1)} %bitcast.223, bf16[128,128]{1,0:T(8,128)(2,1)S(1)} %get-tuple-element.86, bf16[128,128]{1,0:T(8,128)(2,1)S(1)} %get-tuple-element.84), kind=kOutput, calls=%fused_computation.119 | convolution fusion | flops 268566528 | bytes 5308416 | tf_op jit(solution)/shard_map/uy,byk->buk/dot_general | solution.py:91
  25.9 0.7 %fusion.4 = bf16[32,256,128]{1,2,0:T(8,128)(2,1)S(1)} fusion(f32[32,128,256]{2,1,0:T(8,128)S(1)} %fusion.60, bf16[32,128,128]{2,1,0:T(8,128)(2,1)S(1)} %bitcast.221, bf16[128,128]{1,0:T(8,128)(2,1)S(1)} %get-tuple-element.85, bf16[128,128]{1,0:T(8,128)(2,1)S(1)} %get-tuple-element.86), kind=kOutput, calls=%fused_computation.28 | convolution fusion | flops 270663680 | bytes 7405568 | tf_op jit(solution)/shard_map/uy,byk->buk/dot_general | solution.py:93
  26.7 0.6 fusion.138
  27.3 0.2 fusion.44
  27.5 3.8 %select_convert_fusion = bf16[2,16,130,128]{3,1,2,0:T(8,128)(2,1)S(1)} fusion(f32[2,130,128]{2,1,0:T(8,128)S(1)} %get-tuple-element.41, f32[2,130,128]{2,1,0:T(8,128)S(1)} %get-tuple-element.42, f32[2,130,128]{2,1,0:T(8,128)S(1)} %get-tuple-element.40, f32[2,130,128]{2,1,0:T(8,128)S(1)} %get-tuple-element.39, f32[2,130,128]{2,1,0:T(8,128)S(1)} %get-tuple-element.43, ...), kind=kLoop, calls=%fused_computation.20 | loop fusion | flops 11182080 | bytes 2263810 | tf_op jit(solution)/shard_map/convert_element_type | solution.py:62
  31.3 0.5 fusion.15
  31.8 0.5 fusion.16
  32.3 0.5 fusion.17
  32.8 0.5 fusion.18
  33.2 0.5 fusion.19
  33.7 0.5 fusion.22
  34.2 0.4 fusion.24
  34.7 0.5 fusion.26
  35.1 1.1 %fusion.7 = bf16[2,16,128,128]{3,1,2,0:T(8,128)(2,1)S(1)} fusion(f32[2,128,128,16]{2,3,1,0:T(8,128)S(1)} %fusion.22, f32[2,128,128,16]{2,3,1,0:T(8,128)S(1)} %fusion.19, f32[2,128,128,16]{2,3,1,0:T(8,128)S(1)} %fusion.18, f32[2,128,128,16]{2,3,1,0:T(8,128)S(1)} %fusion.24, f32[2,128,128,16]{2,3,1,0:T(8,128)S(1)} %fusion.17, ...), kind=kOutput, calls=%fused_computation.31 | convolution fusion | flops 21495808 | bytes 18894848 | tf_op jit(solution)/shard_map/schw,co->sohw/dot_general | solution.py:70
  36.2 0.3 copy.175
  36.5 0.7 %convolution_convert_fusion = bf16[4096,256]{1,0:T(8,128)(2,1)S(1)} fusion(bf16[4096,128]{1,0:T(8,128)(2,1)S(1)} %bitcast.216, bf16[128,128]{1,0:T(8,128)(2,1)S(1)} %get-tuple-element.83, bf16[128,128]{1,0:T(8,128)(2,1)S(1)} %get-tuple-element.84), kind=kOutput, calls=%fused_computation | convolution fusion | flops 269615104 | bytes 3211264 | tf_op jit(solution)/shard_map/dot_general | solution.py:84
  37.2 0.1 fusion.137
  37.3 0.7 %fusion.59 = f32[32,128,256]{2,1,0:T(8,128)S(1)} fusion(bf16[32,128,128]{2,1,0:T(8,128)(2,1)S(1)} %bitcast.224, bf16[128,128]{1,0:T(8,128)(2,1)S(1)} %get-tuple-element.86, bf16[128,128]{1,0:T(8,128)(2,1)S(1)} %get-tuple-element.84), kind=kOutput, calls=%fused_computation.118 | convolution fusion | flops 268566528 | bytes 5308416 | tf_op jit(solution)/shard_map/uy,byk->buk/dot_general | solution.py:91
  38.1 0.7 %fusion.5 = bf16[32,256,128]{1,2,0:T(8,128)(2,1)S(1)} fusion(f32[32,128,256]{2,1,0:T(8,128)S(1)} %fusion.59, bf16[32,128,128]{2,1,0:T(8,128)(2,1)S(1)} %bitcast.222, bf16[128,128]{1,0:T(8,128)(2,1)S(1)} %get-tuple-element.85, bf16[128,128]{1,0:T(8,128)(2,1)S(1)} %get-tuple-element.86), kind=kOutput, calls=%fused_computation.29 | convolution fusion | flops 270663680 | bytes 7405568 | tf_op jit(solution)/shard_map/uy,byk->buk/dot_general | solution.py:93
  38.8 0.6 fusion.136
  39.4 1.1 %fusion.3 = (bf16[2,128,128]{1,2,0:T(8,128)(2,1)S(1)}, bf16[2,128,128]{1,2,0:T(8,128)(2,1)S(1)}) fusion(bf16[2,1,16,128,128]{3,4,2,0,1:T(8,128)(2,1)S(1)} %bitcast.218, bf16[2,1,16,128,128]{3,4,2,0,1:T(8,128)(2,1)S(1)} %bitcast.217, bf16[2,1,16,128,128]{3,4,2,0,1:T(8,128)(2,1)S(1)} %bitcast.220, bf16[2,1,16,128,128]{3,4,2,0,1:T(8,128)(2,1)S(1)} %bitcast.219, ...), kind=kLoop, calls=%fused_computation.25 | loop fusion | flops 11468800 | bytes 4325378 | tf_op jit(solution)/shard_map/reduce_sum | solution.py:114
  40.5 0.1 copy.178
  40.6 0.1 copy.179
  40.7 0.1 fusion.34
  40.9 0.2 fusion.66
  41.0 0.2 fusion.8
  41.2 0.4 fusion.62
  41.6 0.5 fusion.144
  42.1 0.2 fusion.36
  42.3 0.2 multiply_reduce_fusion.1
  42.6 0.1 copy.185
  42.7 0.1 concatenate.47
  42.8 18.2 %all_to_all.5 = f32[16,2,7]{2,1,0:T(2,128)S(1)} all-to-all(f32[16,2,7]{2,1,0:T(2,128)S(1)} %broadcast_in_dim.37), channel_id=1, replica_groups=mesh['sec'=48,'tile'=16] {'tile'}, dimensions={0} | all-to-all | bytes 1792 | tf_op jit(solution)/shard_map/all_to_all | solution.py:35
  61.4 0.1 copy.221
  61.7 0.6 fusion.103
  62.5 0.1 copy.190
  62.6 0.6 %reshape.360 = f32[2,4]{1,0:T(2,128)} reshape(f32[2,2,2]{2,1,0:T(2,128)S(1)} %copy.190) | data formatting | bytes 64 | tf_op jit(solution)/shard_map/reshape | solution.py:212
  (29 shorter events, 1.2 us)
Async XLA Ops:
  0.6 18.5 %copy-start = (bf16[9,16,16]{2,1,0:T(8,128)(2,1)S(1)}, bf16[9,16,16]{2,1,0:T(8,128)(2,1)}, u32[]{:S(2)}) copy-start(bf16[9,16,16]{2,1,0:T(8,128)(2,1)} %param.11) | copy-start | bytes 13828
  1.4 8.1 %collective-permute-start = (bf16[2,2,128]{2,1,0:T(2,128)(2,1)S(1)}, bf16[2,2,128]{2,1,0:T(2,128)(2,1)S(1)}, u32[]{:S(2)}, u32[]{:S(2)}) collective-permute-start(bf16[2,2,128]{2,1,0:T(2,128)(2,1)S(1)} %get-tuple-element.54), channel_id=1, source_target_pairs={{0,1},{1,2},{2,3},{3,4},{4,5},{5,6},{6,7},{7,8},{8,9},{9,10},{10,1... | collective-permute-start | bytes 3080 | tf_op jit(solution)/shard_map/ppermute | solution.py:20
  4.7 5.5 %collective-permute-start.1 = (bf16[2,2,128]{2,1,0:T(2,128)(2,1)S(1)}, bf16[2,2,128]{2,1,0:T(2,128)(2,1)S(1)}, u32[]{:S(2)}, u32[]{:S(2)}) collective-permute-start(bf16[2,2,128]{2,1,0:T(2,128)(2,1)S(1)} %get-tuple-element.55), channel_id=1, source_target_pairs={{1,0},{2,1},{3,2},{4,3},{5,4},{6,5},{7,6},{8,7},{9,8},{10,9},{11,1... | collective-permute-start | bytes 3080 | tf_op jit(solution)/shard_map/ppermute | solution.py:21
  11.1 16.2 %collective-permute-start.2 = (bf16[2,132,128]{2,1,0:T(8,128)(2,1)S(1)}, bf16[2,132,128]{2,1,0:T(8,128)(2,1)S(1)}, u32[]{:S(2)}, u32[]{:S(2)}) collective-permute-start(bf16[2,132,128]{2,1,0:T(8,128)(2,1)S(1)} %pad_maximum_fusion.2), channel_id=1, source_target_pairs={{16,0},{32,16},{48,32},{64,48},{80,64},{96,80},{112,96},{128,112},... | collective-permute-start | bytes 202760 | tf_op jit(solution)/shard_map/ppermute | solution.py:29
  26.7 0.8 %copy-start.1 = (f32[16]{0:T(128)S(1)}, f32[16]{0:T(128)}, u32[]{:S(2)}) copy-start(f32[16]{0:T(128)} %param.10) | copy-start | bytes 196

commit v10 on v5

--- a/solution.py
+++ b/solution.py
@@ -92,13 +92,7 @@
         "uy,byk->buk", left_cos, half_cos, preferred_element_type=jnp.float32
     ) + jnp.einsum("uy,byk->buk", left_sin, half_sin, preferred_element_type=jnp.float32)
     spec_both = spec_both.astype(jnp.bfloat16)
-    spec_real = spec_both[:, :patch_len]
-    spec_imag = spec_both[:, patch_len:]
-    out_shape = (sec_count, rows_per, channels, patch_len, patch_len)
-    return (
-        spec_real.reshape(out_shape),
-        spec_imag.reshape(out_shape),
-    )
+    return spec_both.reshape(sec_count, rows_per, channels, 2 * patch_len, patch_len)
 
 
 def correlate(own_real, own_imag, part_real, part_imag, pair_valid, cosine, sin_table):
@@ -165,18 +159,14 @@
     row_global = tile_pos * strip_rows - 1 + jnp.arange(strip_rows + 2, dtype=jnp.int32)
     inside = (row_global >= 0) & (row_global < strip_rows * tile_count)
     own_feats = conv_layers(padded_rows, inside, conv1_w, conv1_b, conv2_w)
-    own_real, own_imag = patch_spectra(own_feats, cosine, sin_table, rows_per)
+    own_both = patch_spectra(own_feats, cosine, sin_table, rows_per)
     next_feats = conv_layers(next_rows, inside, conv1_w, conv1_b, conv2_w)
-    next_real, next_imag = patch_spectra(next_feats, cosine, sin_table, rows_per)
-    combined_real = jnp.concatenate([own_real, next_real], axis=0)
-    combined_imag = jnp.concatenate([own_imag, next_imag], axis=0)
+    next_both = patch_spectra(next_feats, cosine, sin_table, rows_per)
+    combined = jnp.concatenate([own_both, next_both], axis=0)
     use_first = (offsets == 1)[:, None, None, None, None]
-    part_real = jnp.where(
-        use_first, combined_real[1 : sec_here + 1], combined_real[2 : sec_here + 2]
-    )
-    part_imag = jnp.where(
-        use_first, combined_imag[1 : sec_here + 1], combined_imag[2 : sec_here + 2]
-    )
+    part_both = jnp.where(use_first, combined[1 : sec_here + 1], combined[2 : sec_here + 2])
+    own_real, own_imag = own_both[..., :patch_len, :], own_both[..., patch_len:, :]
+    part_real, part_imag = part_both[..., :patch_len, :], part_both[..., patch_len:, :]
     section_ids = lax.axis_index("sec") * sec_here + jnp.arange(sec_here, dtype=jnp.int32)
     total_sections = sec_here * lax.axis_size("sec")
     pair_valid = section_ids + offsets < total_sections

time: 63.4 us -> 67 us (1.057)
  the two profiles are of different devices: /device:TPU:512 before, /device:TPU:57 now
where the time goes in v10:
time: 67 us; the launch traced here: 66.5 us
  blocking collectives  16.8 us (25%)
  other arithmetic  15.8 us (24%)
  matrix products  15.3 us (23%)
  starting transfers between devices  8.03 us (12%)
  waiting for transfers between devices  6.09 us (9%)
  local copies, waits for them, and re-layouts  3.64 us (5%)
  between operations  0.97 us (1%)
    all_to_all x1, blocking collectives, tile_sum(): return jnp.sum(lax.all_to_all(copies, axis, 0, 0, tiled=False), axis=0)  16.8 us
    dot_general x18, matrix products, conv_layers(): jnp.einsum('schw,co->sohw', window, conv2_w[3 * tap_row + tap_col], prefe...  9.71 us
    convert_element_type x2, other arithmetic, conv_layers(): jnp.where(inside[None, None, :, None], jax.nn.relu(layer_one), 0.0)  8.24 us
    ppermute x1, waiting for transfers between devices, from_behind(): return lax.ppermute(block, axis, route)  6.08 us
    ppermute x1, starting transfers between devices, from_behind(): return lax.ppermute(block, axis, route)  3.63 us
    ppermute x1, starting transfers between devices, with_halo(): before = lax.ppermute(last, axis, up)  3.1 us
    dot_general x2, matrix products, patch_spectra(): jnp.einsum('uy,byk->buk', left_sin, half_sin, preferred_element_type=jnp....  1.52 us
    dot_general x2, matrix products, patch_spectra(): jnp.einsum('uy,byk->buk', left_cos, half_cos, preferred_element_type=jnp....  1.48 us
  transfers between devices with their start and end apart: 3, of which 1 were waited for; matrix products, arithmetic and copies ran while one was open for 11% of the time, Pallas kernels for 0%

profile of v10, /device:TPU:57, one launch (start us, length us, event | category | flops | bytes accessed | tf_op | source)
XLA Modules:
  0.0 66.5 jit_solution(4755938117868876603)
XLA Ops:
  0.6 0.7 %fusion.135 = (bf16[2,2,128]{2,1,0:T(2,128)(2,1)S(1)}, bf16[2,2,128]{2,1,0:T(2,128)(2,1)S(1)}) fusion(bf16[2,128,128]{2,1,0:T(8,128)(2,1)} %param.6), kind=kLoop, calls=%fused_computation.228 | loop fusion | bytes 4096 | tf_op jit(solution)/shard_map/slice | solution.py:18
  1.4 3.1 %collective-permute-start = (bf16[2,2,128]{2,1,0:T(2,128)(2,1)S(1)}, bf16[2,2,128]{2,1,0:T(2,128)(2,1)S(1)}, u32[]{:S(2)}, u32[]{:S(2)}) collective-permute-start(bf16[2,2,128]{2,1,0:T(2,128)(2,1)S(1)} %get-tuple-element.50), channel_id=1, source_target_pairs={{0,1},{1,2},{2,3},{3,4},{4,5},{5,6},{6,7},{7,8},{8,9},{9,10},{10,1... | collective-permute-start | bytes 3080 | tf_op jit(solution)/shard_map/ppermute | solution.py:20
  4.5 1.3 %collective-permute-start.1 = (bf16[2,2,128]{2,1,0:T(2,128)(2,1)S(1)}, bf16[2,2,128]{2,1,0:T(2,128)(2,1)S(1)}, u32[]{:S(2)}, u32[]{:S(2)}) collective-permute-start(bf16[2,2,128]{2,1,0:T(2,128)(2,1)S(1)} %get-tuple-element.51), channel_id=1, source_target_pairs={{1,0},{2,1},{3,2},{4,3},{5,4},{6,5},{7,6},{8,7},{9,8},{10,9},{11,1... | collective-permute-start | bytes 3080 | tf_op jit(solution)/shard_map/ppermute | solution.py:21
  5.8 0.3 sine_convert_fusion
  6.1 0.3 fusion.61
  6.4 1.0 %bitcast_convert_fusion.8 = (f32[16]{0:T(128)S(1)}, f32[16]{0:T(128)S(1)}, f32[16]{0:T(128)S(1)}, f32[16]{0:T(128)S(1)}, f32[16]{0:T(128)S(1)}, /*index=5*/f32[1...) fusion(bf16[9,16]{1,0:T(8,128)(2,1)} %param.9), kind=kLoop, calls=%fused_computation.184 | loop fusion | flops 144 | bytes 864 | tf_op jit(solution)/shard_map/convert_element_type | solution.py:57
  7.4 0.7 compare_not_fusion
  8.2 0.7 %broadcast_multiply_fusion = (f32[2,1]{0,1:T(1,128)S(1)}, f32[2,1]{0,1:T(1,128)S(1)}, f32[2,1]{0,1:T(1,128)S(1)}) fusion(f32[]{:T(128)S(6)} %sub.56, s32[2]{0:T(128)} %param.7, s32[]{:T(128)S(6)} %mul.465, s32[2,1]{0,1:T(1,128)} %param.8), kind=kLoop, calls=%fused_computation.194 | loop fusion | flops 16 | bytes 48 | tf_op jit(solution)/shard_map/mul | solution.py:187
  8.9 0.1 copy.170
  9.0 0.1 copy.171
  9.1 0.1 copy.172
  9.2 0.9 %pad_maximum_fusion.1 = bf16[2,132,128]{2,1,0:T(8,128)(2,1)S(1)} fusion(bf16[2,2,128]{2,1,0:T(2,128)(2,1)S(1)} %collective-permute-done.1, bf16[2,128,128]{2,1,0:T(8,128)(2,1)} %param.6, bf16[2,2,128]{2,1,0:T(2,128)(2,1)S(1)} %collective-permute-done), kind=kLoop, calls=%fused_computation.97 | loop fusion | flops 202752 | bytes 135168 | tf_op jit(solution)/shard_map/concatenate | solution.py:22
  10.0 1.1 %fusion.35 = (f32[2,130,128]{2,1,0:T(8,128)S(1)}, f32[2,130,128]{2,1,0:T(8,128)S(1)}, f32[2,130,128]{2,1,0:T(8,128)S(1)}, f32[2,130,128]{2,1,0:T(8,128)S(1)}, f3...) fusion(bf16[2,132,128]{2,1,0:T(8,128)(2,1)S(1)} %pad_maximum_fu, ...), kind=kLoop, calls=%fused_computation.81 | loop fusion | flops 499200 | bytes 1404928 | tf_op jit(solution)/shard_map/convert_element_type | solution.py:58
  11.1 4.4 %select_convert_fusion.1 = bf16[2,16,130,128]{3,1,2,0:T(8,128)(2,1)S(1)} fusion(f32[2,130,128]{2,1,0:T(8,128)S(1)} %get-tuple-element.37, f32[16]{0:T(128)S(1)} %get-tuple-element.61, f32[2,130,128]{2,1,0:T(8,128)S(1)} %get-tuple-element.82, f32[16]{0:T(128)S(1)} %get-tuple-element.62, f32[2,130,128]{2,1,0:T(8,128)S(1)} %get-tuple-element.36, ...), kind=kLoop, calls=%fused_computation.21 | loop fusion | flops 11182080 | bytes 2263810 | tf_op jit(solution)/shard_map/convert_element_type | solution.py:62
  15.6 0.5 fusion.10
  16.1 0.5 fusion.11
  16.5 0.5 fusion.12
  17.0 0.5 fusion.13
  17.5 0.4 fusion.25
  18.0 0.5 fusion.27
  18.4 0.5 fusion.29
  18.9 0.5 fusion.9
  19.4 3.6 %collective-permute-start.2 = (bf16[2,132,128]{2,1,0:T(8,128)(2,1)S(1)}, bf16[2,132,128]{2,1,0:T(8,128)(2,1)S(1)}, u32[]{:S(2)}, u32[]{:S(2)}) collective-permute-start(bf16[2,132,128]{2,1,0:T(8,128)(2,1)S(1)} %pad_maximum_fusion.1), channel_id=1, source_target_pairs={{16,0},{32,16},{48,32},{64,48},{80,64},{96,80},{112,96},{128,112},... | collective-permute-start | bytes 202760 | tf_op jit(solution)/shard_map/ppermute | solution.py:29
  23.0 1.1 %fusion.5 = bf16[2,16,128,128]{3,1,2,0:T(8,128)(2,1)S(1)} fusion(f32[2,128,128,16]{2,3,1,0:T(8,128)S(1)} %fusion.25, f32[2,128,128,16]{2,3,1,0:T(8,128)S(1)} %fusion.13, f32[2,128,128,16]{2,3,1,0:T(8,128)S(1)} %fusion.12, f32[2,128,128,16]{2,3,1,0:T(8,128)S(1)} %fusion.27, f32[2,128,128,16]{2,3,1,0:T(8,128)S(1)} %fusion.11, ...), kind=kOutput, calls=%fused_computation.30 | convolution fusion | flops 21495808 | bytes 18894848 | tf_op jit(solution)/shard_map/schw,co->sohw/dot_general | solution.py:70
  24.1 0.3 copy.160
  24.4 0.7 %convolution_convert_fusion.1 = bf16[4096,256]{1,0:T(8,128)(2,1)S(1)} fusion(bf16[4096,128]{1,0:T(8,128)(2,1)S(1)} %bitcast.223, bf16[128,128]{1,0:T(8,128)(2,1)S(1)} %get-tuple-element.78, bf16[128,128]{1,0:T(8,128)(2,1)S(1)} %get-tuple-element.79), kind=kOutput, calls=%fused_computation.1 | convolution fusion | flops 269615104 | bytes 3211264 | tf_op jit(solution)/shard_map/dot_general | solution.py:84
  25.1 0.1 fusion.132
  25.2 0.7 %fusion.57 = f32[32,128,256]{2,1,0:T(8,128)S(1)} fusion(bf16[32,128,128]{2,1,0:T(8,128)(2,1)S(1)} %bitcast.227, bf16[128,128]{1,0:T(8,128)(2,1)S(1)} %get-tuple-element.81, bf16[128,128]{1,0:T(8,128)(2,1)S(1)} %get-tuple-element.79), kind=kOutput, calls=%fused_computation.115 | convolution fusion | flops 268566528 | bytes 5308416 | tf_op jit(solution)/shard_map/uy,byk->buk/dot_general | solution.py:91
  26.0 0.7 %add_convert_fusion.1 = bf16[32,128,256]{2,1,0:T(8,128)(2,1)S(1)} fusion(f32[32,128,256]{2,1,0:T(8,128)S(1)} %fusion.57, bf16[32,128,128]{2,1,0:T(8,128)(2,1)S(1)} %bitcast.225, bf16[128,128]{1,0:T(8,128)(2,1)S(1)} %get-tuple-element.80, bf16[128,128]{1,0:T(8,128)(2,1)S(1)} %get-tuple-element.81), kind=kOutput, calls=%fused_computation.3 | convolution fusion | flops 270663680 | bytes 7405568 | tf_op jit(solution)/shard_map/uy,byk->buk/dot_general | solution.py:93
  26.7 6.1 %collective-permute-done.2 = bf16[2,132,128]{2,1,0:T(8,128)(2,1)S(1)} collective-permute-done((bf16[2,132,128]{2,1,0:T(8,128)(2,1)S(1)}, bf16[2,132,128]{2,1,0:T(8,128)(2,1)S(1)}, u32[]{:S(2)}, u32[]{:S(2)}) %collective-permute-start.2) | collective-permute-done | bytes 67616 | tf_op jit(solution)/shard_map/ppermute | solution.py:29
  32.8 0.2 fusion.41
  33.0 3.8 %select_convert_fusion = bf16[2,16,130,128]{3,1,2,0:T(8,128)(2,1)S(1)} fusion(f32[2,130,128]{2,1,0:T(8,128)S(1)} %get-tuple-element.44, f32[2,130,128]{2,1,0:T(8,128)S(1)} %get-tuple-element.45, f32[2,130,128]{2,1,0:T(8,128)S(1)} %get-tuple-element.43, f32[2,130,128]{2,1,0:T(8,128)S(1)} %get-tuple-element.42, f32[2,130,128]{2,1,0:T(8,128)S(1)} %get-tuple-element.46, ...), kind=kLoop, calls=%fused_computation.20 | loop fusion | flops 11182080 | bytes 2263810 | tf_op jit(solution)/shard_map/convert_element_type | solution.py:62
  36.8 0.5 fusion.14
  37.3 0.5 fusion.15
  37.8 0.5 fusion.16
  38.3 0.5 fusion.17
  38.8 0.5 fusion.18
  39.3 0.4 fusion.19
  39.7 0.5 fusion.21
  40.2 0.5 fusion.23
  40.6 1.1 %fusion.6 = bf16[2,16,128,128]{3,1,2,0:T(8,128)(2,1)S(1)} fusion(f32[2,128,128,16]{2,3,1,0:T(8,128)S(1)} %fusion.19, f32[2,128,128,16]{2,3,1,0:T(8,128)S(1)} %fusion.18, f32[2,128,128,16]{2,3,1,0:T(8,128)S(1)} %fusion.17, f32[2,128,128,16]{2,3,1,0:T(8,128)S(1)} %fusion.21, f32[2,128,128,16]{2,3,1,0:T(8,128)S(1)} %fusion.16, ...), kind=kOutput, calls=%fused_computation.31 | convolution fusion | flops 21495808 | bytes 18894848 | tf_op jit(solution)/shard_map/schw,co->sohw/dot_general | solution.py:70
  41.7 0.3 copy.163
  42.0 0.7 %convolution_convert_fusion = bf16[4096,256]{1,0:T(8,128)(2,1)S(1)} fusion(bf16[4096,128]{1,0:T(8,128)(2,1)S(1)} %bitcast.224, bf16[128,128]{1,0:T(8,128)(2,1)S(1)} %get-tuple-element.78, bf16[128,128]{1,0:T(8,128)(2,1)S(1)} %get-tuple-element.79), kind=kOutput, calls=%fused_computation | convolution fusion | flops 269615104 | bytes 3211264 | tf_op jit(solution)/shard_map/dot_general | solution.py:84
  42.7 0.1 fusion.133
  42.9 0.7 %fusion.56 = f32[32,128,256]{2,1,0:T(8,128)S(1)} fusion(bf16[32,128,128]{2,1,0:T(8,128)(2,1)S(1)} %bitcast.228, bf16[128,128]{1,0:T(8,128)(2,1)S(1)} %get-tuple-element.81, bf16[128,128]{1,0:T(8,128)(2,1)S(1)} %get-tuple-element.79), kind=kOutput, calls=%fused_computation.114 | convolution fusion | flops 268566528 | bytes 5308416 | tf_op jit(solution)/shard_map/uy,byk->buk/dot_general | solution.py:91
  43.6 0.8 %add_convert_fusion = bf16[32,128,256]{2,1,0:T(8,128)(2,1)S(1)} fusion(f32[32,128,256]{2,1,0:T(8,128)S(1)} %fusion.56, bf16[32,128,128]{2,1,0:T(8,128)(2,1)S(1)} %bitcast.226, bf16[128,128]{1,0:T(8,128)(2,1)S(1)} %get-tuple-element.80, bf16[128,128]{1,0:T(8,128)(2,1)S(1)} %get-tuple-element.81), kind=kOutput, calls=%fused_computation.2 | convolution fusion | flops 270663680 | bytes 7405568 | tf_op jit(solution)/shard_map/uy,byk->buk/dot_general | solution.py:93
  44.4 0.3 fusion.4
  44.7 0.8 %fusion.3 = (bf16[2,128,128]{1,2,0:T(8,128)(2,1)S(1)}, bf16[2,128,128]{1,2,0:T(8,128)(2,1)S(1)}) fusion(bf16[2,1,16,256,128]{3,4,2,0,1:T(8,128)(2,1)S(1)} %fusion.4, bf16[2,1,16,256,128]{3,4,2,0,1:T(8,128)(2,1)S(1)} %bitcast.221), kind=kLoop, calls=%fused_computation.25 | loop fusion | flops 6225920 | bytes 4325376 | tf_op jit(solution)/shard_map/reduce_sum | solution.py:108
  45.5 0.1 copy.166
  45.7 0.1 copy.167
  45.8 0.1 fusion.31
  45.9 0.2 fusion.63
  46.1 0.2 fusion.7
  46.3 0.4 fusion.59
  46.7 0.5 fusion.137
  47.2 0.2 fusion.33
  47.4 0.2 multiply_reduce_fusion.1
  47.6 0.1 copy.173
  47.7 0.1 copy.174
  47.8 0.1 concatenate.43
  47.9 16.8 %all_to_all.5 = f32[16,2,7]{2,1,0:T(2,128)S(1)} all-to-all(f32[16,2,7]{2,1,0:T(2,128)S(1)} %broadcast_in_dim.36), channel_id=1, replica_groups=mesh['sec'=48,'tile'=16] {'tile'}, dimensions={0} | all-to-all | bytes 1792 | tf_op jit(solution)/shard_map/all_to_all | solution.py:35
  65.0 0.1 copy.209
  65.3 0.6 subtract_multiply_fusion
  65.9 0.7 copy.177
  (27 shorter events, 0.8 us)
Async XLA Ops:
  0.6 14.9 %copy-start = (bf16[9,16,16]{2,1,0:T(8,128)(2,1)S(1)}, bf16[9,16,16]{2,1,0:T(8,128)(2,1)}, u32[]{:S(2)}) copy-start(bf16[9,16,16]{2,1,0:T(8,128)(2,1)} %param.11) | copy-start | bytes 13828
  1.4 7.8 %collective-permute-start = (bf16[2,2,128]{2,1,0:T(2,128)(2,1)S(1)}, bf16[2,2,128]{2,1,0:T(2,128)(2,1)S(1)}, u32[]{:S(2)}, u32[]{:S(2)}) collective-permute-start(bf16[2,2,128]{2,1,0:T(2,128)(2,1)S(1)} %get-tuple-element.50), channel_id=1, source_target_pairs={{0,1},{1,2},{2,3},{3,4},{4,5},{5,6},{6,7},{7,8},{8,9},{9,10},{10,1... | collective-permute-start | bytes 3080 | tf_op jit(solution)/shard_map/ppermute | solution.py:20
  4.5 4.7 %collective-permute-start.1 = (bf16[2,2,128]{2,1,0:T(2,128)(2,1)S(1)}, bf16[2,2,128]{2,1,0:T(2,128)(2,1)S(1)}, u32[]{:S(2)}, u32[]{:S(2)}) collective-permute-start(bf16[2,2,128]{2,1,0:T(2,128)(2,1)S(1)} %get-tuple-element.51), channel_id=1, source_target_pairs={{1,0},{2,1},{3,2},{4,3},{5,4},{6,5},{7,6},{8,7},{9,8},{10,9},{11,1... | collective-permute-start | bytes 3080 | tf_op jit(solution)/shard_map/ppermute | solution.py:21
  19.4 13.4 %collective-permute-start.2 = (bf16[2,132,128]{2,1,0:T(8,128)(2,1)S(1)}, bf16[2,132,128]{2,1,0:T(8,128)(2,1)S(1)}, u32[]{:S(2)}, u32[]{:S(2)}) collective-permute-start(bf16[2,132,128]{2,1,0:T(8,128)(2,1)S(1)} %pad_maximum_fusion.1), channel_id=1, source_target_pairs={{16,0},{32,16},{48,32},{64,48},{80,64},{96,80},{112,96},{128,112},... | collective-permute-start | bytes 202760 | tf_op jit(solution)/shard_map/ppermute | solution.py:29
  26.0 7.0 %copy-start.1 = (f32[16]{0:T(128)S(1)}, f32[16]{0:T(128)}, u32[]{:S(2)}) copy-start(f32[16]{0:T(128)} %param.10) | copy-start | bytes 196

commit v11 on v5

--- a/solution.py
+++ b/solution.py
@@ -47,7 +47,7 @@
     strip_rows = wide_rows - 2
     patch_len = rows_in.shape[2]
     channels = conv1_w.shape[1]
-    padded = jnp.pad(rows_in, ((0, 0), (0, 0), (1, 1)))
+    padded = jnp.pad(rows_in.astype(jnp.float32), ((0, 0), (0, 0), (1, 1)))
     layer_one = (
         jnp.zeros((sec_count, channels, wide_rows, patch_len), jnp.float32)
         + conv1_b[None, :, None, None]
@@ -55,9 +55,7 @@
     for tap_row in range(3):
         for tap_col in range(3):
             weight_tap = conv1_w[3 * tap_row + tap_col].astype(jnp.float32)
-            window = padded[:, tap_row : tap_row + wide_rows, tap_col : tap_col + patch_len].astype(
-                jnp.float32
-            )
+            window = padded[:, tap_row : tap_row + wide_rows, tap_col : tap_col + patch_len]
             layer_one = layer_one + weight_tap[None, :, None, None] * window[:, None]
     hidden = jnp.where(inside[None, None, :, None], jax.nn.relu(layer_one), 0.0).astype(
         jnp.bfloat16

time: 63.4 us -> 65.9 us (1.039)
  the two profiles are of different devices: /device:TPU:512 before, /device:TPU:57 now
where the time goes in v11:
time: 65.9 us; the launch traced here: 65.6 us
  blocking collectives  16.8 us (25%)
  matrix products  15.3 us (23%)
  other arithmetic  13.6 us (21%)
  starting transfers between devices  8.03 us (12%)
  waiting for transfers between devices  5.48 us (8%)
  local copies, waits for them, and re-layouts  5.38 us (8%)
  between operations  0.98 us (1%)
    all_to_all x1, blocking collectives, tile_sum(): return jnp.sum(lax.all_to_all(copies, axis, 0, 0, tiled=False), axis=0)  16.8 us
    dot_general x18, matrix products, conv_layers(): jnp.einsum('schw,co->sohw', window, conv2_w[3 * tap_row + tap_col], prefe...  9.71 us
    convert_element_type x2, other arithmetic, conv_layers(): jnp.where(inside[None, None, :, None], jax.nn.relu(layer_one), 0.0)  7.46 us
    ppermute x1, waiting for transfers between devices, from_behind(): return lax.ppermute(block, axis, route)  5.47 us
    ppermute x1, starting transfers between devices, from_behind(): return lax.ppermute(block, axis, route)  3.63 us
    ppermute x1, starting transfers between devices, with_halo(): before = lax.ppermute(last, axis, up)  3.1 us
    dot_general x2, matrix products, patch_spectra(): jnp.einsum('uy,byk->buk', left_sin, half_sin, preferred_element_type=jnp....  1.49 us
    dot_general x2, matrix products, patch_spectra(): jnp.einsum('uy,byk->buk', left_cos, half_cos, preferred_element_type=jnp....  1.49 us
  transfers between devices with their start and end apart: 3, of which 1 were waited for; matrix products, arithmetic and copies ran while one was open for 12% of the time, Pallas kernels for 0%

profile of v11, /device:TPU:57, one launch (start us, length us, event | category | flops | bytes accessed | tf_op | source)
XLA Modules:
  0.0 65.6 jit_solution(12046218115296658327)
XLA Ops:
  0.6 0.7 %fusion.130 = (bf16[2,2,128]{2,1,0:T(2,128)(2,1)S(1)}, bf16[2,2,128]{2,1,0:T(2,128)(2,1)S(1)}) fusion(bf16[2,128,128]{2,1,0:T(8,128)(2,1)} %param.6), kind=kLoop, calls=%fused_computation.218 | loop fusion | bytes 4096 | tf_op jit(solution)/shard_map/slice | solution.py:18
  1.4 3.1 %collective-permute-start = (bf16[2,2,128]{2,1,0:T(2,128)(2,1)S(1)}, bf16[2,2,128]{2,1,0:T(2,128)(2,1)S(1)}, u32[]{:S(2)}, u32[]{:S(2)}) collective-permute-start(bf16[2,2,128]{2,1,0:T(2,128)(2,1)S(1)} %get-tuple-element.56), channel_id=1, source_target_pairs={{0,1},{1,2},{2,3},{3,4},{4,5},{5,6},{6,7},{7,8},{8,9},{9,10},{10,1... | collective-permute-start | bytes 3080 | tf_op jit(solution)/shard_map/ppermute | solution.py:20
  4.5 1.3 %collective-permute-start.1 = (bf16[2,2,128]{2,1,0:T(2,128)(2,1)S(1)}, bf16[2,2,128]{2,1,0:T(2,128)(2,1)S(1)}, u32[]{:S(2)}, u32[]{:S(2)}) collective-permute-start(bf16[2,2,128]{2,1,0:T(2,128)(2,1)S(1)} %get-tuple-element.57), channel_id=1, source_target_pairs={{1,0},{2,1},{3,2},{4,3},{5,4},{6,5},{7,6},{8,7},{9,8},{10,9},{11,1... | collective-permute-start | bytes 3080 | tf_op jit(solution)/shard_map/ppermute | solution.py:21
  5.8 0.3 sine_convert_fusion
  6.1 0.3 fusion.52
  6.4 1.0 %bitcast_convert_fusion.8 = (f32[16]{0:T(128)S(1)}, f32[16]{0:T(128)S(1)}, f32[16]{0:T(128)S(1)}, f32[16]{0:T(128)S(1)}, f32[16]{0:T(128)S(1)}, /*index=5*/f32[1...) fusion(bf16[9,16]{1,0:T(8,128)(2,1)} %param.9), kind=kLoop, calls=%fused_computation.170 | loop fusion | flops 144 | bytes 864 | tf_op jit(solution)/shard_map/convert_element_type | solution.py:57
  7.3 0.7 %compare_not_fusion = (pred[2]{0:T(512)(128)(4,1)S(1)}, pred[2]{0:T(512)(128)(4,1)S(1)}) fusion(s32[2]{0:T(128)} %param.7, s32[]{:T(128)S(6)} %mul.465), kind=kLoop, calls=%fused_computation.149 | loop fusion | flops 10 | bytes 16 | tf_op jit(solution)/shard_map/not | solution.py:113
  8.2 0.7 %broadcast_multiply_fusion = (f32[2,1]{0,1:T(1,128)S(1)}, f32[2,1]{0,1:T(1,128)S(1)}, f32[2,1]{0,1:T(1,128)S(1)}) fusion(f32[]{:T(128)S(6)} %sub.56, s32[2]{0:T(128)} %param.7, s32[]{:T(128)S(6)} %mul.465, s32[2,1]{0,1:T(1,128)} %param.8), kind=kLoop, calls=%fused_computation.180 | loop fusion | flops 16 | bytes 48 | tf_op jit(solution)/shard_map/mul | solution.py:195
  8.9 0.1 copy.170
  9.0 0.1 copy.171
  9.2 0.9 %pad_maximum_fusion.2 = (bf16[2,132,128]{2,1,0:T(8,128)(2,1)S(1)}, f32[2,132,128]{2,1,0:T(8,128)S(1)}) fusion(bf16[2,2,128]{2,1,0:T(2,128)(2,1)S(1)} %collective-permute-done.1, bf16[2,128,128]{2,1,0:T(8,128)(2,1)} %param.6, bf16[2,2,128]{2,1,0:T(2,128)(2,1)S(1)} %collective-permute-done), kind=kLoop, calls=%fused_computation.85 | loop fusion | flops 236544 | bytes 270336 | tf_op jit(solution)/shard_map/concatenate | solution.py:22
  10.0 0.3 pad_slice_fusion.35
  10.3 3.6 %select_convert_fusion.1 = bf16[2,16,130,128]{3,1,2,0:T(8,128)(2,1)S(1)} fusion(f32[2,130,128]{2,1,0:T(8,128)S(1)} %get-tuple-element.45, f32[16]{0:T(128)S(1)} %get-tuple-element.67, f32[2,130,128]{2,1,0:T(8,128)S(1)} %get-tuple-element.46, f32[16]{0:T(128)S(1)} %get-tuple-element.68, f32[2,130,128]{2,1,0:T(8,128)S(1)} %get-tuple-element.44, ...), kind=kLoop, calls=%fused_computation.21 | loop fusion | flops 11182080 | bytes 2263810 | tf_op jit(solution)/shard_map/convert_element_type | solution.py:60
  14.0 0.5 fusion.10
  14.5 0.5 fusion.11
  15.0 0.5 fusion.12
  15.5 0.5 fusion.13
  15.9 0.5 fusion.14
  16.4 0.5 fusion.28
  16.9 0.4 fusion.30
  17.3 0.5 fusion.32
  17.8 3.6 %collective-permute-start.2 = (bf16[2,132,128]{2,1,0:T(8,128)(2,1)S(1)}, bf16[2,132,128]{2,1,0:T(8,128)(2,1)S(1)}, u32[]{:S(2)}, u32[]{:S(2)}) collective-permute-start(bf16[2,132,128]{2,1,0:T(8,128)(2,1)S(1)} %get-tuple-element.54), channel_id=1, source_target_pairs={{16,0},{32,16},{48,32},{64,48},{80,64},{96,80},{112,96},{128,112},... | collective-permute-start | bytes 202760 | tf_op jit(solution)/shard_map/ppermute | solution.py:29
  21.4 1.1 %fusion.6 = bf16[2,16,128,128]{3,1,2,0:T(8,128)(2,1)S(1)} fusion(f32[2,128,128,16]{2,3,1,0:T(8,128)S(1)} %fusion.28, f32[2,128,128,16]{2,3,1,0:T(8,128)S(1)} %fusion.14, f32[2,128,128,16]{2,3,1,0:T(8,128)S(1)} %fusion.13, f32[2,128,128,16]{2,3,1,0:T(8,128)S(1)} %fusion.30, f32[2,128,128,16]{2,3,1,0:T(8,128)S(1)} %fusion.12, ...), kind=kOutput, calls=%fused_computation.30 | convolution fusion | flops 21495808 | bytes 18894848 | tf_op jit(solution)/shard_map/schw,co->sohw/dot_general | solution.py:68
  22.5 0.3 copy.160
  22.8 0.7 %convolution_convert_fusion.1 = bf16[4096,256]{1,0:T(8,128)(2,1)S(1)} fusion(bf16[4096,128]{1,0:T(8,128)(2,1)S(1)} %bitcast.222, bf16[128,128]{1,0:T(8,128)(2,1)S(1)} %get-tuple-element.84, bf16[128,128]{1,0:T(8,128)(2,1)S(1)} %get-tuple-element.85), kind=kOutput, calls=%fused_computation.1 | convolution fusion | flops 269615104 | bytes 3211264 | tf_op jit(solution)/shard_map/dot_general | solution.py:82
  23.5 0.1 fusion.127
  23.7 0.7 %fusion.48 = f32[32,128,256]{2,1,0:T(8,128)S(1)} fusion(bf16[32,128,128]{2,1,0:T(8,128)(2,1)S(1)} %bitcast.230, bf16[128,128]{1,0:T(8,128)(2,1)S(1)} %get-tuple-element.87, bf16[128,128]{1,0:T(8,128)(2,1)S(1)} %get-tuple-element.85), kind=kOutput, calls=%fused_computation.101 | convolution fusion | flops 268566528 | bytes 5308416 | tf_op jit(solution)/shard_map/uy,byk->buk/dot_general | solution.py:89
  24.4 0.7 %fusion.4 = bf16[32,256,128]{1,2,0:T(8,128)(2,1)S(1)} fusion(f32[32,128,256]{2,1,0:T(8,128)S(1)} %fusion.48, bf16[32,128,128]{2,1,0:T(8,128)(2,1)S(1)} %bitcast.228, bf16[128,128]{1,0:T(8,128)(2,1)S(1)} %get-tuple-element.86, bf16[128,128]{1,0:T(8,128)(2,1)S(1)} %get-tuple-element.87), kind=kOutput, calls=%fused_computation.28 | convolution fusion | flops 270663680 | bytes 7405568 | tf_op jit(solution)/shard_map/uy,byk->buk/dot_general | solution.py:91
  25.2 0.6 fusion.126
  25.8 5.5 %collective-permute-done.2 = bf16[2,132,128]{2,1,0:T(8,128)(2,1)S(1)} collective-permute-done((bf16[2,132,128]{2,1,0:T(8,128)(2,1)S(1)}, bf16[2,132,128]{2,1,0:T(8,128)(2,1)S(1)}, u32[]{:S(2)}, u32[]{:S(2)}) %collective-permute-start.2) | collective-permute-done | bytes 67616 | tf_op jit(solution)/shard_map/ppermute | solution.py:29
  31.2 0.3 pad_slice_fusion.29
  31.5 3.8 %select_convert_fusion = bf16[2,16,130,128]{3,1,2,0:T(8,128)(2,1)S(1)} fusion(f32[2,130,128]{2,1,0:T(8,128)S(1)} %get-tuple-element.36, f32[2,130,128]{2,1,0:T(8,128)S(1)} %get-tuple-element.88, f32[2,130,128]{2,1,0:T(8,128)S(1)} %get-tuple-element.35, f32[2,130,128]{2,1,0:T(8,128)S(1)} %get-tuple-element.39, f32[2,130,128]{2,1,0:T(8,128)S(1)} %get-tuple-element.89, ...), kind=kLoop, calls=%fused_computation.20 | loop fusion | flops 11182080 | bytes 2263810 | tf_op jit(solution)/shard_map/convert_element_type | solution.py:60
  35.4 0.5 fusion.15
  35.8 0.5 fusion.16
  36.3 0.5 fusion.17
  36.8 0.5 fusion.18
  37.3 0.5 fusion.19
  37.8 0.4 fusion.22
  38.2 0.5 fusion.24
  38.7 0.5 fusion.26
  39.2 1.1 %fusion.7 = bf16[2,16,128,128]{3,1,2,0:T(8,128)(2,1)S(1)} fusion(f32[2,128,128,16]{2,3,1,0:T(8,128)S(1)} %fusion.22, f32[2,128,128,16]{2,3,1,0:T(8,128)S(1)} %fusion.19, f32[2,128,128,16]{2,3,1,0:T(8,128)S(1)} %fusion.18, f32[2,128,128,16]{2,3,1,0:T(8,128)S(1)} %fusion.24, f32[2,128,128,16]{2,3,1,0:T(8,128)S(1)} %fusion.17, ...), kind=kOutput, calls=%fused_computation.31 | convolution fusion | flops 21495808 | bytes 18894848 | tf_op jit(solution)/shard_map/schw,co->sohw/dot_general | solution.py:68
  40.2 0.3 copy.163
  40.5 0.7 %convolution_convert_fusion = bf16[4096,256]{1,0:T(8,128)(2,1)S(1)} fusion(bf16[4096,128]{1,0:T(8,128)(2,1)S(1)} %bitcast.223, bf16[128,128]{1,0:T(8,128)(2,1)S(1)} %get-tuple-element.84, bf16[128,128]{1,0:T(8,128)(2,1)S(1)} %get-tuple-element.85), kind=kOutput, calls=%fused_computation | convolution fusion | flops 269615104 | bytes 3211264 | tf_op jit(solution)/shard_map/dot_general | solution.py:82
  41.2 0.1 fusion.125
  41.4 0.7 %fusion.47 = f32[32,128,256]{2,1,0:T(8,128)S(1)} fusion(bf16[32,128,128]{2,1,0:T(8,128)(2,1)S(1)} %bitcast.231, bf16[128,128]{1,0:T(8,128)(2,1)S(1)} %get-tuple-element.87, bf16[128,128]{1,0:T(8,128)(2,1)S(1)} %get-tuple-element.85), kind=kOutput, calls=%fused_computation.100 | convolution fusion | flops 268566528 | bytes 5308416 | tf_op jit(solution)/shard_map/uy,byk->buk/dot_general | solution.py:89
  42.1 0.7 %fusion.5 = bf16[32,256,128]{1,2,0:T(8,128)(2,1)S(1)} fusion(f32[32,128,256]{2,1,0:T(8,128)S(1)} %fusion.47, bf16[32,128,128]{2,1,0:T(8,128)(2,1)S(1)} %bitcast.229, bf16[128,128]{1,0:T(8,128)(2,1)S(1)} %get-tuple-element.86, bf16[128,128]{1,0:T(8,128)(2,1)S(1)} %get-tuple-element.87), kind=kOutput, calls=%fused_computation.29 | convolution fusion | flops 270663680 | bytes 7405568 | tf_op jit(solution)/shard_map/uy,byk->buk/dot_general | solution.py:91
  42.9 0.6 fusion.124
  43.5 1.1 %fusion.3 = (bf16[2,128,128]{1,2,0:T(8,128)(2,1)S(1)}, bf16[2,128,128]{1,2,0:T(8,128)(2,1)S(1)}) fusion(bf16[2,1,16,128,128]{3,4,2,0,1:T(8,128)(2,1)S(1)} %bitcast.225, bf16[2,1,16,128,128]{3,4,2,0,1:T(8,128)(2,1)S(1)} %bitcast.224, bf16[2,1,16,128,128]{3,4,2,0,1:T(8,128)(2,1)S(1)} %bitcast.227, bf16[2,1,16,128,128]{3,4,2,0,1:T(8,128)(2,1)S(1)} %bitcast.226, ...), kind=kLoop, calls=%fused_computation.25 | loop fusion | flops 11468800 | bytes 4325378 | tf_op jit(solution)/shard_map/reduce_sum | solution.py:112
  44.5 0.1 copy.166
  44.7 0.1 copy.167
  44.8 0.1 fusion.34
  44.9 0.2 fusion.54
  45.1 0.2 fusion.8
  45.3 0.4 fusion.50
  45.7 0.5 fusion.132
  46.2 0.2 fusion.36
  46.4 0.2 multiply_reduce_fusion.1
  46.6 0.1 copy.173
  46.8 0.1 concatenate.39
  46.9 16.8 %all_to_all.5 = f32[16,2,7]{2,1,0:T(2,128)S(1)} all-to-all(f32[16,2,7]{2,1,0:T(2,128)S(1)} %broadcast_in_dim.39), channel_id=1, replica_groups=mesh['sec'=48,'tile'=16] {'tile'}, dimensions={0} | all-to-all | bytes 1792 | tf_op jit(solution)/shard_map/all_to_all | solution.py:35
  64.0 0.1 copy.209
  64.2 0.1 copy.206
  64.3 0.6 subtract_multiply_fusion
  64.9 0.7 copy.177
  (29 shorter events, 0.9 us)
Async XLA Ops:
  0.6 9.7 %copy-start.1 = (f32[16]{0:T(128)S(1)}, f32[16]{0:T(128)}, u32[]{:S(2)}) copy-start(f32[16]{0:T(128)} %param.10) | copy-start | bytes 196
  1.4 7.8 %collective-permute-start = (bf16[2,2,128]{2,1,0:T(2,128)(2,1)S(1)}, bf16[2,2,128]{2,1,0:T(2,128)(2,1)S(1)}, u32[]{:S(2)}, u32[]{:S(2)}) collective-permute-start(bf16[2,2,128]{2,1,0:T(2,128)(2,1)S(1)} %get-tuple-element.56), channel_id=1, source_target_pairs={{0,1},{1,2},{2,3},{3,4},{4,5},{5,6},{6,7},{7,8},{8,9},{9,10},{10,1... | collective-permute-start | bytes 3080 | tf_op jit(solution)/shard_map/ppermute | solution.py:20
  4.5 4.7 %collective-permute-start.1 = (bf16[2,2,128]{2,1,0:T(2,128)(2,1)S(1)}, bf16[2,2,128]{2,1,0:T(2,128)(2,1)S(1)}, u32[]{:S(2)}, u32[]{:S(2)}) collective-permute-start(bf16[2,2,128]{2,1,0:T(2,128)(2,1)S(1)} %get-tuple-element.57), channel_id=1, source_target_pairs={{1,0},{2,1},{3,2},{4,3},{5,4},{6,5},{7,6},{8,7},{9,8},{10,9},{11,1... | collective-permute-start | bytes 3080 | tf_op jit(solution)/shard_map/ppermute | solution.py:21
  10.0 4.0 %copy-start = (bf16[9,16,16]{2,1,0:T(8,128)(2,1)S(1)}, bf16[9,16,16]{2,1,0:T(8,128)(2,1)}, u32[]{:S(2)}) copy-start(bf16[9,16,16]{2,1,0:T(8,128)(2,1)} %param.11) | copy-start | bytes 13828
  17.8 13.4 %collective-permute-start.2 = (bf16[2,132,128]{2,1,0:T(8,128)(2,1)S(1)}, bf16[2,132,128]{2,1,0:T(8,128)(2,1)S(1)}, u32[]{:S(2)}, u32[]{:S(2)}) collective-permute-start(bf16[2,132,128]{2,1,0:T(8,128)(2,1)S(1)} %get-tuple-element.54), channel_id=1, source_target_pairs={{16,0},{32,16},{48,32},{64,48},{80,64},{96,80},{112,96},{128,112},... | collective-permute-start | bytes 202760 | tf_op jit(solution)/shard_map/ppermute | solution.py:29

commit v12 on v5

--- a/solution.py
+++ b/solution.py
@@ -63,16 +63,17 @@
         jnp.bfloat16
     )
     hidden_pad = jnp.pad(hidden, ((0, 0), (0, 0), (0, 0), (1, 1)))
-    layer_two = jnp.zeros((sec_count, channels, strip_rows, patch_len), jnp.float32)
+    layer_two = None
     for tap_row in range(3):
         for tap_col in range(3):
             window = hidden_pad[:, :, tap_row : tap_row + strip_rows, tap_col : tap_col + patch_len]
-            layer_two = layer_two + jnp.einsum(
+            term = jnp.einsum(
                 "schw,co->sohw",
                 window,
                 conv2_w[3 * tap_row + tap_col],
                 preferred_element_type=jnp.float32,
             )
+            layer_two = term if layer_two is None else layer_two + term
     return layer_two.astype(jnp.bfloat16)
 
 

time: 63.4 us -> 63.4 us (level)
  no operation moved by 1% of the time
where the time goes in v12:
time: 63.4 us; the launch traced here: 63 us
  blocking collectives  18.2 us (29%)
  other arithmetic  15.7 us (25%)
  matrix products  15.3 us (24%)
  starting transfers between devices  7.21 us (11%)
  local copies, waits for them, and re-layouts  4.82 us (8%)
  between operations  0.99 us (2%)
  waiting for transfers between devices  0.78 us (1%)
    all_to_all x1, blocking collectives, tile_sum(): return jnp.sum(lax.all_to_all(copies, axis, 0, 0, tiled=False), axis=0)  18.2 us
    dot_general x18, matrix products, conv_layers(): jnp.einsum('schw,co->sohw', window, conv2_w[3 * tap_row + tap_col], prefe...  9.71 us
    convert_element_type x2, other arithmetic, conv_layers(): jnp.where(inside[None, None, :, None], jax.nn.relu(layer_one), 0.0)  8.23 us
    ppermute x1, starting transfers between devices, with_halo(): before = lax.ppermute(last, axis, up)  3.38 us
    ppermute x1, starting transfers between devices, from_behind(): return lax.ppermute(block, axis, route)  2.53 us
    dot_general x2, matrix products, patch_spectra(): jnp.einsum('uy,byk->buk', left_sin, half_sin, preferred_element_type=jnp....  1.49 us
    dot_general x2, matrix products, patch_spectra(): jnp.einsum('uy,byk->buk', left_cos, half_cos, preferred_element_type=jnp....  1.49 us
    dot_general x2, matrix products, patch_spectra(): jnp.dot(flat_rows, jnp.concatenate([cosine, sin_table], axis=1), preferre...  1.36 us
  transfers between devices with their start and end apart: 3, of which 1 were waited for; matrix products, arithmetic and copies ran while one was open for 27% of the time, Pallas kernels for 0%

profile of v12, /device:TPU:512, one launch (start us, length us, event | category | flops | bytes accessed | tf_op | source)
XLA Modules:
  0.0 63.0 jit_solution(16450555333532983575)
XLA Ops:
  0.6 0.7 %fusion.140 = (bf16[2,2,128]{2,1,0:T(2,128)(2,1)S(1)}, bf16[2,2,128]{2,1,0:T(2,128)(2,1)S(1)}) fusion(bf16[2,128,128]{2,1,0:T(8,128)(2,1)} %param.6), kind=kLoop, calls=%fused_computation.234 | loop fusion | bytes 4096 | tf_op jit(solution)/shard_map/slice | solution.py:18
  1.4 3.4 %collective-permute-start = (bf16[2,2,128]{2,1,0:T(2,128)(2,1)S(1)}, bf16[2,2,128]{2,1,0:T(2,128)(2,1)S(1)}, u32[]{:S(2)}, u32[]{:S(2)}) collective-permute-start(bf16[2,2,128]{2,1,0:T(2,128)(2,1)S(1)} %get-tuple-element.54), channel_id=1, source_target_pairs={{0,1},{1,2},{2,3},{3,4},{4,5},{5,6},{6,7},{7,8},{8,9},{9,10},{10,1... | collective-permute-start | bytes 3080 | tf_op jit(solution)/shard_map/ppermute | solution.py:20
  4.7 1.3 %collective-permute-start.1 = (bf16[2,2,128]{2,1,0:T(2,128)(2,1)S(1)}, bf16[2,2,128]{2,1,0:T(2,128)(2,1)S(1)}, u32[]{:S(2)}, u32[]{:S(2)}) collective-permute-start(bf16[2,2,128]{2,1,0:T(2,128)(2,1)S(1)} %get-tuple-element.55), channel_id=1, source_target_pairs={{1,0},{2,1},{3,2},{4,3},{5,4},{6,5},{7,6},{8,7},{9,8},{10,9},{11,1... | collective-permute-start | bytes 3080 | tf_op jit(solution)/shard_map/ppermute | solution.py:21
  6.0 0.3 sine_convert_fusion
  6.3 0.3 fusion.64
  6.6 1.0 %bitcast_convert_fusion.8 = (f32[16]{0:T(128)S(1)}, f32[16]{0:T(128)S(1)}, f32[16]{0:T(128)S(1)}, f32[16]{0:T(128)S(1)}, f32[16]{0:T(128)S(1)}, /*index=5*/f32[1...) fusion(bf16[9,16]{1,0:T(8,128)(2,1)} %param.9), kind=kLoop, calls=%fused_computation.188 | loop fusion | flops 144 | bytes 864 | tf_op jit(solution)/shard_map/convert_element_type | solution.py:57
  7.6 0.7 %compare_not_fusion = (pred[2]{0:T(512)(128)(4,1)S(1)}, pred[2]{0:T(512)(128)(4,1)S(1)}) fusion(s32[2]{0:T(128)} %param.7, s32[]{:T(128)S(6)} %mul.465), kind=kLoop, calls=%fused_computation.167 | loop fusion | flops 10 | bytes 16 | tf_op jit(solution)/shard_map/not | solution.py:116
  8.5 0.7 %broadcast_multiply_fusion = (f32[2,1]{0,1:T(1,128)S(1)}, f32[2,1]{0,1:T(1,128)S(1)}, f32[2,1]{0,1:T(1,128)S(1)}) fusion(f32[]{:T(128)S(6)} %sub.56, s32[2]{0:T(128)} %param.7, s32[]{:T(128)S(6)} %mul.465, s32[2,1]{0,1:T(1,128)} %param.8), kind=kLoop, calls=%fused_computation.198 | loop fusion | flops 16 | bytes 48 | tf_op jit(solution)/shard_map/mul | solution.py:198
  9.2 0.1 copy.170
  9.3 0.1 copy.171
  9.3 0.1 copy.172
  9.4 0.8 %collective-permute-done.1 = bf16[2,2,128]{2,1,0:T(2,128)(2,1)S(1)} collective-permute-done((bf16[2,2,128]{2,1,0:T(2,128)(2,1)S(1)}, bf16[2,2,128]{2,1,0:T(2,128)(2,1)S(1)}, u32[]{:S(2)}, u32[]{:S(2)}) %collective-permute-start.1) | collective-permute-done | bytes 1056 | tf_op jit(solution)/shard_map/ppermute | solution.py:21
  10.2 0.9 %pad_maximum_fusion.2 = bf16[2,132,128]{2,1,0:T(8,128)(2,1)S(1)} fusion(bf16[2,2,128]{2,1,0:T(2,128)(2,1)S(1)} %collective-permute-done.1, bf16[2,128,128]{2,1,0:T(8,128)(2,1)} %param.6, bf16[2,2,128]{2,1,0:T(2,128)(2,1)S(1)} %collective-permute-done), kind=kLoop, calls=%fused_computation.101 | loop fusion | flops 202752 | bytes 135168 | tf_op jit(solution)/shard_map/concatenate | solution.py:22
  11.1 2.5 %collective-permute-start.2 = (bf16[2,132,128]{2,1,0:T(8,128)(2,1)S(1)}, bf16[2,132,128]{2,1,0:T(8,128)(2,1)S(1)}, u32[]{:S(2)}, u32[]{:S(2)}) collective-permute-start(bf16[2,132,128]{2,1,0:T(8,128)(2,1)S(1)} %pad_maximum_fusion.2), channel_id=1, source_target_pairs={{16,0},{32,16},{48,32},{64,48},{80,64},{96,80},{112,96},{128,112},... | collective-permute-start | bytes 202760 | tf_op jit(solution)/shard_map/ppermute | solution.py:29
  13.6 1.1 %fusion.38 = (f32[2,130,128]{2,1,0:T(8,128)S(1)}, f32[2,130,128]{2,1,0:T(8,128)S(1)}, f32[2,130,128]{2,1,0:T(8,128)S(1)}, f32[2,130,128]{2,1,0:T(8,128)S(1)}, f3...) fusion(bf16[2,132,128]{2,1,0:T(8,128)(2,1)S(1)} %pad_maximum_fu, ...), kind=kLoop, calls=%fused_computation.85 | loop fusion | flops 499200 | bytes 1404928 | tf_op jit(solution)/shard_map/convert_element_type | solution.py:58
  14.7 4.4 %select_convert_fusion.1 = bf16[2,16,130,128]{3,1,2,0:T(8,128)(2,1)S(1)} fusion(f32[2,130,128]{2,1,0:T(8,128)S(1)} %get-tuple-element.50, f32[16]{0:T(128)S(1)} %get-tuple-element.65, f32[2,130,128]{2,1,0:T(8,128)S(1)} %get-tuple-element.82, f32[16]{0:T(128)S(1)} %get-tuple-element.66, f32[2,130,128]{2,1,0:T(8,128)S(1)} %get-tuple-element.49, ...), kind=kLoop, calls=%fused_computation.21 | loop fusion | flops 11182080 | bytes 2263810 | tf_op jit(solution)/shard_map/convert_element_type | solution.py:62
  19.2 0.5 fusion.10
  19.6 0.5 fusion.11
  20.1 0.5 fusion.12
  20.6 0.5 fusion.13
  21.1 0.5 fusion.14
  21.6 0.4 fusion.28
  22.0 0.5 fusion.30
  22.5 0.5 fusion.32
  22.9 1.1 %fusion.6 = bf16[2,16,128,128]{3,1,2,0:T(8,128)(2,1)S(1)} fusion(f32[2,128,128,16]{2,3,1,0:T(8,128)S(1)} %fusion.28, f32[2,128,128,16]{2,3,1,0:T(8,128)S(1)} %fusion.14, f32[2,128,128,16]{2,3,1,0:T(8,128)S(1)} %fusion.13, f32[2,128,128,16]{2,3,1,0:T(8,128)S(1)} %fusion.30, f32[2,128,128,16]{2,3,1,0:T(8,128)S(1)} %fusion.12, ...), kind=kOutput, calls=%fused_computation.30 | convolution fusion | flops 21495808 | bytes 18894848 | tf_op jit(solution)/shard_map/schw,co->sohw/dot_general | solution.py:70
  24.0 0.3 copy.160
  24.3 0.7 %convolution_convert_fusion.1 = bf16[4096,256]{1,0:T(8,128)(2,1)S(1)} fusion(bf16[4096,128]{1,0:T(8,128)(2,1)S(1)} %bitcast.222, bf16[128,128]{1,0:T(8,128)(2,1)S(1)} %get-tuple-element.84, bf16[128,128]{1,0:T(8,128)(2,1)S(1)} %get-tuple-element.85), kind=kOutput, calls=%fused_computation.1 | convolution fusion | flops 269615104 | bytes 3211264 | tf_op jit(solution)/shard_map/dot_general | solution.py:85
  25.0 0.1 fusion.138
  25.2 0.7 %fusion.60 = f32[32,128,256]{2,1,0:T(8,128)S(1)} fusion(bf16[32,128,128]{2,1,0:T(8,128)(2,1)S(1)} %bitcast.230, bf16[128,128]{1,0:T(8,128)(2,1)S(1)} %get-tuple-element.87, bf16[128,128]{1,0:T(8,128)(2,1)S(1)} %get-tuple-element.85), kind=kOutput, calls=%fused_computation.119 | convolution fusion | flops 268566528 | bytes 5308416 | tf_op jit(solution)/shard_map/uy,byk->buk/dot_general | solution.py:92
  25.9 0.7 %fusion.4 = bf16[32,256,128]{1,2,0:T(8,128)(2,1)S(1)} fusion(f32[32,128,256]{2,1,0:T(8,128)S(1)} %fusion.60, bf16[32,128,128]{2,1,0:T(8,128)(2,1)S(1)} %bitcast.228, bf16[128,128]{1,0:T(8,128)(2,1)S(1)} %get-tuple-element.86, bf16[128,128]{1,0:T(8,128)(2,1)S(1)} %get-tuple-element.87), kind=kOutput, calls=%fused_computation.28 | convolution fusion | flops 270663680 | bytes 7405568 | tf_op jit(solution)/shard_map/uy,byk->buk/dot_general | solution.py:94
  26.7 0.6 fusion.137
  27.3 0.2 fusion.44
  27.5 3.8 %select_convert_fusion = bf16[2,16,130,128]{3,1,2,0:T(8,128)(2,1)S(1)} fusion(f32[2,130,128]{2,1,0:T(8,128)S(1)} %get-tuple-element.41, f32[2,130,128]{2,1,0:T(8,128)S(1)} %get-tuple-element.42, f32[2,130,128]{2,1,0:T(8,128)S(1)} %get-tuple-element.40, f32[2,130,128]{2,1,0:T(8,128)S(1)} %get-tuple-element.39, f32[2,130,128]{2,1,0:T(8,128)S(1)} %get-tuple-element.43, ...), kind=kLoop, calls=%fused_computation.20 | loop fusion | flops 11182080 | bytes 2263810 | tf_op jit(solution)/shard_map/convert_element_type | solution.py:62
  31.3 0.5 fusion.15
  31.8 0.5 fusion.16
  32.3 0.5 fusion.17
  32.8 0.5 fusion.18
  33.2 0.5 fusion.19
  33.7 0.5 fusion.22
  34.2 0.4 fusion.24
  34.7 0.5 fusion.26
  35.1 1.1 %fusion.7 = bf16[2,16,128,128]{3,1,2,0:T(8,128)(2,1)S(1)} fusion(f32[2,128,128,16]{2,3,1,0:T(8,128)S(1)} %fusion.22, f32[2,128,128,16]{2,3,1,0:T(8,128)S(1)} %fusion.19, f32[2,128,128,16]{2,3,1,0:T(8,128)S(1)} %fusion.18, f32[2,128,128,16]{2,3,1,0:T(8,128)S(1)} %fusion.24, f32[2,128,128,16]{2,3,1,0:T(8,128)S(1)} %fusion.17, ...), kind=kOutput, calls=%fused_computation.31 | convolution fusion | flops 21495808 | bytes 18894848 | tf_op jit(solution)/shard_map/schw,co->sohw/dot_general | solution.py:70
  36.2 0.3 copy.163
  36.5 0.7 %convolution_convert_fusion = bf16[4096,256]{1,0:T(8,128)(2,1)S(1)} fusion(bf16[4096,128]{1,0:T(8,128)(2,1)S(1)} %bitcast.223, bf16[128,128]{1,0:T(8,128)(2,1)S(1)} %get-tuple-element.84, bf16[128,128]{1,0:T(8,128)(2,1)S(1)} %get-tuple-element.85), kind=kOutput, calls=%fused_computation | convolution fusion | flops 269615104 | bytes 3211264 | tf_op jit(solution)/shard_map/dot_general | solution.py:85
  37.2 0.1 fusion.136
  37.3 0.7 %fusion.59 = f32[32,128,256]{2,1,0:T(8,128)S(1)} fusion(bf16[32,128,128]{2,1,0:T(8,128)(2,1)S(1)} %bitcast.231, bf16[128,128]{1,0:T(8,128)(2,1)S(1)} %get-tuple-element.87, bf16[128,128]{1,0:T(8,128)(2,1)S(1)} %get-tuple-element.85), kind=kOutput, calls=%fused_computation.118 | convolution fusion | flops 268566528 | bytes 5308416 | tf_op jit(solution)/shard_map/uy,byk->buk/dot_general | solution.py:92
  38.1 0.7 %fusion.5 = bf16[32,256,128]{1,2,0:T(8,128)(2,1)S(1)} fusion(f32[32,128,256]{2,1,0:T(8,128)S(1)} %fusion.59, bf16[32,128,128]{2,1,0:T(8,128)(2,1)S(1)} %bitcast.229, bf16[128,128]{1,0:T(8,128)(2,1)S(1)} %get-tuple-element.86, bf16[128,128]{1,0:T(8,128)(2,1)S(1)} %get-tuple-element.87), kind=kOutput, calls=%fused_computation.29 | convolution fusion | flops 270663680 | bytes 7405568 | tf_op jit(solution)/shard_map/uy,byk->buk/dot_general | solution.py:94
  38.8 0.6 fusion.135
  39.4 1.1 %fusion.3 = (bf16[2,128,128]{1,2,0:T(8,128)(2,1)S(1)}, bf16[2,128,128]{1,2,0:T(8,128)(2,1)S(1)}) fusion(bf16[2,1,16,128,128]{3,4,2,0,1:T(8,128)(2,1)S(1)} %bitcast.225, bf16[2,1,16,128,128]{3,4,2,0,1:T(8,128)(2,1)S(1)} %bitcast.224, bf16[2,1,16,128,128]{3,4,2,0,1:T(8,128)(2,1)S(1)} %bitcast.227, bf16[2,1,16,128,128]{3,4,2,0,1:T(8,128)(2,1)S(1)} %bitcast.226, ...), kind=kLoop, calls=%fused_computation.25 | loop fusion | flops 11468800 | bytes 4325378 | tf_op jit(solution)/shard_map/reduce_sum | solution.py:115
  40.5 0.1 copy.166
  40.6 0.1 copy.167
  40.7 0.1 fusion.34
  40.9 0.2 fusion.66
  41.0 0.2 fusion.8
  41.2 0.4 fusion.62
  41.6 0.5 fusion.142
  42.1 0.2 fusion.36
  42.3 0.2 multiply_reduce_fusion.1
  42.6 0.1 copy.173
  42.7 0.1 concatenate.47
  42.8 18.2 %all_to_all.5 = f32[16,2,7]{2,1,0:T(2,128)S(1)} all-to-all(f32[16,2,7]{2,1,0:T(2,128)S(1)} %broadcast_in_dim.39), channel_id=1, replica_groups=mesh['sec'=48,'tile'=16] {'tile'}, dimensions={0} | all-to-all | bytes 1792 | tf_op jit(solution)/shard_map/all_to_all | solution.py:35
  61.4 0.1 copy.209
  61.7 0.6 subtract_multiply_fusion
  62.3 0.7 %copy.177 = f32[2,4]{1,0:T(2,128)} copy(f32[2,4]{0,1:T(4,128)S(1)} %pad_maximum_fusion.7) | data formatting | bytes 64
  (28 shorter events, 0.9 us)
Async XLA Ops:
  0.6 18.5 %copy-start = (bf16[9,16,16]{2,1,0:T(8,128)(2,1)S(1)}, bf16[9,16,16]{2,1,0:T(8,128)(2,1)}, u32[]{:S(2)}) copy-start(bf16[9,16,16]{2,1,0:T(8,128)(2,1)} %param.11) | copy-start | bytes 13828
  1.4 8.1 %collective-permute-start = (bf16[2,2,128]{2,1,0:T(2,128)(2,1)S(1)}, bf16[2,2,128]{2,1,0:T(2,128)(2,1)S(1)}, u32[]{:S(2)}, u32[]{:S(2)}) collective-permute-start(bf16[2,2,128]{2,1,0:T(2,128)(2,1)S(1)} %get-tuple-element.54), channel_id=1, source_target_pairs={{0,1},{1,2},{2,3},{3,4},{4,5},{5,6},{6,7},{7,8},{8,9},{9,10},{10,1... | collective-permute-start | bytes 3080 | tf_op jit(solution)/shard_map/ppermute | solution.py:20
  4.7 5.5 %collective-permute-start.1 = (bf16[2,2,128]{2,1,0:T(2,128)(2,1)S(1)}, bf16[2,2,128]{2,1,0:T(2,128)(2,1)S(1)}, u32[]{:S(2)}, u32[]{:S(2)}) collective-permute-start(bf16[2,2,128]{2,1,0:T(2,128)(2,1)S(1)} %get-tuple-element.55), channel_id=1, source_target_pairs={{1,0},{2,1},{3,2},{4,3},{5,4},{6,5},{7,6},{8,7},{9,8},{10,9},{11,1... | collective-permute-start | bytes 3080 | tf_op jit(solution)/shard_map/ppermute | solution.py:21
  11.1 16.2 %collective-permute-start.2 = (bf16[2,132,128]{2,1,0:T(8,128)(2,1)S(1)}, bf16[2,132,128]{2,1,0:T(8,128)(2,1)S(1)}, u32[]{:S(2)}, u32[]{:S(2)}) collective-permute-start(bf16[2,132,128]{2,1,0:T(8,128)(2,1)S(1)} %pad_maximum_fusion.2), channel_id=1, source_target_pairs={{16,0},{32,16},{48,32},{64,48},{80,64},{96,80},{112,96},{128,112},... | collective-permute-start | bytes 202760 | tf_op jit(solution)/shard_map/ppermute | solution.py:29
  26.7 0.8 %copy-start.1 = (f32[16]{0:T(128)S(1)}, f32[16]{0:T(128)}, u32[]{:S(2)}) copy-start(f32[16]{0:T(128)} %param.10) | copy-start | bytes 196
